TPU v7x, 128 devices: a whole 4x4x4 slice. The times are simulated.
128 devices in a mesh: tm: 128 (over x, y, z, core).
Axes of the slice: x: 4, y: 4, z: 4, core: 2. Of those that a mesh axis runs over, the one named last changes fastest.
Arguments:
- observations: float32 [4096, 4, 64], P('tm'), may hold values from -6 to 6
- decay: float32 [4096, 128], P('tm'), may hold values from 0 to 1
- transition: float32 [128, 128], replicated, may hold values from -1 to 1
- obs_map: float32 [64, 128], replicated, may hold values from -0.0625 to 0.0625
- noise_precision: float32 [64], replicated, may hold values from 0.01 to 0.2
- smoother_gain: float32 [128, 128], replicated, may hold values from -1 to 1
Outputs:
- filtered: float32 [4096, 4, 128], P('tm')
- smoothed: float32 [4096, 4, 128], P('tm')
All inputs are finite; a program needn't handle non-finite values.
Results may differ from a plain program's by a relative error of at most 0.0003.
Values sent between devices are 32-bit elements; how exact they have to be, the bound alone decides.
No kernel may reach another device: no remote copies, remote signals or barrier semaphores. Data moves between devices by JAX's collectives and lax.ppermute only.
A program may use at most 128 MiB of HBM per device.

v0:
```python
import jax
import jax.numpy as jnp
from jax import lax
from jax.sharding import PartitionSpec as P

HIGHEST = lax.Precision.HIGHEST


def dot(a, b):
    return jnp.dot(a, b, precision=HIGHEST)


def shifted(x, by):
    count = lax.axis_size("tm")
    pairs = [(i, i + by) for i in range(count) if 0 <= i + by < count]
    return lax.ppermute(x, "tm", pairs)


def up_sweep(maps, adds):
    levels = [(maps, adds)]
    while maps.shape[0] > 1:
        pairs = maps.reshape((-1, 2) + maps.shape[1:])
        if adds is not None:
            halves = adds.reshape((-1, 2) + adds.shape[1:])
            adds = (
                jnp.einsum("tbj,tjk->tbk", halves[:, 0], pairs[:, 1], precision=HIGHEST)
                + halves[:, 1]
            )
        maps = jnp.einsum("tij,tjk->tik", pairs[:, 0], pairs[:, 1], precision=HIGHEST)
        levels.append((maps, adds))
    return levels


def down_sweep_maps(levels):
    size = levels[0][0].shape[-1]
    excl = None
    for maps, _ in reversed(levels[:-1]):
        left = maps.reshape((-1, 2) + maps.shape[1:])[:, 0]
        if excl is None:
            excl = jnp.eye(size, dtype=jnp.float32)[None]
            odd = left
        else:
            odd = jnp.einsum("tij,tjk->tik", excl, left, precision=HIGHEST)
        excl = jnp.stack([excl, odd], 1).reshape((-1,) + maps.shape[1:])
    return excl


def down_sweep_adds(levels, adds_levels):
    excl = None
    for (maps, _), adds in zip(reversed(levels[:-1]), reversed(adds_levels[:-1])):
        left_map = maps.reshape((-1, 2) + maps.shape[1:])[:, 0]
        left_add = adds.reshape((-1, 2) + adds.shape[1:])[:, 0]
        if excl is None:
            excl = jnp.zeros_like(left_add[:1])
            odd = left_add
        else:
            odd = jnp.einsum("tbj,tjk->tbk", excl, left_map, precision=HIGHEST) + left_add
        excl = jnp.stack([excl, odd], 1).reshape((-1,) + adds.shape[1:])
    return excl


def up_sweep_adds(levels, adds):
    out = [adds]
    for maps, _ in levels[:-1]:
        pairs = maps.reshape((-1, 2) + maps.shape[1:])
        halves = adds.reshape((-1, 2) + adds.shape[1:])
        adds = (
            jnp.einsum("tbj,tjk->tbk", halves[:, 0], pairs[:, 1], precision=HIGHEST)
            + halves[:, 1]
        )
        out.append(adds)
    return out


def exchanged(x, bit):
    count = lax.axis_size("tm")
    return lax.ppermute(x, "tm", [(i, i ^ bit) for i in range(count)])


def batched(lhs, rhs):
    return jnp.einsum("kij,kjl->kil", jnp.stack(lhs), jnp.stack(rhs), precision=HIGHEST)


def local(observations, decay, transition, obs_map, noise_precision, smoother_gain):
    size = transition.shape[0]
    count = lax.axis_size("tm")
    index = lax.axis_index("tm")
    gain_rows = obs_map * noise_precision[:, None]
    closed_rows = transition.T - dot(transition.T, dot(obs_map.T, gain_rows))
    forward_adds = jnp.einsum("wyn,nx->wyx", observations, gain_rows, precision=HIGHEST)

    following = shifted(decay[:1], -1)
    upcoming = jnp.concatenate([decay[1:], following], 0)
    step_maps = jnp.stack([decay, upcoming[::-1]])[:, :, :, None] * jnp.stack(
        [closed_rows, smoother_gain.T]
    )[:, None]

    tree = [(step_maps, forward_adds)]
    maps, adds = step_maps, forward_adds
    while maps.shape[1] > 1:
        pairs = maps.reshape((2, -1, 2) + maps.shape[2:])
        halves = adds.reshape((-1, 2) + adds.shape[1:])
        adds = (
            jnp.einsum("tbj,tjk->tbk", halves[:, 0], pairs[0, :, 1], precision=HIGHEST)
            + halves[:, 1]
        )
        maps = jnp.einsum("dtij,dtjk->dtik", pairs[:, :, 0], pairs[:, :, 1], precision=HIGHEST)
        tree.append((maps, adds))
    forward_tree = [(m[0], a) for m, a in tree]
    backward_tree = [(m[1], None) for m, _ in tree]

    rounds = []
    bit = 1
    while bit < count:
        rounds.append(bit)
        bit *= 2
    eye = jnp.eye(size, dtype=jnp.float32)
    total_map, total_add, before_map, before_add = maps[0, 0], adds[0], eye, jnp.zeros_like(adds[0])
    back_total, back_before = maps[1, 0], eye
    stored = []
    late = forward_tree
    for k, bit in enumerate(rounds):
        upper = (index & bit) != 0
        if k == len(rounds) - 1:
            got_add = exchanged(total_add, bit)
            entering = jnp.where(upper, dot(got_add, before_map) + before_add, before_add)
            stored.append((back_total, back_total, back_before))
            break
        message = jnp.concatenate([total_map, total_add, back_total], 0)
        got = exchanged(message, bit)
        if k == 0:
            late, got = lax.optimization_barrier((late, got))
        got_map, got_add, got_back = got[:size], got[size:-size], got[-size:]
        first_map = jnp.where(upper, got_map, total_map)
        second_map = jnp.where(upper, total_map, got_map)
        first_add = jnp.where(upper, got_add, total_add)
        second_add = jnp.where(upper, total_add, got_add)
        back_first = jnp.where(upper, back_total, got_back)
        back_second = jnp.where(upper, got_back, back_total)
        stored.append((back_total, back_second, back_before))
        products = batched(
            [first_map, got_map, back_first, got_back],
            [second_map, before_map, back_second, back_before],
        )
        offsets = batched([first_add, got_add], [second_map, before_map])
        total_map, total_add = products[0], offsets[0] + second_add
        before_map = jnp.where(upper, products[1], before_map)
        before_add = jnp.where(upper, offsets[1] + before_add, before_add)
        back_total = products[2]
        back_before = jnp.where(upper, back_before, products[3])

    excl_maps = down_sweep_maps(late)
    excl_adds = down_sweep_adds(late, [a for _, a in late])
    previous = jnp.einsum("bs,tsr->tbr", entering, excl_maps, precision=HIGHEST) + excl_adds
    filtered = (
        jnp.einsum("tbs,sr->tbr", previous * decay[:, None, :], closed_rows, precision=HIGHEST)
        + forward_adds
    )
    predicted = jnp.einsum(
        "tbs,sr->tbr", filtered * upcoming[:, None, :], transition.T, precision=HIGHEST
    )
    backward_adds = filtered - jnp.einsum(
        "tbs,sr->tbr", predicted * upcoming[:, None, :], smoother_gain.T, precision=HIGHEST
    )
    back_adds = up_sweep_adds(backward_tree, backward_adds[::-1])

    total_add = back_adds[-1][0]
    before_add = jnp.zeros_like(total_add)
    late_b = (backward_tree, back_adds)
    for k, bit in enumerate(rounds):
        upper = (index & bit) != 0
        own_map, second_map, own_before = stored[k]
        got_add = exchanged(total_add, bit)
        if k == 0:
            late_b, got_add = lax.optimization_barrier((late_b, got_add))
        if k == len(rounds) - 1:
            before_add = jnp.where(upper, before_add, dot(got_add, own_before) + before_add)
            break
        first_add = jnp.where(upper, total_add, got_add)
        second_add = jnp.where(upper, got_add, total_add)
        offsets = batched([first_add, got_add], [second_map, own_before])
        total_add = offsets[0] + second_add
        before_add = jnp.where(upper, before_add, offsets[1] + before_add)
    arriving = before_add
    back_excl_maps = down_sweep_maps(late_b[0])
    back_excl_adds = down_sweep_adds(late_b[0], late_b[1])
    following_state = (
        jnp.einsum("bs,tsr->tbr", arriving, back_excl_maps, precision=HIGHEST) + back_excl_adds
    )[::-1]
    smoothed = (
        jnp.einsum(
            "tbs,sr->tbr", following_state * upcoming[:, None, :], smoother_gain.T, precision=HIGHEST
        )
        + backward_adds
    )
    return filtered, smoothed


def solution(mesh):
    in_specs = (P("tm", None, None), P("tm", None), P(), P(), P(), P())
    out_specs = (P("tm", None, None), P("tm", None, None))
    return jax.shard_map(local, mesh=mesh, in_specs=in_specs, out_specs=out_specs, check_vma=False)
```

profile of v0, /device:TPU:6, one launch (start us, length us, event | category | flops | bytes accessed | tf_op | source)
XLA Modules:
  0.0 121.7 jit_solution(8288175849834738156)
XLA Ops:
  1.4 8.1 %collective-permute-start = (f32[1,128]{1,0:T(1,128)S(1)}, f32[1,128]{1,0:T(1,128)S(1)}, u32[]{:S(2)}, u32[]{:S(2)}) collective-permute-start(f32[1,128]{1,0:T(1,128)S(1)} %slice.428), channel_id=1, source_target_pairs={{1,0},{2,1},{3,2},{4,3},{5,4},{6,5},{7,6},{8,7},{9,8},{10,9},{11,1... | collective-permute-start | bytes 1544 | tf_op jit(solution)/shard_map/ppermute | solution.py:16
  10.8 1.2 fusion.200
  12.0 1.1 convolution_subtract_fusion
  18.0 1.1 broadcast_multiply_fusion.1
  19.1 2.2 %fusion.295 = (f32[1,32,128,128]{3,2,1,0:T(8,128)}, f32[32,128,128]{2,1,0:T(8,128)S(1)}, f32[32,128,128]{2,1,0:T(8,128)S(1)}) fusion(f32[2,32,128,128]{3,2,1,0:T(8,128)S(1)} %broadcast_multiply_fusion.1), kind=kLoop, calls=%fused_computation.547 | loop fusion | bytes 10485760 | tf_op jit(solution)/shard_map/slice | solution.py:110
  21.3 1.1 broadcast_multiply_fusion
  22.4 2.3 %fusion = f32[2,16,128,128]{3,2,1,0:T(8,128)S(1)} fusion(f32[2,16,2,128,128]{4,3,1,0,2:T(8,128)S(1)} %broadcast_multiply_fusion), kind=kOutput, calls=%fused_computation.1 | convolution fusion | flops 805306368 | bytes 6291456 | tf_op jit(solution)/shard_map/dtij,dtjk->dtik/dot_general | solution.py:107
  24.7 1.3 %fusion.296 = (f32[1,16,128,128]{3,2,1,0:T(8,128)}, f32[16,128,128]{2,1,0:T(8,128)S(1)}, f32[16,128,128]{2,1,0:T(8,128)S(1)}) fusion(f32[2,16,128,128]{3,2,1,0:T(8,128)S(1)} %fusion), kind=kLoop, calls=%fused_computation.548 | loop fusion | bytes 5242880 | tf_op jit(solution)/shard_map/slice | solution.py:110
  26.0 1.2 fusion.13
  27.2 1.2 fusion.297
  38.6 4.5 %collective-permute-done.2 = f32[260,128]{1,0:T(8,128)S(1)} collective-permute-done((f32[260,128]{1,0:T(8,128)S(1)}, f32[260,128]{1,0:T(8,128)S(1)}, u32[]{:S(2)}, u32[]{:S(2)}) %collective-permute-start.2) | collective-permute-done | bytes 133152 | tf_op jit(solution)/shard_map/ppermute | solution.py:77
  44.6 5.8 %collective-permute-done.3 = f32[260,128]{1,0:T(8,128)S(1)} collective-permute-done((f32[260,128]{1,0:T(8,128)S(1)}, f32[260,128]{1,0:T(8,128)S(1)}, u32[]{:S(2)}, u32[]{:S(2)}) %collective-permute-start.3) | collective-permute-done | bytes 133152 | tf_op jit(solution)/shard_map/ppermute | solution.py:77
  51.5 5.1 %collective-permute-done.4 = f32[260,128]{1,0:T(8,128)S(1)} collective-permute-done((f32[260,128]{1,0:T(8,128)S(1)}, f32[260,128]{1,0:T(8,128)S(1)}, u32[]{:S(2)}, u32[]{:S(2)}) %collective-permute-start.4) | collective-permute-done | bytes 133152 | tf_op jit(solution)/shard_map/ppermute | solution.py:77
  57.5 1.2 convolution_bitcast_fusion.1
  58.7 5.2 %collective-permute-done.5 = f32[260,128]{1,0:T(8,128)S(1)} collective-permute-done((f32[260,128]{1,0:T(8,128)S(1)}, f32[260,128]{1,0:T(8,128)S(1)}, u32[]{:S(2)}, u32[]{:S(2)}) %collective-permute-start.5) | collective-permute-done | bytes 133152 | tf_op jit(solution)/shard_map/ppermute | solution.py:77
  65.6 4.2 %collective-permute-done.6 = f32[260,128]{1,0:T(8,128)S(1)} collective-permute-done((f32[260,128]{1,0:T(8,128)S(1)}, f32[260,128]{1,0:T(8,128)S(1)}, u32[]{:S(2)}, u32[]{:S(2)}) %collective-permute-start.6) | collective-permute-done | bytes 133152 | tf_op jit(solution)/shard_map/ppermute | solution.py:77
  70.1 1.2 collective-permute-start.7
  71.7 3.8 %collective-permute-done.7 = f32[4,128]{1,0:T(4,128)S(1)} collective-permute-done((f32[4,128]{1,0:T(4,128)S(1)}, f32[4,128]{1,0:T(4,128)S(1)}, u32[]{:S(2)}, u32[]{:S(2)}) %collective-permute-start.7) | collective-permute-done | bytes 2080 | tf_op jit(solution)/shard_map/ppermute | solution.py:77
  75.7 1.2 fusion.301
  78.7 1.5 %rev.10 = f32[32,4,128]{2,0,1:T(8,128)} reverse(f32[32,4,128]{2,0,1:T(8,128)} %convolution_subtract_fusion.1), dimensions={0} | reverse | bytes 131072 | tf_op jit(solution)/shard_map/rev | solution.py:165
  81.2 2.2 %convolution_add_fusion.3 = f32[16,4,128]{2,1,0:T(4,128)S(1)} fusion(f32[16,2,128,128]{3,2,1,0:T(8,128)} %bitcast.824, f32[16,1,4,128]{3,1,0,2:T(1,128)S(1)} %get-tuple-element.135, f32[16,1,4,128]{3,1,0,2:T(1,128)S(1)} %get-tuple-element.134), kind=kOutput, calls=%fused_computation.23 | convolution fusion | flops 12591104 | bytes 1146880 | tf_op jit(solution)/shard_map/tbj,tjk->tbk/dot_general | solution.py:68
  83.5 1.6 %convolution_add_fusion.7 = f32[8,4,128]{2,1,0:T(4,128)S(1)} fusion(f32[8,2,128,128]{3,2,1,0:T(8,128)} %bitcast.835, f32[8,2,4,128]{3,2,1,0:T(4,128)S(1)} %bitcast.872), kind=kOutput, calls=%fused_computation.29 | convolution fusion | flops 6295552 | bytes 573440 | tf_op jit(solution)/shard_map/tbj,tjk->tbk/dot_general | solution.py:68
  85.0 1.3 %convolution_add_fusion.11 = f32[4,4,128]{2,1,0:T(4,128)S(1)} fusion(f32[4,2,128,128]{3,2,1,0:T(8,128)} %bitcast.844, f32[4,2,4,128]{3,2,1,0:T(4,128)S(1)} %bitcast.880), kind=kOutput, calls=%fused_computation.35 | convolution fusion | flops 3147776 | bytes 286720 | tf_op jit(solution)/shard_map/tbj,tjk->tbk/dot_general | solution.py:68
  90.9 1.2 convolution_bitcast_fusion
  92.7 1.7 %collective-permute-done.9 = f32[4,128]{1,0:T(4,128)S(1)} collective-permute-done((f32[4,128]{1,0:T(4,128)S(1)}, f32[4,128]{1,0:T(4,128)S(1)}, u32[]{:S(2)}, u32[]{:S(2)}) %collective-permute-start.9) | collective-permute-done | bytes 2080 | tf_op jit(solution)/shard_map/ppermute | solution.py:77
  94.7 5.0 %collective-permute-done.10 = f32[4,128]{1,0:T(4,128)S(1)} collective-permute-done((f32[4,128]{1,0:T(4,128)S(1)}, f32[4,128]{1,0:T(4,128)S(1)}, u32[]{:S(2)}, u32[]{:S(2)}) %collective-permute-start.10) | collective-permute-done | bytes 2080 | tf_op jit(solution)/shard_map/ppermute | solution.py:77
  100.6 3.0 %collective-permute-done.11 = f32[4,128]{1,0:T(4,128)S(1)} collective-permute-done((f32[4,128]{1,0:T(4,128)S(1)}, f32[4,128]{1,0:T(4,128)S(1)}, u32[]{:S(2)}, u32[]{:S(2)}) %collective-permute-start.11) | collective-permute-done | bytes 2080 | tf_op jit(solution)/shard_map/ppermute | solution.py:77
  104.2 4.9 %collective-permute-done.12 = f32[4,128]{1,0:T(4,128)S(1)} collective-permute-done((f32[4,128]{1,0:T(4,128)S(1)}, f32[4,128]{1,0:T(4,128)S(1)}, u32[]{:S(2)}, u32[]{:S(2)}) %collective-permute-start.12) | collective-permute-done | bytes 2080 | tf_op jit(solution)/shard_map/ppermute | solution.py:77
  110.7 2.3 %collective-permute-done.13 = f32[4,128]{1,0:T(4,128)S(1)} collective-permute-done((f32[4,128]{1,0:T(4,128)S(1)}, f32[4,128]{1,0:T(4,128)S(1)}, u32[]{:S(2)}, u32[]{:S(2)}) %collective-permute-start.13) | collective-permute-done | bytes 2080 | tf_op jit(solution)/shard_map/ppermute | solution.py:77
  114.4 4.0 %collective-permute-done.14 = f32[4,128]{1,0:T(4,128)S(1)} collective-permute-done((f32[4,128]{1,0:T(4,128)S(1)}, f32[4,128]{1,0:T(4,128)S(1)}, u32[]{:S(2)}, u32[]{:S(2)}) %collective-permute-start.14) | collective-permute-done | bytes 2080 | tf_op jit(solution)/shard_map/ppermute | solution.py:77
  118.3 1.2 fusion.10
  119.5 1.2 fusion.302
  (270 shorter events, 35.9 us)
Async XLA Ops:
  0.6 14.1 %copy-start = (f32[32,4,64]{2,1,0:T(4,128)S(1)}, f32[32,4,64]{2,1,0:T(4,128)}, u32[]{:S(2)}) copy-start(f32[32,4,64]{2,1,0:T(4,128)} %param.6) | copy-start | bytes 98308
  1.4 15.8 %collective-permute-start = (f32[1,128]{1,0:T(1,128)S(1)}, f32[1,128]{1,0:T(1,128)S(1)}, u32[]{:S(2)}, u32[]{:S(2)}) collective-permute-start(f32[1,128]{1,0:T(1,128)S(1)} %slice.428), channel_id=1, source_target_pairs={{1,0},{2,1},{3,2},{4,3},{5,4},{6,5},{7,6},{8,7},{9,8},{10,9},{11,1... | collective-permute-start | bytes 1544 | tf_op jit(solution)/shard_map/ppermute | solution.py:16
  32.9 1.6 %collective-permute-start.1 = (f32[260,128]{1,0:T(8,128)S(1)}, f32[260,128]{1,0:T(8,128)S(1)}, u32[]{:S(2)}, u32[]{:S(2)}) collective-permute-start(f32[260,128]{1,0:T(8,128)S(1)} %pad_maximum_fusion.12), channel_id=1, source_target_pairs={{0,1},{1,0},{2,3},{3,2},{4,5},{5,4},{6,7},{7,6},{8,9},{9,8},{10,11... | collective-permute-start | bytes 399368 | tf_op jit(solution)/shard_map/ppermute | solution.py:77
  37.1 38.4 %copy-start.3 = (f32[4,128,128]{2,1,0:T(8,128)}, f32[4,128,128]{2,1,0:T(8,128)S(1)}, u32[]{:S(2)}) copy-start(f32[4,128,128]{2,1,0:T(8,128)S(1)} %fusion.16) | copy-start | bytes 786436
  37.4 5.7 %collective-permute-start.2 = (f32[260,128]{1,0:T(8,128)S(1)}, f32[260,128]{1,0:T(8,128)S(1)}, u32[]{:S(2)}, u32[]{:S(2)}) collective-permute-start(f32[260,128]{1,0:T(8,128)S(1)} %pad_maximum_fusion.13), channel_id=1, source_target_pairs={{0,2},{1,3},{2,0},{3,1},{4,6},{5,7},{6,4},{7,5},{8,10},{9,11},{10,... | collective-permute-start | bytes 399368 | tf_op jit(solution)/shard_map/ppermute | solution.py:77
  43.5 32.0 %copy-start.4 = (f32[4,128,128]{2,1,0:T(8,128)}, f32[4,128,128]{2,1,0:T(8,128)S(1)}, u32[]{:S(2)}) copy-start(f32[4,128,128]{2,1,0:T(8,128)S(1)} %fusion.31) | copy-start | bytes 786436
  43.8 6.6 %collective-permute-start.3 = (f32[260,128]{1,0:T(8,128)S(1)}, f32[260,128]{1,0:T(8,128)S(1)}, u32[]{:S(2)}, u32[]{:S(2)}) collective-permute-start(f32[260,128]{1,0:T(8,128)S(1)} %pad_maximum_fusion.14), channel_id=1, source_target_pairs={{0,4},{1,5},{2,6},{3,7},{4,0},{5,1},{6,2},{7,3},{8,12},{9,13},{10,... | collective-permute-start | bytes 399368 | tf_op jit(solution)/shard_map/ppermute | solution.py:77
  50.9 24.6 %copy-start.5 = (f32[4,128,128]{2,1,0:T(8,128)}, f32[4,128,128]{2,1,0:T(8,128)S(1)}, u32[]{:S(2)}) copy-start(f32[4,128,128]{2,1,0:T(8,128)S(1)} %fusion.46) | copy-start | bytes 786436
  51.2 5.3 %collective-permute-start.4 = (f32[260,128]{1,0:T(8,128)S(1)}, f32[260,128]{1,0:T(8,128)S(1)}, u32[]{:S(2)}, u32[]{:S(2)}) collective-permute-start(f32[260,128]{1,0:T(8,128)S(1)} %pad_maximum_fusion.15), channel_id=1, source_target_pairs={{0,8},{1,9},{2,10},{3,11},{4,12},{5,13},{6,14},{7,15},{8,0},{9,1},... | collective-permute-start | bytes 399368 | tf_op jit(solution)/shard_map/ppermute | solution.py:77
  57.0 18.5 %copy-start.6 = (f32[4,128,128]{2,1,0:T(8,128)}, f32[4,128,128]{2,1,0:T(8,128)S(1)}, u32[]{:S(2)}) copy-start(f32[4,128,128]{2,1,0:T(8,128)S(1)} %fusion.61) | copy-start | bytes 786436
  57.3 6.6 %collective-permute-start.5 = (f32[260,128]{1,0:T(8,128)S(1)}, f32[260,128]{1,0:T(8,128)S(1)}, u32[]{:S(2)}, u32[]{:S(2)}) collective-permute-start(f32[260,128]{1,0:T(8,128)S(1)} %pad_maximum_fusion.16), channel_id=1, source_target_pairs={{0,16},{1,17},{2,18},{3,19},{4,20},{5,21},{6,22},{7,23},{8,24},{9,... | collective-permute-start | bytes 399368 | tf_op jit(solution)/shard_map/ppermute | solution.py:77
  64.4 11.1 %copy-start.7 = (f32[4,128,128]{2,1,0:T(8,128)}, f32[4,128,128]{2,1,0:T(8,128)S(1)}, u32[]{:S(2)}) copy-start(f32[4,128,128]{2,1,0:T(8,128)S(1)} %fusion.76) | copy-start | bytes 786436
  64.7 5.1 %collective-permute-start.6 = (f32[260,128]{1,0:T(8,128)S(1)}, f32[260,128]{1,0:T(8,128)S(1)}, u32[]{:S(2)}, u32[]{:S(2)}) collective-permute-start(f32[260,128]{1,0:T(8,128)S(1)} %pad_maximum_fusion.17), channel_id=1, source_target_pairs={{0,32},{1,33},{2,34},{3,35},{4,36},{5,37},{6,38},{7,39},{8,40},{9,... | collective-permute-start | bytes 399368 | tf_op jit(solution)/shard_map/ppermute | solution.py:77
  65.5 11.4 %copy-start.27 = (f32[128,128]{1,0:T(8,128)S(1)}, f32[128,128]{1,0:T(8,128)}, u32[]{:S(2)}) copy-start(f32[128,128]{1,0:T(8,128)} %copy-done.26) | copy-start | bytes 196612
  65.6 11.4 %copy-start.45 = (f32[32,128]{1,0:T(8,128)S(1)}, f32[32,128]{1,0:T(8,128)}, u32[]{:S(2)}) copy-start(f32[32,128]{1,0:T(8,128)} %param.7) | copy-start | bytes 49156
  69.9 8.0 %copy-start.24 = (f32[128,128]{1,0:T(8,128)S(1)}, f32[128,128]{1,0:T(8,128)}, u32[]{:S(2)}) copy-start(f32[128,128]{1,0:T(8,128)} %param.11) | copy-start | bytes 196612
  70.1 5.4 %collective-permute-start.7 = (f32[4,128]{1,0:T(4,128)S(1)}, f32[4,128]{1,0:T(4,128)S(1)}, u32[]{:S(2)}, u32[]{:S(2)}) collective-permute-start(f32[4,128]{1,0:T(4,128)S(1)} %fusion.267), channel_id=1, source_target_pairs={{0,64},{1,65},{2,66},{3,67},{4,68},{5,69},{6,70},{7,71},{8,72},{9,... | collective-permute-start | bytes 6152 | tf_op jit(solution)/shard_map/ppermute | solution.py:77
  80.2 7.7 %copy-start.2 = (f32[4,128,128]{2,1,0:T(8,128)S(1)}, f32[4,128,128]{2,1,0:T(8,128)}, u32[]{:S(2)}) copy-start(f32[4,128,128]{2,1,0:T(8,128)} %get-tuple-element.36) | copy-start | bytes 786436
  86.7 1.2 collective-permute-start.8
  90.7 3.6 %collective-permute-start.9 = (f32[4,128]{1,0:T(4,128)S(1)}, f32[4,128]{1,0:T(4,128)S(1)}, u32[]{:S(2)}, u32[]{:S(2)}) collective-permute-start(f32[4,128]{1,0:T(4,128)S(1)} %fusion.264), channel_id=1, source_target_pairs={{0,2},{1,3},{2,0},{3,1},{4,6},{5,7},{6,4},{7,5},{8,10},{9,11},{10,... | collective-permute-start | bytes 6152 | tf_op jit(solution)/shard_map/ppermute | solution.py:77
  92.1 11.6 %copy-start.18 = (f32[1,128,128]{2,1,0:T(8,128)S(1)}, f32[1,128,128]{2,1,0:T(8,128)}, u32[]{:S(2)}) copy-start(f32[1,128,128]{2,1,0:T(8,128)} %copy-done.17) | copy-start | bytes 196612
  92.1 11.6 %copy-start.38 = (f32[1,128,128]{2,1,0:T(8,128)S(1)}, f32[1,128,128]{2,1,0:T(8,128)}, u32[]{:S(2)}) copy-start(f32[1,128,128]{2,1,0:T(8,128)} %copy-done.37) | copy-start | bytes 196612
  92.1 12.0 %copy-start.28 = (f32[32,4,128]{2,0,1:T(8,128)S(1)}, f32[32,4,128]{2,0,1:T(8,128)}, u32[]{:S(2)}) copy-start(f32[32,4,128]{2,0,1:T(8,128)} %rev.10) | copy-start | bytes 196612
  92.1 16.9 %copy-start.20 = (f32[1,128,128]{2,1,0:T(8,128)S(1)}, f32[1,128,128]{2,1,0:T(8,128)}, u32[]{:S(2)}) copy-start(f32[1,128,128]{2,1,0:T(8,128)} %copy-done.19) | copy-start | bytes 196612
  92.2 16.9 %copy-start.42 = (f32[1,128,128]{2,1,0:T(8,128)S(1)}, f32[1,128,128]{2,1,0:T(8,128)}, u32[]{:S(2)}) copy-start(f32[1,128,128]{2,1,0:T(8,128)} %copy-done.41) | copy-start | bytes 196612
  92.4 20.6 %copy-start.40 = (f32[1,128,128]{2,1,0:T(8,128)S(1)}, f32[1,128,128]{2,1,0:T(8,128)}, u32[]{:S(2)}) copy-start(f32[1,128,128]{2,1,0:T(8,128)} %copy-done.39) | copy-start | bytes 196612
  92.4 20.6 %copy-start.44 = (f32[1,128,128]{2,1,0:T(8,128)S(1)}, f32[1,128,128]{2,1,0:T(8,128)}, u32[]{:S(2)}) copy-start(f32[1,128,128]{2,1,0:T(8,128)} %copy-done.43) | copy-start | bytes 196612
  94.6 5.2 %collective-permute-start.10 = (f32[4,128]{1,0:T(4,128)S(1)}, f32[4,128]{1,0:T(4,128)S(1)}, u32[]{:S(2)}, u32[]{:S(2)}) collective-permute-start(f32[4,128]{1,0:T(4,128)S(1)} %fusion.263), channel_id=1, source_target_pairs={{0,4},{1,5},{2,6},{3,7},{4,0},{5,1},{6,2},{7,3},{8,12},{9,13},{10,... | collective-permute-start | bytes 6152 | tf_op jit(solution)/shard_map/ppermute | solution.py:77
  100.0 3.6 %collective-permute-start.11 = (f32[4,128]{1,0:T(4,128)S(1)}, f32[4,128]{1,0:T(4,128)S(1)}, u32[]{:S(2)}, u32[]{:S(2)}) collective-permute-start(f32[4,128]{1,0:T(4,128)S(1)} %fusion.262), channel_id=1, source_target_pairs={{0,8},{1,9},{2,10},{3,11},{4,12},{5,13},{6,14},{7,15},{8,0},{9,1},... | collective-permute-start | bytes 6152 | tf_op jit(solution)/shard_map/ppermute | solution.py:77
  103.9 5.2 %collective-permute-start.12 = (f32[4,128]{1,0:T(4,128)S(1)}, f32[4,128]{1,0:T(4,128)S(1)}, u32[]{:S(2)}, u32[]{:S(2)}) collective-permute-start(f32[4,128]{1,0:T(4,128)S(1)} %fusion.261), channel_id=1, source_target_pairs={{0,16},{1,17},{2,18},{3,19},{4,20},{5,21},{6,22},{7,23},{8,24},{9,... | collective-permute-start | bytes 6152 | tf_op jit(solution)/shard_map/ppermute | solution.py:77
  109.3 3.6 %collective-permute-start.13 = (f32[4,128]{1,0:T(4,128)S(1)}, f32[4,128]{1,0:T(4,128)S(1)}, u32[]{:S(2)}, u32[]{:S(2)}) collective-permute-start(f32[4,128]{1,0:T(4,128)S(1)} %fusion.260), channel_id=1, source_target_pairs={{0,32},{1,33},{2,34},{3,35},{4,36},{5,37},{6,38},{7,39},{8,40},{9,... | collective-permute-start | bytes 6152 | tf_op jit(solution)/shard_map/ppermute | solution.py:77
  113.2 5.2 %collective-permute-start.14 = (f32[4,128]{1,0:T(4,128)S(1)}, f32[4,128]{1,0:T(4,128)S(1)}, u32[]{:S(2)}, u32[]{:S(2)}) collective-permute-start(f32[4,128]{1,0:T(4,128)S(1)} %fusion.259), channel_id=1, source_target_pairs={{0,64},{1,65},{2,66},{3,67},{4,68},{5,69},{6,70},{7,71},{8,72},{9,... | collective-permute-start | bytes 6152 | tf_op jit(solution)/shard_map/ppermute | solution.py:77
  (32 other events, 144.2 us)
where the time goes:
time: 123 us; the launch traced here: 122 us
  waiting for transfers between devices  50.6 us (41%)
  matrix products  35.3 us (29%)
  local copies, waits for them, and re-layouts  15.8 us (13%)
  starting transfers between devices  12.1 us (10%)
  other arithmetic  5.96 us (5%)
  between operations  1.97 us (2%)
    ppermute x14, waiting for transfers between devices, exchanged(): return lax.ppermute(x, 'tm', [(i, i ^ bit) for i in range(count)])  50.6 us
    ppermute x1, starting transfers between devices, shifted(): return lax.ppermute(x, 'tm', pairs)  8.09 us
    slice x4, local copies, waits for them, and re-layouts, local(): backward_tree = [(m[1], None) for m, _ in tree]  5.5 us
    dot_general x5, matrix products, up_sweep_adds(): jnp.einsum('tbj,tjk->tbk', halves[:, 0], pairs[:, 1], precision=HIGHEST)  5.47 us
    dot_general x8, matrix products, down_sweep_maps(): odd = jnp.einsum('tij,tjk->tik', excl, left, precision=HIGHEST)  5 us
    dot_general x18, matrix products, batched(): jnp.einsum('kij,kjl->kil', jnp.stack(lhs), jnp.stack(rhs), precision=HIGH...  4.97 us
    dot_general x5, matrix products, local(): jnp.einsum('dtij,dtjk->dtik', pairs[:, :, 0], pairs[:, :, 1], precision=H...  4.8 us
    dot_general x8, matrix products, down_sweep_adds(): jnp.einsum('tbj,tjk->tbk', excl, left_map, precision=HIGHEST) + left_add  4.08 us
  transfers between devices with their start and end apart: 15, of which 14 were waited for; matrix products, arithmetic and copies ran while one was open for 13% of the time, Pallas kernels for 0%

commit v1 on v0

--- a/solution.py
+++ b/solution.py
@@ -3,11 +3,11 @@
 from jax import lax
 from jax.sharding import PartitionSpec as P
 
-HIGHEST = lax.Precision.HIGHEST
+PRECISION = lax.Precision.HIGHEST
 
 
 def dot(a, b):
-    return jnp.dot(a, b, precision=HIGHEST)
+    return jnp.dot(a, b, precision=PRECISION)
 
 
 def shifted(x, by):
@@ -23,10 +23,10 @@
         if adds is not None:
             halves = adds.reshape((-1, 2) + adds.shape[1:])
             adds = (
-                jnp.einsum("tbj,tjk->tbk", halves[:, 0], pairs[:, 1], precision=HIGHEST)
+                jnp.einsum("tbj,tjk->tbk", halves[:, 0], pairs[:, 1], precision=PRECISION)
                 + halves[:, 1]
             )
-        maps = jnp.einsum("tij,tjk->tik", pairs[:, 0], pairs[:, 1], precision=HIGHEST)
+        maps = jnp.einsum("tij,tjk->tik", pairs[:, 0], pairs[:, 1], precision=PRECISION)
         levels.append((maps, adds))
     return levels
 
@@ -40,7 +40,7 @@
             excl = jnp.eye(size, dtype=jnp.float32)[None]
             odd = left
         else:
-            odd = jnp.einsum("tij,tjk->tik", excl, left, precision=HIGHEST)
+            odd = jnp.einsum("tij,tjk->tik", excl, left, precision=PRECISION)
         excl = jnp.stack([excl, odd], 1).reshape((-1,) + maps.shape[1:])
     return excl
 
@@ -54,7 +54,7 @@
             excl = jnp.zeros_like(left_add[:1])
             odd = left_add
         else:
-            odd = jnp.einsum("tbj,tjk->tbk", excl, left_map, precision=HIGHEST) + left_add
+            odd = jnp.einsum("tbj,tjk->tbk", excl, left_map, precision=PRECISION) + left_add
         excl = jnp.stack([excl, odd], 1).reshape((-1,) + adds.shape[1:])
     return excl
 
@@ -65,7 +65,7 @@
         pairs = maps.reshape((-1, 2) + maps.shape[1:])
         halves = adds.reshape((-1, 2) + adds.shape[1:])
         adds = (
-            jnp.einsum("tbj,tjk->tbk", halves[:, 0], pairs[:, 1], precision=HIGHEST)
+            jnp.einsum("tbj,tjk->tbk", halves[:, 0], pairs[:, 1], precision=PRECISION)
             + halves[:, 1]
         )
         out.append(adds)
@@ -78,7 +78,7 @@
 
 
 def batched(lhs, rhs):
-    return jnp.einsum("kij,kjl->kil", jnp.stack(lhs), jnp.stack(rhs), precision=HIGHEST)
+    return jnp.einsum("kij,kjl->kil", jnp.stack(lhs), jnp.stack(rhs), precision=PRECISION)
 
 
 def local(observations, decay, transition, obs_map, noise_precision, smoother_gain):
@@ -87,7 +87,7 @@
     index = lax.axis_index("tm")
     gain_rows = obs_map * noise_precision[:, None]
     closed_rows = transition.T - dot(transition.T, dot(obs_map.T, gain_rows))
-    forward_adds = jnp.einsum("wyn,nx->wyx", observations, gain_rows, precision=HIGHEST)
+    forward_adds = jnp.einsum("wyn,nx->wyx", observations, gain_rows, precision=PRECISION)
 
     following = shifted(decay[:1], -1)
     upcoming = jnp.concatenate([decay[1:], following], 0)
@@ -101,10 +101,10 @@
         pairs = maps.reshape((2, -1, 2) + maps.shape[2:])
         halves = adds.reshape((-1, 2) + adds.shape[1:])
         adds = (
-            jnp.einsum("tbj,tjk->tbk", halves[:, 0], pairs[0, :, 1], precision=HIGHEST)
+            jnp.einsum("tbj,tjk->tbk", halves[:, 0], pairs[0, :, 1], precision=PRECISION)
             + halves[:, 1]
         )
-        maps = jnp.einsum("dtij,dtjk->dtik", pairs[:, :, 0], pairs[:, :, 1], precision=HIGHEST)
+        maps = jnp.einsum("dtij,dtjk->dtik", pairs[:, :, 0], pairs[:, :, 1], precision=PRECISION)
         tree.append((maps, adds))
     forward_tree = [(m[0], a) for m, a in tree]
     backward_tree = [(m[1], None) for m, _ in tree]
@@ -149,20 +149,23 @@
         back_total = products[2]
         back_before = jnp.where(upper, back_before, products[3])
 
-    excl_maps = down_sweep_maps(late)
-    excl_adds = down_sweep_adds(late, [a for _, a in late])
-    previous = jnp.einsum("bs,tsr->tbr", entering, excl_maps, precision=HIGHEST) + excl_adds
-    filtered = (
-        jnp.einsum("tbs,sr->tbr", previous * decay[:, None, :], closed_rows, precision=HIGHEST)
-        + forward_adds
+    excl_maps = down_sweep_maps(late)[::-1]
+    excl_adds = down_sweep_adds(late, [a for _, a in late])[::-1]
+    decay_back = decay[::-1][:, None, :]
+    ahead_back = upcoming[::-1][:, None, :]
+    previous = jnp.einsum("bs,tsr->tbr", entering, excl_maps, precision=PRECISION) + excl_adds
+    filtered_back = (
+        jnp.einsum("tbs,sr->tbr", previous * decay_back, closed_rows, precision=PRECISION)
+        + forward_adds[::-1]
     )
     predicted = jnp.einsum(
-        "tbs,sr->tbr", filtered * upcoming[:, None, :], transition.T, precision=HIGHEST
-    )
-    backward_adds = filtered - jnp.einsum(
-        "tbs,sr->tbr", predicted * upcoming[:, None, :], smoother_gain.T, precision=HIGHEST
-    )
-    back_adds = up_sweep_adds(backward_tree, backward_adds[::-1])
+        "tbs,sr->tbr", filtered_back * ahead_back, transition.T, precision=PRECISION
+    )
+    backward_adds = filtered_back - jnp.einsum(
+        "tbs,sr->tbr", predicted * ahead_back, smoother_gain.T, precision=PRECISION
+    )
+    back_adds = up_sweep_adds(backward_tree, backward_adds)
+    filtered = filtered_back[::-1]
 
     total_add = back_adds[-1][0]
     before_add = jnp.zeros_like(total_add)
@@ -185,14 +188,14 @@
     back_excl_maps = down_sweep_maps(late_b[0])
     back_excl_adds = down_sweep_adds(late_b[0], late_b[1])
     following_state = (
-        jnp.einsum("bs,tsr->tbr", arriving, back_excl_maps, precision=HIGHEST) + back_excl_adds
-    )[::-1]
+        jnp.einsum("bs,tsr->tbr", arriving, back_excl_maps, precision=PRECISION) + back_excl_adds
+    )
     smoothed = (
         jnp.einsum(
-            "tbs,sr->tbr", following_state * upcoming[:, None, :], smoother_gain.T, precision=HIGHEST
+            "tbs,sr->tbr", following_state * ahead_back, smoother_gain.T, precision=PRECISION
         )
         + backward_adds
-    )
+    )[::-1]
     return filtered, smoothed
 
 

time: 123 us -> 137 us (1.11)
  waiting for transfers between devices: 50.6 us -> 38.2 us
  local copies, waits for them, and re-layouts: 15.8 us -> 27.5 us
  other arithmetic: 5.96 us -> 15.1 us
  starting transfers between devices: 12.1 us -> 14.5 us
  matrix products: 35.3 us -> 37.3 us
    ppermute x14, waiting for transfers between devices: 50.6 us -> 38.2 us  [exchanged(): return lax.ppermute(x, 'tm', [(i, i ^ bit) for i in range(count)])]
    rev x2 -> x6, local copies, waits for them, and re-layouts: 1.48 us -> 7.46 us  [the longest x1 3.16 us: local(): excl_maps = down_sweep_maps(late)[::-1]]
    unnamed x100 -> x146, local copies, waits for them, and re-layouts: 3.21 us -> 6.47 us
    ppermute x14, starting transfers between devices: 4.05 us -> 6.44 us  [exchanged(): return lax.ppermute(x, 'tm', [(i, i ^ bit) for i in range(count)])]
    dot_general x60, matrix products: 35.3 us -> 37.3 us  [the longest x18 6.82 us: batched(): jnp.einsum('kij,kjl->kil', jnp.stack(lhs), jnp.stack(rhs), precision=PREC...]
    another operation x6, other arithmetic: 0.18 us -> 2.17 us  [batched(): jnp.stack(rhs)]
    another operation x12, other arithmetic: 0.06 us -> 1.48 us  [batched(): jnp.stack(lhs)]
    add x6, other arithmetic: 0.04 us -> 1.42 us  [local(): total_map, total_add = (products[0], offsets[0] + second_add)]
  transfers between devices with their start and end apart: 15 -> 15, of which waited for: 14 -> 13; matrix products, arithmetic and copies ran while one was open for 13% -> 20% of each run, Pallas kernels for 0% -> 0%
where the time goes in v1:
time: 137 us; the launch traced here: 134 us
  waiting for transfers between devices  38.2 us (28%)
  matrix products  37.3 us (27%)
  local copies, waits for them, and re-layouts  27.5 us (20%)
  other arithmetic  15.1 us (11%)
  starting transfers between devices  14.5 us (11%)
  between operations  1.92 us (1%)
    ppermute x14, waiting for transfers between devices, exchanged(): return lax.ppermute(x, 'tm', [(i, i ^ bit) for i in range(count)])  38.2 us
    ppermute x1, starting transfers between devices, shifted(): return lax.ppermute(x, 'tm', pairs)  8.09 us
    dot_general x18, matrix products, batched(): jnp.einsum('kij,kjl->kil', jnp.stack(lhs), jnp.stack(rhs), precision=PREC...  6.82 us
    dot_general x8, matrix products, down_sweep_maps(): odd = jnp.einsum('tij,tjk->tik', excl, left, precision=PRECISION)  6.62 us
    unnamed x146, local copies, waits for them, and re-layouts  6.47 us
    ppermute x14, starting transfers between devices, exchanged(): return lax.ppermute(x, 'tm', [(i, i ^ bit) for i in range(count)])  6.44 us
    slice x4, local copies, waits for them, and re-layouts, local(): backward_tree = [(m[1], None) for m, _ in tree]  5.58 us
    dot_general x8, matrix products, down_sweep_adds(): jnp.einsum('tbj,tjk->tbk', excl, left_map, precision=PRECISION) + left_add  4.99 us
  transfers between devices with their start and end apart: 15, of which 13 were waited for; matrix products, arithmetic and copies ran while one was open for 20% of the time, Pallas kernels for 0%

profile of v1, /device:TPU:6, one launch (start us, length us, event | category | flops | bytes accessed | tf_op | source)
XLA Modules:
  0.0 134.5 jit_solution(6710314853946323349)
XLA Ops:
  1.4 8.1 %collective-permute-start = (f32[1,128]{1,0:T(1,128)S(1)}, f32[1,128]{1,0:T(1,128)S(1)}, u32[]{:S(2)}, u32[]{:S(2)}) collective-permute-start(f32[1,128]{1,0:T(1,128)S(1)} %slice.428), channel_id=1, source_target_pairs={{1,0},{2,1},{3,2},{4,3},{5,4},{6,5},{7,6},{8,7},{9,8},{10,9},{11,1... | collective-permute-start | bytes 1544 | tf_op jit(solution)/shard_map/ppermute | solution.py:16
  10.8 1.3 rev.25
  12.2 1.2 fusion.202
  19.3 1.1 broadcast_multiply_fusion.1
  20.5 2.2 %fusion.297 = (f32[1,32,128,128]{3,2,1,0:T(8,128)}, f32[32,128,128]{2,1,0:T(8,128)S(1)}, f32[32,128,128]{2,1,0:T(8,128)S(1)}) fusion(f32[2,32,128,128]{3,2,1,0:T(8,128)S(1)} %broadcast_multiply_fusion.1), kind=kLoop, calls=%fused_computation.548 | loop fusion | bytes 10485760 | tf_op jit(solution)/shard_map/slice | solution.py:110
  22.7 1.1 broadcast_multiply_fusion
  23.8 2.3 %fusion = f32[2,16,128,128]{3,2,1,0:T(8,128)S(1)} fusion(f32[2,16,2,128,128]{4,3,1,0,2:T(8,128)S(1)} %broadcast_multiply_fusion), kind=kOutput, calls=%fused_computation.1 | convolution fusion | flops 805306368 | bytes 6291456 | tf_op jit(solution)/shard_map/dtij,dtjk->dtik/dot_general | solution.py:107
  26.1 1.3 fusion.298
  27.5 1.2 fusion.13
  28.7 1.2 fusion.299
  43.9 1.5 %rev.24 = f32[32,4,128]{2,0,1:T(8,128)} reverse(f32[32,4,128]{2,0,1:T(8,128)} %bitcast.867), dimensions={0} | reverse | bytes 131072 | tf_op jit(solution)/shard_map/rev | solution.py:153
  46.5 1.6 %collective-permute-done.2 = f32[260,128]{1,0:T(8,128)} collective-permute-done((f32[260,128]{1,0:T(8,128)}, f32[260,128]{1,0:T(8,128)}, u32[]{:S(2)}, u32[]{:S(2)}) %collective-permute-start.2) | collective-permute-done | bytes 133152 | tf_op jit(solution)/shard_map/ppermute | solution.py:77
  52.6 5.8 %collective-permute-done.3 = f32[260,128]{1,0:T(8,128)S(1)} collective-permute-done((f32[260,128]{1,0:T(8,128)S(1)}, f32[260,128]{1,0:T(8,128)S(1)}, u32[]{:S(2)}, u32[]{:S(2)}) %collective-permute-start.3) | collective-permute-done | bytes 133152 | tf_op jit(solution)/shard_map/ppermute | solution.py:77
  60.0 4.6 %collective-permute-done.4 = f32[260,128]{1,0:T(8,128)S(1)} collective-permute-done((f32[260,128]{1,0:T(8,128)S(1)}, f32[260,128]{1,0:T(8,128)S(1)}, u32[]{:S(2)}, u32[]{:S(2)}) %collective-permute-start.4) | collective-permute-done | bytes 133152 | tf_op jit(solution)/shard_map/ppermute | solution.py:77
  65.9 1.2 convolution_bitcast_fusion.1
  67.1 4.9 %collective-permute-done.5 = f32[260,128]{1,0:T(8,128)S(1)} collective-permute-done((f32[260,128]{1,0:T(8,128)S(1)}, f32[260,128]{1,0:T(8,128)S(1)}, u32[]{:S(2)}, u32[]{:S(2)}) %collective-permute-start.5) | collective-permute-done | bytes 133152 | tf_op jit(solution)/shard_map/ppermute | solution.py:77
  74.6 1.5 %copy.87 = f32[16,2,128,128]{3,2,1,0:T(8,128)} copy(f32[16,2,128,128]{3,2,0,1:T(8,128)S(1)} %pad_maximum_fusion) | data formatting | bytes 4194304 | tf_op jit(solution)/shard_map/stack | solution.py:44
  76.1 3.2 %rev.23 = f32[32,128,128]{2,1,0:T(8,128)} reverse(f32[32,128,128]{2,1,0:T(8,128)} %bitcast.823), dimensions={0} | reverse | bytes 4194304 | tf_op jit(solution)/shard_map/rev | solution.py:152
  84.0 1.4 %fusion.91 = f32[4,128,128]{2,1,0:T(8,128)S(1)} fusion(f32[1,128,128]{2,1,0:T(8,128)S(1)} %get-tuple-element.109, f32[1,128,128]{2,1,0:T(8,128)S(1)} %get-tuple-element.64, f32[1,128,128]{2,1,0:T(8,128)S(1)} %get-tuple-element.108, f32[1,128,128]{2,1,0:T(8,128)S(1)} %get-tuple-element.63, f32[1,128,128]{2,1,0:T(8,128)} %get-tuple-element.88, ...), kind=kOutput, calls=%fused_computation.157 | convolution fusion | flops 101056512 | bytes 786432 | tf_op jit(solution)/shard_map/kij,kjl->kil/dot_general | solution.py:81
  85.4 2.7 %collective-permute-done.7 = f32[4,128]{1,0:T(4,128)S(1)} collective-permute-done((f32[4,128]{1,0:T(4,128)S(1)}, f32[4,128]{1,0:T(4,128)S(1)}, u32[]{:S(2)}, u32[]{:S(2)}) %collective-permute-start.7) | collective-permute-done | bytes 2080 | tf_op jit(solution)/shard_map/ppermute | solution.py:77
  88.1 1.2 fusion.12
  89.3 1.2 fusion.303
  98.4 1.2 convolution_bitcast_fusion.6
  99.5 1.1 fusion.7
  104.3 1.2 convolution_bitcast_fusion
  107.8 4.8 %collective-permute-done.10 = f32[4,128]{1,0:T(4,128)S(1)} collective-permute-done((f32[4,128]{1,0:T(4,128)S(1)}, f32[4,128]{1,0:T(4,128)S(1)}, u32[]{:S(2)}, u32[]{:S(2)}) %collective-permute-start.10) | collective-permute-done | bytes 2080 | tf_op jit(solution)/shard_map/ppermute | solution.py:77
  113.5 3.0 %collective-permute-done.11 = f32[4,128]{1,0:T(4,128)S(1)} collective-permute-done((f32[4,128]{1,0:T(4,128)S(1)}, f32[4,128]{1,0:T(4,128)S(1)}, u32[]{:S(2)}, u32[]{:S(2)}) %collective-permute-start.11) | collective-permute-done | bytes 2080 | tf_op jit(solution)/shard_map/ppermute | solution.py:77
  117.4 4.5 %collective-permute-done.12 = f32[4,128]{1,0:T(4,128)S(1)} collective-permute-done((f32[4,128]{1,0:T(4,128)S(1)}, f32[4,128]{1,0:T(4,128)S(1)}, u32[]{:S(2)}, u32[]{:S(2)}) %collective-permute-start.12) | collective-permute-done | bytes 2080 | tf_op jit(solution)/shard_map/ppermute | solution.py:77
  122.1 1.7 %collective-permute-start.13 = (f32[4,128]{1,0:T(4,128)S(1)}, f32[4,128]{1,0:T(4,128)S(1)}, u32[]{:S(2)}, u32[]{:S(2)}) collective-permute-start(f32[4,128]{1,0:T(4,128)S(1)} %fusion.262), channel_id=1, source_target_pairs={{0,32},{1,33},{2,34},{3,35},{4,36},{5,37},{6,38},{7,39},{8,40},{9,... | collective-permute-start | bytes 6152 | tf_op jit(solution)/shard_map/ppermute | solution.py:77
  127.3 3.9 %collective-permute-done.14 = f32[4,128]{1,0:T(4,128)S(1)} collective-permute-done((f32[4,128]{1,0:T(4,128)S(1)}, f32[4,128]{1,0:T(4,128)S(1)}, u32[]{:S(2)}, u32[]{:S(2)}) %collective-permute-start.14) | collective-permute-done | bytes 2080 | tf_op jit(solution)/shard_map/ppermute | solution.py:77
  131.2 1.2 fusion.10
  132.3 1.2 fusion.304
  (319 shorter events, 57.2 us)
Async XLA Ops:
  0.6 12.7 %copy-start = (f32[32,4,64]{2,1,0:T(4,128)S(1)}, f32[32,4,64]{2,1,0:T(4,128)}, u32[]{:S(2)}) copy-start(f32[32,4,64]{2,1,0:T(4,128)} %param.6) | copy-start | bytes 98308
  1.4 17.2 %collective-permute-start = (f32[1,128]{1,0:T(1,128)S(1)}, f32[1,128]{1,0:T(1,128)S(1)}, u32[]{:S(2)}, u32[]{:S(2)}) collective-permute-start(f32[1,128]{1,0:T(1,128)S(1)} %slice.428), channel_id=1, source_target_pairs={{1,0},{2,1},{3,2},{4,3},{5,4},{6,5},{7,6},{8,7},{9,8},{10,9},{11,1... | collective-permute-start | bytes 1544 | tf_op jit(solution)/shard_map/ppermute | solution.py:16
  22.7 19.5 %copy-start.1 = (f32[32,128,128]{2,1,0:T(8,128)}, f32[32,128,128]{2,1,0:T(8,128)S(1)}, u32[]{:S(2)}) copy-start(f32[32,128,128]{2,1,0:T(8,128)S(1)} %get-tuple-element.28) | copy-start | bytes 6291460
  27.5 9.6 %copy-start.5 = (f32[16,128,128]{2,1,0:T(8,128)}, f32[16,128,128]{2,1,0:T(8,128)S(1)}, u32[]{:S(2)}) copy-start(f32[16,128,128]{2,1,0:T(8,128)S(1)} %get-tuple-element.27) | copy-start | bytes 3145732
  34.4 1.6 %collective-permute-start.1 = (f32[260,128]{1,0:T(8,128)S(1)}, f32[260,128]{1,0:T(8,128)S(1)}, u32[]{:S(2)}, u32[]{:S(2)}) collective-permute-start(f32[260,128]{1,0:T(8,128)S(1)} %pad_maximum_fusion.12), channel_id=1, source_target_pairs={{0,1},{1,0},{2,3},{3,2},{4,5},{5,4},{6,7},{7,6},{8,9},{9,8},{10,11... | collective-permute-start | bytes 399368 | tf_op jit(solution)/shard_map/ppermute | solution.py:77
  42.2 6.0 %collective-permute-start.2 = (f32[260,128]{1,0:T(8,128)}, f32[260,128]{1,0:T(8,128)}, u32[]{:S(2)}, u32[]{:S(2)}) collective-permute-start(f32[260,128]{1,0:T(8,128)} %pad_maximum_fusion.13), channel_id=1, source_target_pairs={{0,2},{1,3},{2,0},{3,1},{4,6},{5,7},{6,4},{7,5},{8,10},{9,11},{10,... | collective-permute-start | bytes 399368 | tf_op jit(solution)/shard_map/ppermute | solution.py:77
  51.8 6.6 %collective-permute-start.3 = (f32[260,128]{1,0:T(8,128)S(1)}, f32[260,128]{1,0:T(8,128)S(1)}, u32[]{:S(2)}, u32[]{:S(2)}) collective-permute-start(f32[260,128]{1,0:T(8,128)S(1)} %pad_maximum_fusion.14), channel_id=1, source_target_pairs={{0,4},{1,5},{2,6},{3,7},{4,0},{5,1},{6,2},{7,3},{8,12},{9,13},{10,... | collective-permute-start | bytes 399368 | tf_op jit(solution)/shard_map/ppermute | solution.py:77
  59.2 5.3 %collective-permute-start.4 = (f32[260,128]{1,0:T(8,128)S(1)}, f32[260,128]{1,0:T(8,128)S(1)}, u32[]{:S(2)}, u32[]{:S(2)}) collective-permute-start(f32[260,128]{1,0:T(8,128)S(1)} %pad_maximum_fusion.15), channel_id=1, source_target_pairs={{0,8},{1,9},{2,10},{3,11},{4,12},{5,13},{6,14},{7,15},{8,0},{9,1},... | collective-permute-start | bytes 399368 | tf_op jit(solution)/shard_map/ppermute | solution.py:77
  65.4 6.6 %collective-permute-start.5 = (f32[260,128]{1,0:T(8,128)S(1)}, f32[260,128]{1,0:T(8,128)S(1)}, u32[]{:S(2)}, u32[]{:S(2)}) collective-permute-start(f32[260,128]{1,0:T(8,128)S(1)} %pad_maximum_fusion.16), channel_id=1, source_target_pairs={{0,16},{1,17},{2,18},{3,19},{4,20},{5,21},{6,22},{7,23},{8,24},{9,... | collective-permute-start | bytes 399368 | tf_op jit(solution)/shard_map/ppermute | solution.py:77
  74.1 5.3 %collective-permute-start.6 = (f32[260,128]{1,0:T(8,128)}, f32[260,128]{1,0:T(8,128)}, u32[]{:S(2)}, u32[]{:S(2)}) collective-permute-start(f32[260,128]{1,0:T(8,128)} %pad_maximum_fusion.17), channel_id=1, source_target_pairs={{0,32},{1,33},{2,34},{3,35},{4,36},{5,37},{6,38},{7,39},{8,40},{9,... | collective-permute-start | bytes 399368 | tf_op jit(solution)/shard_map/ppermute | solution.py:77
  79.2 10.1 %copy-start.3 = (f32[32,128,128]{2,1,0:T(8,128)S(1)}, f32[32,128,128]{2,1,0:T(8,128)}, u32[]{:S(2)}) copy-start(f32[32,128,128]{2,1,0:T(8,128)} %rev.23) | copy-start | bytes 6291460
  79.2 11.3 %copy-start.35 = (f32[128,128]{1,0:T(8,128)S(1)}, f32[128,128]{1,0:T(8,128)}, u32[]{:S(2)}) copy-start(f32[128,128]{1,0:T(8,128)} %copy-done.34) | copy-start | bytes 196612
  79.2 11.3 %copy-start.52 = (f32[32,4,128]{2,0,1:T(8,128)S(1)}, f32[32,4,128]{2,0,1:T(8,128)}, u32[]{:S(2)}) copy-start(f32[32,4,128]{2,0,1:T(8,128)} %rev.26) | copy-start | bytes 196612
  79.2 11.3 %copy-start.53 = (f32[32,4,128]{2,0,1:T(8,128)S(1)}, f32[32,4,128]{2,0,1:T(8,128)}, u32[]{:S(2)}) copy-start(f32[32,4,128]{2,0,1:T(8,128)} %rev.24) | copy-start | bytes 196612
  79.2 11.3 %copy-start.61 = (f32[32,128]{1,0:T(8,128)S(1)}, f32[32,128]{1,0:T(8,128)}, u32[]{:S(2)}) copy-start(f32[32,128]{1,0:T(8,128)} %rev.25) | copy-start | bytes 49156
  80.5 10.3 %copy-start.38 = (f32[128,128]{1,0:T(8,128)S(1)}, f32[128,128]{1,0:T(8,128)}, u32[]{:S(2)}) copy-start(f32[128,128]{1,0:T(8,128)} %param.8) | copy-start | bytes 196612
  81.2 10.2 %copy-start.36 = (f32[128,128]{1,0:T(8,128)S(1)}, f32[128,128]{1,0:T(8,128)}, u32[]{:S(2)}) copy-start(f32[128,128]{1,0:T(8,128)} %param.11) | copy-start | bytes 196612
  83.0 5.1 %collective-permute-start.7 = (f32[4,128]{1,0:T(4,128)S(1)}, f32[4,128]{1,0:T(4,128)S(1)}, u32[]{:S(2)}, u32[]{:S(2)}) collective-permute-start(f32[4,128]{1,0:T(4,128)S(1)} %fusion.269), channel_id=1, source_target_pairs={{0,64},{1,65},{2,66},{3,67},{4,68},{5,69},{6,70},{7,71},{8,72},{9,... | collective-permute-start | bytes 6152 | tf_op jit(solution)/shard_map/ppermute | solution.py:77
  95.2 1.6 %collective-permute-start.8 = (f32[4,128]{1,0:T(4,128)}, f32[4,128]{1,0:T(4,128)S(1)}, u32[]{:S(2)}, u32[]{:S(2)}) collective-permute-start(f32[4,128]{1,0:T(4,128)} %convolution_add_fusion.19), channel_id=1, source_target_pairs={{0,1},{1,0},{2,3},{3,2},{4,5},{5,4},{6,7},{7,6},{8,9},{9,8},{10,11... | collective-permute-start | bytes 6152 | tf_op jit(solution)/shard_map/ppermute | solution.py:77
  103.6 3.6 %collective-permute-start.9 = (f32[4,128]{1,0:T(4,128)S(1)}, f32[4,128]{1,0:T(4,128)S(1)}, u32[]{:S(2)}, u32[]{:S(2)}) collective-permute-start(f32[4,128]{1,0:T(4,128)S(1)} %fusion.266), channel_id=1, source_target_pairs={{0,2},{1,3},{2,0},{3,1},{4,6},{5,7},{6,4},{7,5},{8,10},{9,11},{10,... | collective-permute-start | bytes 6152 | tf_op jit(solution)/shard_map/ppermute | solution.py:77
  105.6 10.9 %copy-start.28 = (f32[1,128,128]{2,1,0:T(8,128)S(1)}, f32[1,128,128]{2,1,0:T(8,128)}, u32[]{:S(2)}) copy-start(f32[1,128,128]{2,1,0:T(8,128)} %copy-done.27) | copy-start | bytes 196612
  105.6 10.9 %copy-start.46 = (f32[1,128,128]{2,1,0:T(8,128)S(1)}, f32[1,128,128]{2,1,0:T(8,128)}, u32[]{:S(2)}) copy-start(f32[1,128,128]{2,1,0:T(8,128)} %copy-done.45) | copy-start | bytes 196612
  105.6 11.7 %copy-start.21 = (f32[32,4,128]{2,0,1:T(8,128)S(1)}, f32[32,4,128]{2,0,1:T(8,128)}, u32[]{:S(2)}) copy-start(f32[32,4,128]{2,0,1:T(8,128)} %copy-done.20) | copy-start | bytes 196612
  105.6 16.3 %copy-start.30 = (f32[1,128,128]{2,1,0:T(8,128)S(1)}, f32[1,128,128]{2,1,0:T(8,128)}, u32[]{:S(2)}) copy-start(f32[1,128,128]{2,1,0:T(8,128)} %copy-done.29) | copy-start | bytes 196612
  105.6 16.3 %copy-start.49 = (f32[1,128,128]{2,1,0:T(8,128)S(1)}, f32[1,128,128]{2,1,0:T(8,128)}, u32[]{:S(2)}) copy-start(f32[1,128,128]{2,1,0:T(8,128)} %copy-done.48) | copy-start | bytes 196612
  105.9 19.9 %copy-start.47 = (f32[1,128,128]{2,1,0:T(8,128)S(1)}, f32[1,128,128]{2,1,0:T(8,128)}, u32[]{:S(2)}) copy-start(f32[1,128,128]{2,1,0:T(8,128)} %get-tuple-element.88) | copy-start | bytes 196612
  105.9 19.9 %copy-start.51 = (f32[1,128,128]{2,1,0:T(8,128)S(1)}, f32[1,128,128]{2,1,0:T(8,128)}, u32[]{:S(2)}) copy-start(f32[1,128,128]{2,1,0:T(8,128)} %copy-done.50) | copy-start | bytes 196612
  107.4 5.2 %collective-permute-start.10 = (f32[4,128]{1,0:T(4,128)S(1)}, f32[4,128]{1,0:T(4,128)S(1)}, u32[]{:S(2)}, u32[]{:S(2)}) collective-permute-start(f32[4,128]{1,0:T(4,128)S(1)} %fusion.265), channel_id=1, source_target_pairs={{0,4},{1,5},{2,6},{3,7},{4,0},{5,1},{6,2},{7,3},{8,12},{9,13},{10,... | collective-permute-start | bytes 6152 | tf_op jit(solution)/shard_map/ppermute | solution.py:77
  112.8 3.6 %collective-permute-start.11 = (f32[4,128]{1,0:T(4,128)S(1)}, f32[4,128]{1,0:T(4,128)S(1)}, u32[]{:S(2)}, u32[]{:S(2)}) collective-permute-start(f32[4,128]{1,0:T(4,128)S(1)} %fusion.264), channel_id=1, source_target_pairs={{0,8},{1,9},{2,10},{3,11},{4,12},{5,13},{6,14},{7,15},{8,0},{9,1},... | collective-permute-start | bytes 6152 | tf_op jit(solution)/shard_map/ppermute | solution.py:77
  116.7 5.2 %collective-permute-start.12 = (f32[4,128]{1,0:T(4,128)S(1)}, f32[4,128]{1,0:T(4,128)S(1)}, u32[]{:S(2)}, u32[]{:S(2)}) collective-permute-start(f32[4,128]{1,0:T(4,128)S(1)} %fusion.263), channel_id=1, source_target_pairs={{0,16},{1,17},{2,18},{3,19},{4,20},{5,21},{6,22},{7,23},{8,24},{9,... | collective-permute-start | bytes 6152 | tf_op jit(solution)/shard_map/ppermute | solution.py:77
  122.1 3.6 %collective-permute-start.13 = (f32[4,128]{1,0:T(4,128)S(1)}, f32[4,128]{1,0:T(4,128)S(1)}, u32[]{:S(2)}, u32[]{:S(2)}) collective-permute-start(f32[4,128]{1,0:T(4,128)S(1)} %fusion.262), channel_id=1, source_target_pairs={{0,32},{1,33},{2,34},{3,35},{4,36},{5,37},{6,38},{7,39},{8,40},{9,... | collective-permute-start | bytes 6152 | tf_op jit(solution)/shard_map/ppermute | solution.py:77
  126.0 5.2 %collective-permute-start.14 = (f32[4,128]{1,0:T(4,128)S(1)}, f32[4,128]{1,0:T(4,128)S(1)}, u32[]{:S(2)}, u32[]{:S(2)}) collective-permute-start(f32[4,128]{1,0:T(4,128)S(1)} %fusion.261), channel_id=1, source_target_pairs={{0,64},{1,65},{2,66},{3,67},{4,68},{5,69},{6,70},{7,71},{8,72},{9,... | collective-permute-start | bytes 6152 | tf_op jit(solution)/shard_map/ppermute | solution.py:77
  (55 other events, 194.6 us)

commit v2 on v0

--- a/solution.py
+++ b/solution.py
@@ -16,52 +16,51 @@
     return lax.ppermute(x, "tm", pairs)
 
 
-def up_sweep(maps, adds):
-    levels = [(maps, adds)]
-    while maps.shape[0] > 1:
-        pairs = maps.reshape((-1, 2) + maps.shape[1:])
-        if adds is not None:
-            halves = adds.reshape((-1, 2) + adds.shape[1:])
-            adds = (
-                jnp.einsum("tbj,tjk->tbk", halves[:, 0], pairs[:, 1], precision=HIGHEST)
-                + halves[:, 1]
-            )
-        maps = jnp.einsum("tij,tjk->tik", pairs[:, 0], pairs[:, 1], precision=HIGHEST)
-        levels.append((maps, adds))
-    return levels
-
-
-def down_sweep_maps(levels):
-    size = levels[0][0].shape[-1]
+def step_right(x, scale, weights):
+    return jnp.einsum("tbs,sr->tbr", x * scale[:, None, :], weights, precision=HIGHEST)
+
+
+def pair_maps(first_scale, second_scale, weights):
+    scaled = weights[None] * second_scale[:, None, :]
+    product = jnp.einsum("tij,jk->tik", scaled, weights, precision=HIGHEST)
+    return first_scale[:, :, None] * product
+
+
+def down_sweep_maps(maps_levels, even_scale, weights):
+    size = weights.shape[0]
+    eye = jnp.eye(size, dtype=jnp.float32)[None]
     excl = None
-    for maps, _ in reversed(levels[:-1]):
+    for maps in reversed(maps_levels[:-1]):
         left = maps.reshape((-1, 2) + maps.shape[1:])[:, 0]
         if excl is None:
-            excl = jnp.eye(size, dtype=jnp.float32)[None]
-            odd = left
+            excl, odd = eye, left
         else:
             odd = jnp.einsum("tij,tjk->tik", excl, left, precision=HIGHEST)
-        excl = jnp.stack([excl, odd], 1).reshape((-1,) + maps.shape[1:])
-    return excl
-
-
-def down_sweep_adds(levels, adds_levels):
+        excl = interleave(excl, odd)
+    if excl is None:
+        excl = eye
+    return interleave(excl, step_right(excl, even_scale, weights))
+
+
+def down_sweep_adds(maps_levels, adds_levels, step_adds, even_scale, weights):
     excl = None
-    for (maps, _), adds in zip(reversed(levels[:-1]), reversed(adds_levels[:-1])):
+    for maps, adds in zip(reversed(maps_levels[:-1]), reversed(adds_levels[:-1])):
         left_map = maps.reshape((-1, 2) + maps.shape[1:])[:, 0]
         left_add = adds.reshape((-1, 2) + adds.shape[1:])[:, 0]
         if excl is None:
-            excl = jnp.zeros_like(left_add[:1])
-            odd = left_add
+            excl, odd = jnp.zeros_like(left_add[:1]), left_add
         else:
             odd = jnp.einsum("tbj,tjk->tbk", excl, left_map, precision=HIGHEST) + left_add
-        excl = jnp.stack([excl, odd], 1).reshape((-1,) + adds.shape[1:])
-    return excl
-
-
-def up_sweep_adds(levels, adds):
-    out = [adds]
-    for maps, _ in levels[:-1]:
+        excl = interleave(excl, odd)
+    if excl is None:
+        excl = jnp.zeros_like(step_adds[:1])
+    return interleave(excl, step_right(excl, even_scale, weights) + step_adds[0::2])
+
+
+def up_sweep_adds(maps_levels, step_adds, odd_scale, weights):
+    adds = step_right(step_adds[0::2], odd_scale, weights) + step_adds[1::2]
+    out = [step_adds, adds]
+    for maps in maps_levels[:-1]:
         pairs = maps.reshape((-1, 2) + maps.shape[1:])
         halves = adds.reshape((-1, 2) + adds.shape[1:])
         adds = (
@@ -70,6 +69,10 @@
         )
         out.append(adds)
     return out
+
+
+def interleave(even, odd):
+    return jnp.stack([even, odd], 1).reshape((-1,) + even.shape[1:])
 
 
 def exchanged(x, bit):
@@ -91,12 +94,13 @@
 
     following = shifted(decay[:1], -1)
     upcoming = jnp.concatenate([decay[1:], following], 0)
-    step_maps = jnp.stack([decay, upcoming[::-1]])[:, :, :, None] * jnp.stack(
-        [closed_rows, smoother_gain.T]
-    )[:, None]
-
-    tree = [(step_maps, forward_adds)]
-    maps, adds = step_maps, forward_adds
+    backward_scale = upcoming[::-1]
+    maps = jnp.stack([
+        pair_maps(decay[0::2], decay[1::2], closed_rows),
+        pair_maps(backward_scale[0::2], backward_scale[1::2], smoother_gain.T),
+    ])
+    adds = step_right(forward_adds[0::2], decay[1::2], closed_rows) + forward_adds[1::2]
+    tree = [(maps, adds)]
     while maps.shape[1] > 1:
         pairs = maps.reshape((2, -1, 2) + maps.shape[2:])
         halves = adds.reshape((-1, 2) + adds.shape[1:])
@@ -106,8 +110,9 @@
         )
         maps = jnp.einsum("dtij,dtjk->dtik", pairs[:, :, 0], pairs[:, :, 1], precision=HIGHEST)
         tree.append((maps, adds))
-    forward_tree = [(m[0], a) for m, a in tree]
-    backward_tree = [(m[1], None) for m, _ in tree]
+    forward_maps = [m[0] for m, _ in tree]
+    forward_tree = (forward_maps, [a for _, a in tree])
+    backward_maps = [m[1] for m, _ in tree]
 
     rounds = []
     bit = 1
@@ -149,8 +154,8 @@
         back_total = products[2]
         back_before = jnp.where(upper, back_before, products[3])
 
-    excl_maps = down_sweep_maps(late)
-    excl_adds = down_sweep_adds(late, [a for _, a in late])
+    excl_maps = down_sweep_maps(late[0], decay[0::2], closed_rows)
+    excl_adds = down_sweep_adds(late[0], late[1], forward_adds, decay[0::2], closed_rows)
     previous = jnp.einsum("bs,tsr->tbr", entering, excl_maps, precision=HIGHEST) + excl_adds
     filtered = (
         jnp.einsum("tbs,sr->tbr", previous * decay[:, None, :], closed_rows, precision=HIGHEST)
@@ -162,11 +167,11 @@
     backward_adds = filtered - jnp.einsum(
         "tbs,sr->tbr", predicted * upcoming[:, None, :], smoother_gain.T, precision=HIGHEST
     )
-    back_adds = up_sweep_adds(backward_tree, backward_adds[::-1])
+    back_adds = up_sweep_adds(backward_maps, backward_adds[::-1], backward_scale[1::2], smoother_gain.T)
 
     total_add = back_adds[-1][0]
     before_add = jnp.zeros_like(total_add)
-    late_b = (backward_tree, back_adds)
+    late_b = (backward_maps, back_adds)
     for k, bit in enumerate(rounds):
         upper = (index & bit) != 0
         own_map, second_map, own_before = stored[k]
@@ -182,8 +187,10 @@
         total_add = offsets[0] + second_add
         before_add = jnp.where(upper, before_add, offsets[1] + before_add)
     arriving = before_add
-    back_excl_maps = down_sweep_maps(late_b[0])
-    back_excl_adds = down_sweep_adds(late_b[0], late_b[1])
+    back_excl_maps = down_sweep_maps(late_b[0], backward_scale[0::2], smoother_gain.T)
+    back_excl_adds = down_sweep_adds(
+        late_b[0], late_b[1][1:], late_b[1][0], backward_scale[0::2], smoother_gain.T
+    )
     following_state = (
         jnp.einsum("bs,tsr->tbr", arriving, back_excl_maps, precision=HIGHEST) + back_excl_adds
     )[::-1]

time: 123 us -> 111 us (0.902)
  matrix products: 35.3 us -> 29 us
  other arithmetic: 5.96 us -> 2.21 us
  waiting for transfers between devices: 50.6 us -> 48.5 us
  starting transfers between devices: 12.1 us -> 13.9 us
    dot_general x0 -> x8, matrix products: none -> 6.32 us  [the longest x6 4.34 us: step_right(): jnp.einsum('tbs,sr->tbr', x * scale[:, None, :], weights, precision=HIGHEST)]
    dot_general x5 -> x4, matrix products: 5.47 us -> 1.23 us  [up_sweep_adds(): jnp.einsum('tbj,tjk->tbk', halves[:, 0], pairs[:, 1], precision=HIGHEST)]
    dot_general x8 -> x6, matrix products: 5 us -> 2.61 us  [down_sweep_maps(): odd = jnp.einsum('tij,tjk->tik', excl, left, precision=HIGHEST)]
    dot_general x5 -> x4, matrix products: 4.8 us -> 2.46 us  [local(): jnp.einsum('dtij,dtjk->dtik', pairs[:, :, 0], pairs[:, :, 1], precision=H...]
    unnamed x100 -> x130, local copies, waits for them, and re-layouts: 3.21 us -> 5.52 us
    ppermute x14, waiting for transfers between devices: 50.6 us -> 48.5 us  [exchanged(): return lax.ppermute(x, 'tm', [(i, i ^ bit) for i in range(count)])]
    mul x2, other arithmetic: 2.29 us -> 0.21 us  [step_right(): x * scale[:, None, :]]
    dot_general x8 -> x6, matrix products: 4.08 us -> 2.12 us  [down_sweep_adds(): jnp.einsum('tbj,tjk->tbk', excl, left_map, precision=HIGHEST) + left_add]
  transfers between devices with their start and end apart: 15 -> 15, of which waited for: 14 -> 13; matrix products, arithmetic and copies ran while one was open for 13% -> 16% of each run, Pallas kernels for 0% -> 0%
where the time goes in v2:
time: 111 us; the launch traced here: 110 us
  waiting for transfers between devices  48.5 us (44%)
  matrix products  29 us (26%)
  local copies, waits for them, and re-layouts  14.6 us (13%)
  starting transfers between devices  13.9 us (13%)
  other arithmetic  2.21 us (2%)
  between operations  2.17 us (2%)
    ppermute x14, waiting for transfers between devices, exchanged(): return lax.ppermute(x, 'tm', [(i, i ^ bit) for i in range(count)])  48.5 us
    ppermute x1, starting transfers between devices, shifted(): return lax.ppermute(x, 'tm', pairs)  8.09 us
    ppermute x14, starting transfers between devices, exchanged(): return lax.ppermute(x, 'tm', [(i, i ^ bit) for i in range(count)])  5.84 us
    unnamed x130, local copies, waits for them, and re-layouts  5.52 us
    dot_general x18, matrix products, batched(): jnp.einsum('kij,kjl->kil', jnp.stack(lhs), jnp.stack(rhs), precision=HIGH...  4.93 us
    dot_general x6, matrix products, step_right(): jnp.einsum('tbs,sr->tbr', x * scale[:, None, :], weights, precision=HIGHEST)  4.34 us
    dot_general x4, matrix products, dot(): return jnp.dot(a, b, precision=HIGHEST)  3.66 us
    dot_general x6, matrix products, down_sweep_maps(): odd = jnp.einsum('tij,tjk->tik', excl, left, precision=HIGHEST)  2.61 us
  transfers between devices with their start and end apart: 15, of which 13 were waited for; matrix products, arithmetic and copies ran while one was open for 16% of the time, Pallas kernels for 0%

profile of v2, /device:TPU:6, one launch (start us, length us, event | category | flops | bytes accessed | tf_op | source)
XLA Modules:
  0.0 110.5 jit_solution(15419799411418097109)
XLA Ops:
  1.4 8.1 %collective-permute-start = (f32[1,128]{1,0:T(1,128)S(1)}, f32[1,128]{1,0:T(1,128)S(1)}, u32[]{:S(2)}, u32[]{:S(2)}) collective-permute-start(f32[1,128]{1,0:T(1,128)S(1)} %slice.427), channel_id=1, source_target_pairs={{1,0},{2,1},{3,2},{4,3},{5,4},{6,5},{7,6},{8,7},{9,8},{10,9},{11,1... | collective-permute-start | bytes 1544 | tf_op jit(solution)/shard_map/ppermute | solution.py:16
  11.6 1.2 %fusion.223 = f32[128,128]{1,0:T(8,128)S(1)} fusion(f32[64,128]{1,0:T(8,128)} %param.9, f32[64]{0:T(128)} %param.10), kind=kOutput, calls=%fused_computation.366 | convolution fusion | flops 12591104 | bytes 98560 | tf_op jit(solution)/shard_map/dot_general | solution.py:10
  12.8 1.0 convolution_bitcast_fusion.8
  14.6 1.1 %convolution_subtract_fusion = f32[128,128]{1,0:T(8,128)S(1)} fusion(f32[128,128]{1,0:T(8,128)} %param.8, f32[128,128]{1,0:T(8,128)S(1)} %fusion.223), kind=kOutput, calls=%fused_computation.13 | convolution fusion | flops 25182208 | bytes 196608 | tf_op jit(solution)/shard_map/dot_general | solution.py:10
  15.8 0.9 copy.49
  17.1 1.0 convolution_multiply_fusion
  18.7 1.0 broadcast_multiply_fusion
  19.7 1.1 %fusion.13 = f32[2,8,128,128]{3,2,1,0:T(8,128)S(1)} fusion(f32[1,8,2,128,128]{4,3,2,1,0:T(8,128)S(1)} %bitcast.752, f32[1,8,2,128,128]{4,3,2,1,0:T(8,128)S(1)} %bitcast.747), kind=kOutput, calls=%fused_computation.51 | convolution fusion | flops 403177472 | bytes 5242880 | tf_op jit(solution)/shard_map/dtij,dtjk->dtik/dot_general | solution.py:111
  20.9 1.2 %fusion.329 = (f32[1,8,128,128]{3,2,1,0:T(8,128)}, f32[8,128,128]{2,1,0:T(8,128)}, f32[8,128,128]{2,1,0:T(8,128)S(1)}) fusion(f32[2,8,128,128]{3,2,1,0:T(8,128)S(1)} %fusion.13), kind=kLoop, calls=%fused_computation.556 | loop fusion | bytes 2621440 | tf_op jit(solution)/shard_map/slice | solution.py:115
  22.7 0.8 fusion.330
  30.3 5.2 %collective-permute-done.2 = f32[260,128]{1,0:T(8,128)S(1)} collective-permute-done((f32[260,128]{1,0:T(8,128)S(1)}, f32[260,128]{1,0:T(8,128)S(1)}, u32[]{:S(2)}, u32[]{:S(2)}) %collective-permute-start.2) | collective-permute-done | bytes 133152 | tf_op jit(solution)/shard_map/ppermute | solution.py:80
  37.6 5.9 %collective-permute-done.3 = f32[260,128]{1,0:T(8,128)S(1)} collective-permute-done((f32[260,128]{1,0:T(8,128)S(1)}, f32[260,128]{1,0:T(8,128)S(1)}, u32[]{:S(2)}, u32[]{:S(2)}) %collective-permute-start.3) | collective-permute-done | bytes 133152 | tf_op jit(solution)/shard_map/ppermute | solution.py:80
  45.5 4.7 %collective-permute-done.4 = f32[260,128]{1,0:T(8,128)S(1)} collective-permute-done((f32[260,128]{1,0:T(8,128)S(1)}, f32[260,128]{1,0:T(8,128)S(1)}, u32[]{:S(2)}, u32[]{:S(2)}) %collective-permute-start.4) | collective-permute-done | bytes 133152 | tf_op jit(solution)/shard_map/ppermute | solution.py:80
  52.0 1.0 convolution_bitcast_fusion.1
  53.0 5.1 %collective-permute-done.5 = f32[260,128]{1,0:T(8,128)S(1)} collective-permute-done((f32[260,128]{1,0:T(8,128)S(1)}, f32[260,128]{1,0:T(8,128)S(1)}, u32[]{:S(2)}, u32[]{:S(2)}) %collective-permute-start.5) | collective-permute-done | bytes 133152 | tf_op jit(solution)/shard_map/ppermute | solution.py:80
  60.0 4.0 %collective-permute-done.6 = f32[260,128]{1,0:T(8,128)S(1)} collective-permute-done((f32[260,128]{1,0:T(8,128)S(1)}, f32[260,128]{1,0:T(8,128)S(1)}, u32[]{:S(2)}, u32[]{:S(2)}) %collective-permute-start.6) | collective-permute-done | bytes 133152 | tf_op jit(solution)/shard_map/ppermute | solution.py:80
  64.3 1.2 %collective-permute-start.7 = (f32[4,128]{1,0:T(4,128)S(1)}, f32[4,128]{1,0:T(4,128)S(1)}, u32[]{:S(2)}, u32[]{:S(2)}) collective-permute-start(f32[4,128]{1,0:T(4,128)S(1)} %fusion.300), channel_id=1, source_target_pairs={{0,64},{1,65},{2,66},{3,67},{4,68},{5,69},{6,70},{7,71},{8,72},{9,... | collective-permute-start | bytes 6152 | tf_op jit(solution)/shard_map/ppermute | solution.py:80
  65.9 3.5 %collective-permute-done.7 = f32[4,128]{1,0:T(4,128)S(1)} collective-permute-done((f32[4,128]{1,0:T(4,128)S(1)}, f32[4,128]{1,0:T(4,128)S(1)}, u32[]{:S(2)}, u32[]{:S(2)}) %collective-permute-start.7) | collective-permute-done | bytes 2080 | tf_op jit(solution)/shard_map/ppermute | solution.py:80
  69.7 1.2 %fusion.333 = f32[32,128,4]{1,2,0:T(4,128)S(1)} fusion(f32[32,128,128]{2,1,0:T(8,128)S(1)} %bitcast.759, f32[4,128,1]{1,0,2:T(4,128)S(1)} %fusion.10), kind=kOutput, calls=%fused_computation.560 | convolution fusion | flops 25165824 | bytes 2164736 | tf_op jit(solution)/shard_map/bs,tsr->tbr/dot_general | solution.py:159
  71.8 0.9 convolution_add_fusion.2
  78.0 1.0 convolution_bitcast_fusion
  81.2 1.7 %collective-permute-done.9 = f32[4,128]{1,0:T(4,128)S(1)} collective-permute-done((f32[4,128]{1,0:T(4,128)S(1)}, f32[4,128]{1,0:T(4,128)S(1)}, u32[]{:S(2)}, u32[]{:S(2)}) %collective-permute-start.9) | collective-permute-done | bytes 2080 | tf_op jit(solution)/shard_map/ppermute | solution.py:80
  83.3 5.0 %collective-permute-done.10 = f32[4,128]{1,0:T(4,128)S(1)} collective-permute-done((f32[4,128]{1,0:T(4,128)S(1)}, f32[4,128]{1,0:T(4,128)S(1)}, u32[]{:S(2)}, u32[]{:S(2)}) %collective-permute-start.10) | collective-permute-done | bytes 2080 | tf_op jit(solution)/shard_map/ppermute | solution.py:80
  89.4 3.0 %collective-permute-done.11 = f32[4,128]{1,0:T(4,128)S(1)} collective-permute-done((f32[4,128]{1,0:T(4,128)S(1)}, f32[4,128]{1,0:T(4,128)S(1)}, u32[]{:S(2)}, u32[]{:S(2)}) %collective-permute-start.11) | collective-permute-done | bytes 2080 | tf_op jit(solution)/shard_map/ppermute | solution.py:80
  93.1 0.8 slice.558
  94.0 3.8 %collective-permute-done.12 = f32[4,128]{1,0:T(4,128)S(1)} collective-permute-done((f32[4,128]{1,0:T(4,128)S(1)}, f32[4,128]{1,0:T(4,128)S(1)}, u32[]{:S(2)}, u32[]{:S(2)}) %collective-permute-start.12) | collective-permute-done | bytes 2080 | tf_op jit(solution)/shard_map/ppermute | solution.py:80
  98.6 0.9 add_bitcast_fusion
  99.6 2.1 %collective-permute-done.13 = f32[4,128]{1,0:T(4,128)S(1)} collective-permute-done((f32[4,128]{1,0:T(4,128)S(1)}, f32[4,128]{1,0:T(4,128)S(1)}, u32[]{:S(2)}, u32[]{:S(2)}) %collective-permute-start.13) | collective-permute-done | bytes 2080 | tf_op jit(solution)/shard_map/ppermute | solution.py:80
  101.9 1.2 %collective-permute-start.14 = (f32[4,128]{1,0:T(4,128)S(1)}, f32[4,128]{1,0:T(4,128)S(1)}, u32[]{:S(2)}, u32[]{:S(2)}) collective-permute-start(f32[4,128]{1,0:T(4,128)S(1)} %fusion.292), channel_id=1, source_target_pairs={{0,64},{1,65},{2,66},{3,67},{4,68},{5,69},{6,70},{7,71},{8,72},{9,... | collective-permute-start | bytes 6152 | tf_op jit(solution)/shard_map/ppermute | solution.py:80
  103.4 3.6 %collective-permute-done.14 = f32[4,128]{1,0:T(4,128)S(1)} collective-permute-done((f32[4,128]{1,0:T(4,128)S(1)}, f32[4,128]{1,0:T(4,128)S(1)}, u32[]{:S(2)}, u32[]{:S(2)}) %collective-permute-start.14) | collective-permute-done | bytes 2080 | tf_op jit(solution)/shard_map/ppermute | solution.py:80
  107.1 1.2 %fusion.8 = f32[4,128,1]{1,0,2:T(4,128)S(1)} fusion(f32[4,128]{1,0:T(4,128)S(1)} %collective-permute-done.14, f32[4,128,128]{2,1,0:T(8,128)} %copy-done.53, f32[4,128,128]{2,1,0:T(8,128)} %copy-done.9, f32[4,128,128]{2,1,0:T(8,128)} %copy-done.8, f32[4,128,128]{2,1,0:T(8,128)} %copy-done.7, f32[4,128,128]{2,1,0:T(8,128)} %copy-done.6, ...), kind=kOutput, calls=%fused_computation.43 | convolution fusion | flops 924160 | bytes 416256 | tf_op jit(solution)/shard_map/dot_general | solution.py:10
  108.3 1.2 %fusion.334 = f32[32,128,4]{1,2,0:T(4,128)S(1)} fusion(f32[32,128,128]{2,1,0:T(8,128)S(1)} %bitcast.760, f32[4,128,1]{1,0,2:T(4,128)S(1)} %fusion.8), kind=kOutput, calls=%fused_computation.561 | convolution fusion | flops 25165824 | bytes 2164736 | tf_op jit(solution)/shard_map/bs,tsr->tbr/dot_general | solution.py:195
  (305 shorter events, 32.4 us)
Async XLA Ops:
  0.6 12.2 %copy-start = (f32[32,4,64]{2,1,0:T(4,128)S(1)}, f32[32,4,64]{2,1,0:T(4,128)}, u32[]{:S(2)}) copy-start(f32[32,4,64]{2,1,0:T(4,128)} %param.6) | copy-start | bytes 98308
  0.6 18.1 %copy-start.1 = (f32[128,128]{1,0:T(8,128)S(1)}, f32[128,128]{1,0:T(8,128)}, u32[]{:S(2)}) copy-start(f32[128,128]{1,0:T(8,128)} %param.11) | copy-start | bytes 196612
  1.4 17.2 %collective-permute-start = (f32[1,128]{1,0:T(1,128)S(1)}, f32[1,128]{1,0:T(1,128)S(1)}, u32[]{:S(2)}, u32[]{:S(2)}) collective-permute-start(f32[1,128]{1,0:T(1,128)S(1)} %slice.427), channel_id=1, source_target_pairs={{1,0},{2,1},{3,2},{4,3},{5,4},{6,5},{7,6},{8,7},{9,8},{10,9},{11,1... | collective-permute-start | bytes 1544 | tf_op jit(solution)/shard_map/ppermute | solution.py:16
  24.9 1.4 %collective-permute-start.1 = (f32[260,128]{1,0:T(8,128)S(1)}, f32[260,128]{1,0:T(8,128)S(1)}, u32[]{:S(2)}, u32[]{:S(2)}) collective-permute-start(f32[260,128]{1,0:T(8,128)S(1)} %pad_maximum_fusion.13), channel_id=1, source_target_pairs={{0,1},{1,0},{2,3},{3,2},{4,5},{5,4},{6,7},{7,6},{8,9},{9,8},{10,11... | collective-permute-start | bytes 399368 | tf_op jit(solution)/shard_map/ppermute | solution.py:80
  29.5 39.9 %copy-start.5 = (f32[4,128,128]{2,1,0:T(8,128)}, f32[4,128,128]{2,1,0:T(8,128)S(1)}, u32[]{:S(2)}) copy-start(f32[4,128,128]{2,1,0:T(8,128)S(1)} %fusion.27) | copy-start | bytes 786436
  29.8 5.7 %collective-permute-start.2 = (f32[260,128]{1,0:T(8,128)S(1)}, f32[260,128]{1,0:T(8,128)S(1)}, u32[]{:S(2)}, u32[]{:S(2)}) collective-permute-start(f32[260,128]{1,0:T(8,128)S(1)} %pad_maximum_fusion.14), channel_id=1, source_target_pairs={{0,2},{1,3},{2,0},{3,1},{4,6},{5,7},{6,4},{7,5},{8,10},{9,11},{10,... | collective-permute-start | bytes 399368 | tf_op jit(solution)/shard_map/ppermute | solution.py:80
  36.6 32.9 %copy-start.6 = (f32[4,128,128]{2,1,0:T(8,128)}, f32[4,128,128]{2,1,0:T(8,128)S(1)}, u32[]{:S(2)}) copy-start(f32[4,128,128]{2,1,0:T(8,128)S(1)} %fusion.42) | copy-start | bytes 786436
  36.6 8.9 %copy-start.15 = (f32[1,128,128]{2,1,0:T(8,128)}, f32[1,128,128]{2,1,0:T(8,128)S(1)}, u32[]{:S(2)}) copy-start(f32[1,128,128]{2,1,0:T(8,128)S(1)} %get-tuple-element.88) | copy-start | bytes 196612
  36.9 6.6 %collective-permute-start.3 = (f32[260,128]{1,0:T(8,128)S(1)}, f32[260,128]{1,0:T(8,128)S(1)}, u32[]{:S(2)}, u32[]{:S(2)}) collective-permute-start(f32[260,128]{1,0:T(8,128)S(1)} %pad_maximum_fusion.15), channel_id=1, source_target_pairs={{0,4},{1,5},{2,6},{3,7},{4,0},{5,1},{6,2},{7,3},{8,12},{9,13},{10,... | collective-permute-start | bytes 399368 | tf_op jit(solution)/shard_map/ppermute | solution.py:80
  44.6 24.9 %copy-start.7 = (f32[4,128,128]{2,1,0:T(8,128)}, f32[4,128,128]{2,1,0:T(8,128)S(1)}, u32[]{:S(2)}) copy-start(f32[4,128,128]{2,1,0:T(8,128)S(1)} %fusion.57) | copy-start | bytes 786436
  44.9 5.3 %collective-permute-start.4 = (f32[260,128]{1,0:T(8,128)S(1)}, f32[260,128]{1,0:T(8,128)S(1)}, u32[]{:S(2)}, u32[]{:S(2)}) collective-permute-start(f32[260,128]{1,0:T(8,128)S(1)} %pad_maximum_fusion.16), channel_id=1, source_target_pairs={{0,8},{1,9},{2,10},{3,11},{4,12},{5,13},{6,14},{7,15},{8,0},{9,1},... | collective-permute-start | bytes 399368 | tf_op jit(solution)/shard_map/ppermute | solution.py:80
  51.2 18.2 %copy-start.8 = (f32[4,128,128]{2,1,0:T(8,128)}, f32[4,128,128]{2,1,0:T(8,128)S(1)}, u32[]{:S(2)}) copy-start(f32[4,128,128]{2,1,0:T(8,128)S(1)} %fusion.72) | copy-start | bytes 786436
  51.5 6.6 %collective-permute-start.5 = (f32[260,128]{1,0:T(8,128)S(1)}, f32[260,128]{1,0:T(8,128)S(1)}, u32[]{:S(2)}, u32[]{:S(2)}) collective-permute-start(f32[260,128]{1,0:T(8,128)S(1)} %pad_maximum_fusion.17), channel_id=1, source_target_pairs={{0,16},{1,17},{2,18},{3,19},{4,20},{5,21},{6,22},{7,23},{8,24},{9,... | collective-permute-start | bytes 399368 | tf_op jit(solution)/shard_map/ppermute | solution.py:80
  58.6 10.9 %copy-start.9 = (f32[4,128,128]{2,1,0:T(8,128)}, f32[4,128,128]{2,1,0:T(8,128)S(1)}, u32[]{:S(2)}) copy-start(f32[4,128,128]{2,1,0:T(8,128)S(1)} %fusion.87) | copy-start | bytes 786436
  58.9 5.1 %collective-permute-start.6 = (f32[260,128]{1,0:T(8,128)S(1)}, f32[260,128]{1,0:T(8,128)S(1)}, u32[]{:S(2)}, u32[]{:S(2)}) collective-permute-start(f32[260,128]{1,0:T(8,128)S(1)} %pad_maximum_fusion.18), channel_id=1, source_target_pairs={{0,32},{1,33},{2,34},{3,35},{4,36},{5,37},{6,38},{7,39},{8,40},{9,... | collective-permute-start | bytes 399368 | tf_op jit(solution)/shard_map/ppermute | solution.py:80
  60.0 10.9 %copy-start.24 = (f32[32,4,128]{2,0,1:T(8,128)S(1)}, f32[32,4,128]{2,0,1:T(8,128)}, u32[]{:S(2)}) copy-start(f32[32,4,128]{2,0,1:T(8,128)} %copy-done.23) | copy-start | bytes 196612
  60.0 10.9 %copy-start.47 = (f32[32,128]{1,0:T(8,128)S(1)}, f32[32,128]{1,0:T(8,128)}, u32[]{:S(2)}) copy-start(f32[32,128]{1,0:T(8,128)} %param.7) | copy-start | bytes 49156
  64.3 5.2 %collective-permute-start.7 = (f32[4,128]{1,0:T(4,128)S(1)}, f32[4,128]{1,0:T(4,128)S(1)}, u32[]{:S(2)}, u32[]{:S(2)}) collective-permute-start(f32[4,128]{1,0:T(4,128)S(1)} %fusion.300), channel_id=1, source_target_pairs={{0,64},{1,65},{2,66},{3,67},{4,68},{5,69},{6,70},{7,71},{8,72},{9,... | collective-permute-start | bytes 6152 | tf_op jit(solution)/shard_map/ppermute | solution.py:80
  74.0 1.3 %collective-permute-start.8 = (f32[4,128]{1,0:T(4,128)S(1)}, f32[4,128]{1,0:T(4,128)S(1)}, u32[]{:S(2)}, u32[]{:S(2)}) collective-permute-start(f32[4,128]{1,0:T(4,128)S(1)} %convolution_add_fusion.18), channel_id=1, source_target_pairs={{0,1},{1,0},{2,3},{3,2},{4,5},{5,4},{6,7},{7,6},{8,9},{9,8},{10,11... | collective-permute-start | bytes 6152 | tf_op jit(solution)/shard_map/ppermute | solution.py:80
  79.2 3.7 %collective-permute-start.9 = (f32[4,128]{1,0:T(4,128)S(1)}, f32[4,128]{1,0:T(4,128)S(1)}, u32[]{:S(2)}, u32[]{:S(2)}) collective-permute-start(f32[4,128]{1,0:T(4,128)S(1)} %fusion.297), channel_id=1, source_target_pairs={{0,2},{1,3},{2,0},{3,1},{4,6},{5,7},{6,4},{7,5},{8,10},{9,11},{10,... | collective-permute-start | bytes 6152 | tf_op jit(solution)/shard_map/ppermute | solution.py:80
  79.8 12.6 %copy-start.18 = (f32[1,128,128]{2,1,0:T(8,128)S(1)}, f32[1,128,128]{2,1,0:T(8,128)}, u32[]{:S(2)}) copy-start(f32[1,128,128]{2,1,0:T(8,128)} %copy-done.17) | copy-start | bytes 196612
  79.9 12.6 %copy-start.36 = (f32[1,128,128]{2,1,0:T(8,128)S(1)}, f32[1,128,128]{2,1,0:T(8,128)}, u32[]{:S(2)}) copy-start(f32[1,128,128]{2,1,0:T(8,128)} %copy-done.35) | copy-start | bytes 196612
  79.9 17.9 %copy-start.20 = (f32[1,128,128]{2,1,0:T(8,128)S(1)}, f32[1,128,128]{2,1,0:T(8,128)}, u32[]{:S(2)}) copy-start(f32[1,128,128]{2,1,0:T(8,128)} %copy-done.19) | copy-start | bytes 196612
  79.9 17.9 %copy-start.40 = (f32[1,128,128]{2,1,0:T(8,128)S(1)}, f32[1,128,128]{2,1,0:T(8,128)}, u32[]{:S(2)}) copy-start(f32[1,128,128]{2,1,0:T(8,128)} %copy-done.39) | copy-start | bytes 196612
  79.9 21.8 %copy-start.38 = (f32[1,128,128]{2,1,0:T(8,128)S(1)}, f32[1,128,128]{2,1,0:T(8,128)}, u32[]{:S(2)}) copy-start(f32[1,128,128]{2,1,0:T(8,128)} %copy-done.37) | copy-start | bytes 196612
  79.9 21.8 %copy-start.42 = (f32[1,128,128]{2,1,0:T(8,128)S(1)}, f32[1,128,128]{2,1,0:T(8,128)}, u32[]{:S(2)}) copy-start(f32[1,128,128]{2,1,0:T(8,128)} %copy-done.41) | copy-start | bytes 196612
  83.1 10.0 %copy-start.60 = (f32[2,4,128]{2,1,0:T(4,128)}, f32[2,4,128]{2,1,0:T(4,128)S(1)}, u32[]{:S(2)}) copy-start(f32[2,4,128]{2,1,0:T(4,128)S(1)} %fusion.142) | copy-start | bytes 12292
  83.1 5.2 %collective-permute-start.10 = (f32[4,128]{1,0:T(4,128)S(1)}, f32[4,128]{1,0:T(4,128)S(1)}, u32[]{:S(2)}, u32[]{:S(2)}) collective-permute-start(f32[4,128]{1,0:T(4,128)S(1)} %fusion.296), channel_id=1, source_target_pairs={{0,4},{1,5},{2,6},{3,7},{4,0},{5,1},{6,2},{7,3},{8,12},{9,13},{10,... | collective-permute-start | bytes 6152 | tf_op jit(solution)/shard_map/ppermute | solution.py:80
  88.5 3.9 %collective-permute-start.11 = (f32[4,128]{1,0:T(4,128)S(1)}, f32[4,128]{1,0:T(4,128)S(1)}, u32[]{:S(2)}, u32[]{:S(2)}) collective-permute-start(f32[4,128]{1,0:T(4,128)S(1)} %fusion.295), channel_id=1, source_target_pairs={{0,8},{1,9},{2,10},{3,11},{4,12},{5,13},{6,14},{7,15},{8,0},{9,1},... | collective-permute-start | bytes 6152 | tf_op jit(solution)/shard_map/ppermute | solution.py:80
  92.7 5.2 %collective-permute-start.12 = (f32[4,128]{1,0:T(4,128)S(1)}, f32[4,128]{1,0:T(4,128)S(1)}, u32[]{:S(2)}, u32[]{:S(2)}) collective-permute-start(f32[4,128]{1,0:T(4,128)S(1)} %fusion.294), channel_id=1, source_target_pairs={{0,16},{1,17},{2,18},{3,19},{4,20},{5,21},{6,22},{7,23},{8,24},{9,... | collective-permute-start | bytes 6152 | tf_op jit(solution)/shard_map/ppermute | solution.py:80
  98.0 3.6 %collective-permute-start.13 = (f32[4,128]{1,0:T(4,128)S(1)}, f32[4,128]{1,0:T(4,128)S(1)}, u32[]{:S(2)}, u32[]{:S(2)}) collective-permute-start(f32[4,128]{1,0:T(4,128)S(1)} %fusion.293), channel_id=1, source_target_pairs={{0,32},{1,33},{2,34},{3,35},{4,36},{5,37},{6,38},{7,39},{8,40},{9,... | collective-permute-start | bytes 6152 | tf_op jit(solution)/shard_map/ppermute | solution.py:80
  101.9 5.2 %collective-permute-start.14 = (f32[4,128]{1,0:T(4,128)S(1)}, f32[4,128]{1,0:T(4,128)S(1)}, u32[]{:S(2)}, u32[]{:S(2)}) collective-permute-start(f32[4,128]{1,0:T(4,128)S(1)} %fusion.292), channel_id=1, source_target_pairs={{0,64},{1,65},{2,66},{3,67},{4,68},{5,69},{6,70},{7,71},{8,72},{9,... | collective-permute-start | bytes 6152 | tf_op jit(solution)/shard_map/ppermute | solution.py:80
  (47 other events, 190.6 us)

commit v3 on v2

--- a/solution.py
+++ b/solution.py
@@ -75,9 +75,17 @@
     return jnp.stack([even, odd], 1).reshape((-1,) + even.shape[1:])
 
 
+def partner(i, bit):
+    if bit >= 4 and (bit.bit_length() - 1) % 2 == 0:
+        low = bit // 2
+        position = (i // low) % 4
+        return i + (3 - 2 * position) * low
+    return i ^ bit
+
+
 def exchanged(x, bit):
     count = lax.axis_size("tm")
-    return lax.ppermute(x, "tm", [(i, i ^ bit) for i in range(count)])
+    return lax.ppermute(x, "tm", [(i, partner(i, bit)) for i in range(count)])
 
 
 def batched(lhs, rhs):

time: 111 us -> 110 us (level)
  starting transfers between devices: 13.9 us -> 11.1 us
    ppermute x14, starting transfers between devices: 5.84 us -> 2.98 us  [exchanged(): return lax.ppermute(x, 'tm', [(i, partner(i, bit)) for i in range(count)])]
where the time goes in v3:
time: 110 us; the launch traced here: 109 us
  waiting for transfers between devices  49.2 us (45%)
  matrix products  29.1 us (26%)
  local copies, waits for them, and re-layouts  14.9 us (14%)
  starting transfers between devices  11.1 us (10%)
  other arithmetic  2.22 us (2%)
  between operations  2.21 us (2%)
    ppermute x14, waiting for transfers between devices, exchanged(): return lax.ppermute(x, 'tm', [(i, partner(i, bit)) for i in range(count)])  49.2 us
    ppermute x1, starting transfers between devices, shifted(): return lax.ppermute(x, 'tm', pairs)  8.09 us
    unnamed x130, local copies, waits for them, and re-layouts  5.84 us
    dot_general x18, matrix products, batched(): jnp.einsum('kij,kjl->kil', jnp.stack(lhs), jnp.stack(rhs), precision=HIGH...  4.94 us
    dot_general x6, matrix products, step_right(): jnp.einsum('tbs,sr->tbr', x * scale[:, None, :], weights, precision=HIGHEST)  4.35 us
    dot_general x4, matrix products, dot(): return jnp.dot(a, b, precision=HIGHEST)  3.66 us
    ppermute x14, starting transfers between devices, exchanged(): return lax.ppermute(x, 'tm', [(i, partner(i, bit)) for i in range(count)])  2.98 us
    dot_general x6, matrix products, down_sweep_maps(): odd = jnp.einsum('tij,tjk->tik', excl, left, precision=HIGHEST)  2.61 us
  transfers between devices with their start and end apart: 15, of which 13 were waited for; matrix products, arithmetic and copies ran while one was open for 16% of the time, Pallas kernels for 0%

profile of v3, /device:TPU:6, one launch (start us, length us, event | category | flops | bytes accessed | tf_op | source)
XLA Modules:
  0.0 108.7 jit_solution(3384091346100162138)
XLA Ops:
  0.7 0.7 slice.427
  1.4 8.1 %collective-permute-start = (f32[1,128]{1,0:T(1,128)S(1)}, f32[1,128]{1,0:T(1,128)S(1)}, u32[]{:S(2)}, u32[]{:S(2)}) collective-permute-start(f32[1,128]{1,0:T(1,128)S(1)} %slice.427), channel_id=1, source_target_pairs={{1,0},{2,1},{3,2},{4,3},{5,4},{6,5},{7,6},{8,7},{9,8},{10,9},{11,1... | collective-permute-start | bytes 1544 | tf_op jit(solution)/shard_map/ppermute | solution.py:16
  10.9 0.7 slice.426
  11.6 1.2 %fusion.223 = f32[128,128]{1,0:T(8,128)S(1)} fusion(f32[64,128]{1,0:T(8,128)} %param.9, f32[64]{0:T(128)} %param.10), kind=kOutput, calls=%fused_computation.366 | convolution fusion | flops 12591104 | bytes 98560 | tf_op jit(solution)/shard_map/dot_general | solution.py:10
  12.8 1.0 convolution_bitcast_fusion.8
  14.6 1.1 %convolution_subtract_fusion = f32[128,128]{1,0:T(8,128)S(1)} fusion(f32[128,128]{1,0:T(8,128)} %param.8, f32[128,128]{1,0:T(8,128)S(1)} %fusion.223), kind=kOutput, calls=%fused_computation.13 | convolution fusion | flops 25182208 | bytes 196608 | tf_op jit(solution)/shard_map/dot_general | solution.py:10
  15.8 0.9 copy.49
  17.1 1.0 convolution_multiply_fusion
  18.7 1.0 broadcast_multiply_fusion
  19.7 1.1 %fusion.13 = f32[2,8,128,128]{3,2,1,0:T(8,128)S(1)} fusion(f32[1,8,2,128,128]{4,3,2,1,0:T(8,128)S(1)} %bitcast.752, f32[1,8,2,128,128]{4,3,2,1,0:T(8,128)S(1)} %bitcast.747), kind=kOutput, calls=%fused_computation.51 | convolution fusion | flops 403177472 | bytes 5242880 | tf_op jit(solution)/shard_map/dtij,dtjk->dtik/dot_general | solution.py:119
  20.9 1.2 %fusion.329 = (f32[1,8,128,128]{3,2,1,0:T(8,128)}, f32[8,128,128]{2,1,0:T(8,128)}, f32[8,128,128]{2,1,0:T(8,128)S(1)}) fusion(f32[2,8,128,128]{3,2,1,0:T(8,128)S(1)} %fusion.13), kind=kLoop, calls=%fused_computation.556 | loop fusion | bytes 2621440 | tf_op jit(solution)/shard_map/slice | solution.py:123
  22.7 0.8 fusion.330
  30.3 5.2 %collective-permute-done.2 = f32[260,128]{1,0:T(8,128)S(1)} collective-permute-done((f32[260,128]{1,0:T(8,128)S(1)}, f32[260,128]{1,0:T(8,128)S(1)}, u32[]{:S(2)}, u32[]{:S(2)}) %collective-permute-start.2) | collective-permute-done | bytes 133152 | tf_op jit(solution)/shard_map/ppermute | solution.py:88
  37.6 5.6 %collective-permute-done.3 = f32[260,128]{1,0:T(8,128)S(1)} collective-permute-done((f32[260,128]{1,0:T(8,128)S(1)}, f32[260,128]{1,0:T(8,128)S(1)}, u32[]{:S(2)}, u32[]{:S(2)}) %collective-permute-start.3) | collective-permute-done | bytes 133152 | tf_op jit(solution)/shard_map/ppermute | solution.py:88
  45.2 4.7 %collective-permute-done.4 = f32[260,128]{1,0:T(8,128)S(1)} collective-permute-done((f32[260,128]{1,0:T(8,128)S(1)}, f32[260,128]{1,0:T(8,128)S(1)}, u32[]{:S(2)}, u32[]{:S(2)}) %collective-permute-start.4) | collective-permute-done | bytes 133152 | tf_op jit(solution)/shard_map/ppermute | solution.py:88
  51.8 1.0 convolution_bitcast_fusion.1
  52.8 4.7 %collective-permute-done.5 = f32[260,128]{1,0:T(8,128)S(1)} collective-permute-done((f32[260,128]{1,0:T(8,128)S(1)}, f32[260,128]{1,0:T(8,128)S(1)}, u32[]{:S(2)}, u32[]{:S(2)}) %collective-permute-start.5) | collective-permute-done | bytes 133152 | tf_op jit(solution)/shard_map/ppermute | solution.py:88
  59.4 4.0 %collective-permute-done.6 = f32[260,128]{1,0:T(8,128)S(1)} collective-permute-done((f32[260,128]{1,0:T(8,128)S(1)}, f32[260,128]{1,0:T(8,128)S(1)}, u32[]{:S(2)}, u32[]{:S(2)}) %collective-permute-start.6) | collective-permute-done | bytes 133152 | tf_op jit(solution)/shard_map/ppermute | solution.py:88
  64.2 4.4 %collective-permute-done.7 = f32[4,128]{1,0:T(4,128)S(1)} collective-permute-done((f32[4,128]{1,0:T(4,128)S(1)}, f32[4,128]{1,0:T(4,128)S(1)}, u32[]{:S(2)}, u32[]{:S(2)}) %collective-permute-start.7) | collective-permute-done | bytes 2080 | tf_op jit(solution)/shard_map/ppermute | solution.py:88
  68.8 1.2 %fusion.333 = f32[32,128,4]{1,2,0:T(4,128)S(1)} fusion(f32[32,128,128]{2,1,0:T(8,128)S(1)} %bitcast.759, f32[4,128,1]{1,0,2:T(4,128)S(1)} %fusion.10), kind=kOutput, calls=%fused_computation.560 | convolution fusion | flops 25165824 | bytes 2164736 | tf_op jit(solution)/shard_map/bs,tsr->tbr/dot_general | solution.py:167
  70.9 0.9 convolution_add_fusion.2
  77.1 1.0 convolution_bitcast_fusion
  80.3 1.7 %collective-permute-done.9 = f32[4,128]{1,0:T(4,128)S(1)} collective-permute-done((f32[4,128]{1,0:T(4,128)S(1)}, f32[4,128]{1,0:T(4,128)S(1)}, u32[]{:S(2)}, u32[]{:S(2)}) %collective-permute-start.9) | collective-permute-done | bytes 2080 | tf_op jit(solution)/shard_map/ppermute | solution.py:88
  82.4 4.7 %collective-permute-done.10 = f32[4,128]{1,0:T(4,128)S(1)} collective-permute-done((f32[4,128]{1,0:T(4,128)S(1)}, f32[4,128]{1,0:T(4,128)S(1)}, u32[]{:S(2)}, u32[]{:S(2)}) %collective-permute-start.10) | collective-permute-done | bytes 2080 | tf_op jit(solution)/shard_map/ppermute | solution.py:88
  88.2 3.0 %collective-permute-done.11 = f32[4,128]{1,0:T(4,128)S(1)} collective-permute-done((f32[4,128]{1,0:T(4,128)S(1)}, f32[4,128]{1,0:T(4,128)S(1)}, u32[]{:S(2)}, u32[]{:S(2)}) %collective-permute-start.11) | collective-permute-done | bytes 2080 | tf_op jit(solution)/shard_map/ppermute | solution.py:88
  92.0 0.8 slice.558
  92.9 3.4 %collective-permute-done.12 = f32[4,128]{1,0:T(4,128)S(1)} collective-permute-done((f32[4,128]{1,0:T(4,128)S(1)}, f32[4,128]{1,0:T(4,128)S(1)}, u32[]{:S(2)}, u32[]{:S(2)}) %collective-permute-start.12) | collective-permute-done | bytes 2080 | tf_op jit(solution)/shard_map/ppermute | solution.py:88
  96.6 0.9 add_bitcast_fusion
  97.6 2.6 %collective-permute-done.13 = f32[4,128]{1,0:T(4,128)S(1)} collective-permute-done((f32[4,128]{1,0:T(4,128)S(1)}, f32[4,128]{1,0:T(4,128)S(1)}, u32[]{:S(2)}, u32[]{:S(2)}) %collective-permute-start.13) | collective-permute-done | bytes 2080 | tf_op jit(solution)/shard_map/ppermute | solution.py:88
  100.9 4.4 %collective-permute-done.14 = f32[4,128]{1,0:T(4,128)S(1)} collective-permute-done((f32[4,128]{1,0:T(4,128)S(1)}, f32[4,128]{1,0:T(4,128)S(1)}, u32[]{:S(2)}, u32[]{:S(2)}) %collective-permute-start.14) | collective-permute-done | bytes 2080 | tf_op jit(solution)/shard_map/ppermute | solution.py:88
  105.3 1.2 %fusion.8 = f32[4,128,1]{1,0,2:T(4,128)S(1)} fusion(f32[4,128]{1,0:T(4,128)S(1)} %collective-permute-done.14, f32[4,128,128]{2,1,0:T(8,128)} %copy-done.53, f32[4,128,128]{2,1,0:T(8,128)} %copy-done.9, f32[4,128,128]{2,1,0:T(8,128)} %copy-done.8, f32[4,128,128]{2,1,0:T(8,128)} %copy-done.7, f32[4,128,128]{2,1,0:T(8,128)} %copy-done.6, ...), kind=kOutput, calls=%fused_computation.43 | convolution fusion | flops 924160 | bytes 416256 | tf_op jit(solution)/shard_map/dot_general | solution.py:10
  106.5 1.2 %fusion.334 = f32[32,128,4]{1,2,0:T(4,128)S(1)} fusion(f32[32,128,128]{2,1,0:T(8,128)S(1)} %bitcast.760, f32[4,128,1]{1,0,2:T(4,128)S(1)} %fusion.8), kind=kOutput, calls=%fused_computation.561 | convolution fusion | flops 25165824 | bytes 2164736 | tf_op jit(solution)/shard_map/bs,tsr->tbr/dot_general | solution.py:203
  (305 shorter events, 30.8 us)
Async XLA Ops:
  0.6 12.2 %copy-start = (f32[32,4,64]{2,1,0:T(4,128)S(1)}, f32[32,4,64]{2,1,0:T(4,128)}, u32[]{:S(2)}) copy-start(f32[32,4,64]{2,1,0:T(4,128)} %param.6) | copy-start | bytes 98308
  0.6 18.1 %copy-start.1 = (f32[128,128]{1,0:T(8,128)S(1)}, f32[128,128]{1,0:T(8,128)}, u32[]{:S(2)}) copy-start(f32[128,128]{1,0:T(8,128)} %param.11) | copy-start | bytes 196612
  1.4 17.2 %collective-permute-start = (f32[1,128]{1,0:T(1,128)S(1)}, f32[1,128]{1,0:T(1,128)S(1)}, u32[]{:S(2)}, u32[]{:S(2)}) collective-permute-start(f32[1,128]{1,0:T(1,128)S(1)} %slice.427), channel_id=1, source_target_pairs={{1,0},{2,1},{3,2},{4,3},{5,4},{6,5},{7,6},{8,7},{9,8},{10,9},{11,1... | collective-permute-start | bytes 1544 | tf_op jit(solution)/shard_map/ppermute | solution.py:16
  10.9 8.8 %copy-start.50 = (f32[16,128]{1,0:T(8,128)}, f32[16,128]{1,0:T(8,128)S(1)}, u32[]{:S(2)}) copy-start(f32[16,128]{1,0:T(8,128)S(1)} %slice.424) | copy-start | bytes 24580
  24.9 1.4 %collective-permute-start.1 = (f32[260,128]{1,0:T(8,128)S(1)}, f32[260,128]{1,0:T(8,128)S(1)}, u32[]{:S(2)}, u32[]{:S(2)}) collective-permute-start(f32[260,128]{1,0:T(8,128)S(1)} %pad_maximum_fusion.13), channel_id=1, source_target_pairs={{0,1},{1,0},{2,3},{3,2},{4,5},{5,4},{6,7},{7,6},{8,9},{9,8},{10,11... | collective-permute-start | bytes 399368 | tf_op jit(solution)/shard_map/ppermute | solution.py:88
  29.5 39.0 %copy-start.5 = (f32[4,128,128]{2,1,0:T(8,128)}, f32[4,128,128]{2,1,0:T(8,128)S(1)}, u32[]{:S(2)}) copy-start(f32[4,128,128]{2,1,0:T(8,128)S(1)} %fusion.27) | copy-start | bytes 786436
  29.8 5.7 %collective-permute-start.2 = (f32[260,128]{1,0:T(8,128)S(1)}, f32[260,128]{1,0:T(8,128)S(1)}, u32[]{:S(2)}, u32[]{:S(2)}) collective-permute-start(f32[260,128]{1,0:T(8,128)S(1)} %pad_maximum_fusion.14), channel_id=1, source_target_pairs={{0,2},{1,3},{2,0},{3,1},{4,6},{5,7},{6,4},{7,5},{8,10},{9,11},{10,... | collective-permute-start | bytes 399368 | tf_op jit(solution)/shard_map/ppermute | solution.py:88
  36.6 32.0 %copy-start.6 = (f32[4,128,128]{2,1,0:T(8,128)}, f32[4,128,128]{2,1,0:T(8,128)S(1)}, u32[]{:S(2)}) copy-start(f32[4,128,128]{2,1,0:T(8,128)S(1)} %fusion.42) | copy-start | bytes 786436
  36.9 6.3 %collective-permute-start.3 = (f32[260,128]{1,0:T(8,128)S(1)}, f32[260,128]{1,0:T(8,128)S(1)}, u32[]{:S(2)}, u32[]{:S(2)}) collective-permute-start(f32[260,128]{1,0:T(8,128)S(1)} %pad_maximum_fusion.15), channel_id=1, source_target_pairs={{0,6},{1,7},{2,4},{3,5},{4,2},{5,3},{6,0},{7,1},{8,14},{9,15},{10,... | collective-permute-start | bytes 399368 | tf_op jit(solution)/shard_map/ppermute | solution.py:88
  44.3 24.3 %copy-start.7 = (f32[4,128,128]{2,1,0:T(8,128)}, f32[4,128,128]{2,1,0:T(8,128)S(1)}, u32[]{:S(2)}) copy-start(f32[4,128,128]{2,1,0:T(8,128)S(1)} %fusion.57) | copy-start | bytes 786436
  44.6 5.3 %collective-permute-start.4 = (f32[260,128]{1,0:T(8,128)S(1)}, f32[260,128]{1,0:T(8,128)S(1)}, u32[]{:S(2)}, u32[]{:S(2)}) collective-permute-start(f32[260,128]{1,0:T(8,128)S(1)} %pad_maximum_fusion.16), channel_id=1, source_target_pairs={{0,8},{1,9},{2,10},{3,11},{4,12},{5,13},{6,14},{7,15},{8,0},{9,1},... | collective-permute-start | bytes 399368 | tf_op jit(solution)/shard_map/ppermute | solution.py:88
  50.9 17.6 %copy-start.8 = (f32[4,128,128]{2,1,0:T(8,128)}, f32[4,128,128]{2,1,0:T(8,128)S(1)}, u32[]{:S(2)}) copy-start(f32[4,128,128]{2,1,0:T(8,128)S(1)} %fusion.72) | copy-start | bytes 786436
  51.2 6.3 %collective-permute-start.5 = (f32[260,128]{1,0:T(8,128)S(1)}, f32[260,128]{1,0:T(8,128)S(1)}, u32[]{:S(2)}, u32[]{:S(2)}) collective-permute-start(f32[260,128]{1,0:T(8,128)S(1)} %pad_maximum_fusion.17), channel_id=1, source_target_pairs={{0,24},{1,25},{2,26},{3,27},{4,28},{5,29},{6,30},{7,31},{8,16},{9,... | collective-permute-start | bytes 399368 | tf_op jit(solution)/shard_map/ppermute | solution.py:88
  58.0 10.6 %copy-start.9 = (f32[4,128,128]{2,1,0:T(8,128)}, f32[4,128,128]{2,1,0:T(8,128)S(1)}, u32[]{:S(2)}) copy-start(f32[4,128,128]{2,1,0:T(8,128)S(1)} %fusion.87) | copy-start | bytes 786436
  58.3 5.1 %collective-permute-start.6 = (f32[260,128]{1,0:T(8,128)S(1)}, f32[260,128]{1,0:T(8,128)S(1)}, u32[]{:S(2)}, u32[]{:S(2)}) collective-permute-start(f32[260,128]{1,0:T(8,128)S(1)} %pad_maximum_fusion.18), channel_id=1, source_target_pairs={{0,32},{1,33},{2,34},{3,35},{4,36},{5,37},{6,38},{7,39},{8,40},{9,... | collective-permute-start | bytes 399368 | tf_op jit(solution)/shard_map/ppermute | solution.py:88
  59.4 10.6 %copy-start.24 = (f32[32,4,128]{2,0,1:T(8,128)S(1)}, f32[32,4,128]{2,0,1:T(8,128)}, u32[]{:S(2)}) copy-start(f32[32,4,128]{2,0,1:T(8,128)} %copy-done.23) | copy-start | bytes 196612
  59.4 10.6 %copy-start.47 = (f32[32,128]{1,0:T(8,128)S(1)}, f32[32,128]{1,0:T(8,128)}, u32[]{:S(2)}) copy-start(f32[32,128]{1,0:T(8,128)} %param.7) | copy-start | bytes 49156
  63.7 4.9 %collective-permute-start.7 = (f32[4,128]{1,0:T(4,128)S(1)}, f32[4,128]{1,0:T(4,128)S(1)}, u32[]{:S(2)}, u32[]{:S(2)}) collective-permute-start(f32[4,128]{1,0:T(4,128)S(1)} %fusion.300), channel_id=1, source_target_pairs={{0,96},{1,97},{2,98},{3,99},{4,100},{5,101},{6,102},{7,103},{8,104... | collective-permute-start | bytes 6152 | tf_op jit(solution)/shard_map/ppermute | solution.py:88
  73.1 1.3 %collective-permute-start.8 = (f32[4,128]{1,0:T(4,128)S(1)}, f32[4,128]{1,0:T(4,128)S(1)}, u32[]{:S(2)}, u32[]{:S(2)}) collective-permute-start(f32[4,128]{1,0:T(4,128)S(1)} %convolution_add_fusion.18), channel_id=1, source_target_pairs={{0,1},{1,0},{2,3},{3,2},{4,5},{5,4},{6,7},{7,6},{8,9},{9,8},{10,11... | collective-permute-start | bytes 6152 | tf_op jit(solution)/shard_map/ppermute | solution.py:88
  78.3 3.7 %collective-permute-start.9 = (f32[4,128]{1,0:T(4,128)S(1)}, f32[4,128]{1,0:T(4,128)S(1)}, u32[]{:S(2)}, u32[]{:S(2)}) collective-permute-start(f32[4,128]{1,0:T(4,128)S(1)} %fusion.297), channel_id=1, source_target_pairs={{0,2},{1,3},{2,0},{3,1},{4,6},{5,7},{6,4},{7,5},{8,10},{9,11},{10,... | collective-permute-start | bytes 6152 | tf_op jit(solution)/shard_map/ppermute | solution.py:88
  79.0 12.3 %copy-start.18 = (f32[1,128,128]{2,1,0:T(8,128)S(1)}, f32[1,128,128]{2,1,0:T(8,128)}, u32[]{:S(2)}) copy-start(f32[1,128,128]{2,1,0:T(8,128)} %copy-done.17) | copy-start | bytes 196612
  79.0 12.3 %copy-start.36 = (f32[1,128,128]{2,1,0:T(8,128)S(1)}, f32[1,128,128]{2,1,0:T(8,128)}, u32[]{:S(2)}) copy-start(f32[1,128,128]{2,1,0:T(8,128)} %copy-done.35) | copy-start | bytes 196612
  79.0 17.4 %copy-start.20 = (f32[1,128,128]{2,1,0:T(8,128)S(1)}, f32[1,128,128]{2,1,0:T(8,128)}, u32[]{:S(2)}) copy-start(f32[1,128,128]{2,1,0:T(8,128)} %copy-done.19) | copy-start | bytes 196612
  79.0 17.3 %copy-start.40 = (f32[1,128,128]{2,1,0:T(8,128)S(1)}, f32[1,128,128]{2,1,0:T(8,128)}, u32[]{:S(2)}) copy-start(f32[1,128,128]{2,1,0:T(8,128)} %copy-done.39) | copy-start | bytes 196612
  79.0 21.2 %copy-start.38 = (f32[1,128,128]{2,1,0:T(8,128)S(1)}, f32[1,128,128]{2,1,0:T(8,128)}, u32[]{:S(2)}) copy-start(f32[1,128,128]{2,1,0:T(8,128)} %copy-done.37) | copy-start | bytes 196612
  79.0 21.2 %copy-start.42 = (f32[1,128,128]{2,1,0:T(8,128)S(1)}, f32[1,128,128]{2,1,0:T(8,128)}, u32[]{:S(2)}) copy-start(f32[1,128,128]{2,1,0:T(8,128)} %copy-done.41) | copy-start | bytes 196612
  82.2 9.8 %copy-start.60 = (f32[2,4,128]{2,1,0:T(4,128)}, f32[2,4,128]{2,1,0:T(4,128)S(1)}, u32[]{:S(2)}) copy-start(f32[2,4,128]{2,1,0:T(4,128)S(1)} %fusion.142) | copy-start | bytes 12292
  82.2 4.9 %collective-permute-start.10 = (f32[4,128]{1,0:T(4,128)S(1)}, f32[4,128]{1,0:T(4,128)S(1)}, u32[]{:S(2)}, u32[]{:S(2)}) collective-permute-start(f32[4,128]{1,0:T(4,128)S(1)} %fusion.296), channel_id=1, source_target_pairs={{0,6},{1,7},{2,4},{3,5},{4,2},{5,3},{6,0},{7,1},{8,14},{9,15},{10,... | collective-permute-start | bytes 6152 | tf_op jit(solution)/shard_map/ppermute | solution.py:88
  87.4 3.9 %collective-permute-start.11 = (f32[4,128]{1,0:T(4,128)S(1)}, f32[4,128]{1,0:T(4,128)S(1)}, u32[]{:S(2)}, u32[]{:S(2)}) collective-permute-start(f32[4,128]{1,0:T(4,128)S(1)} %fusion.295), channel_id=1, source_target_pairs={{0,8},{1,9},{2,10},{3,11},{4,12},{5,13},{6,14},{7,15},{8,0},{9,1},... | collective-permute-start | bytes 6152 | tf_op jit(solution)/shard_map/ppermute | solution.py:88
  91.5 4.9 %collective-permute-start.12 = (f32[4,128]{1,0:T(4,128)S(1)}, f32[4,128]{1,0:T(4,128)S(1)}, u32[]{:S(2)}, u32[]{:S(2)}) collective-permute-start(f32[4,128]{1,0:T(4,128)S(1)} %fusion.294), channel_id=1, source_target_pairs={{0,24},{1,25},{2,26},{3,27},{4,28},{5,29},{6,30},{7,31},{8,16},{9,... | collective-permute-start | bytes 6152 | tf_op jit(solution)/shard_map/ppermute | solution.py:88
  96.6 3.6 %collective-permute-start.13 = (f32[4,128]{1,0:T(4,128)S(1)}, f32[4,128]{1,0:T(4,128)S(1)}, u32[]{:S(2)}, u32[]{:S(2)}) collective-permute-start(f32[4,128]{1,0:T(4,128)S(1)} %fusion.293), channel_id=1, source_target_pairs={{0,32},{1,33},{2,34},{3,35},{4,36},{5,37},{6,38},{7,39},{8,40},{9,... | collective-permute-start | bytes 6152 | tf_op jit(solution)/shard_map/ppermute | solution.py:88
  100.5 4.9 %collective-permute-start.14 = (f32[4,128]{1,0:T(4,128)S(1)}, f32[4,128]{1,0:T(4,128)S(1)}, u32[]{:S(2)}, u32[]{:S(2)}) collective-permute-start(f32[4,128]{1,0:T(4,128)S(1)} %fusion.292), channel_id=1, source_target_pairs={{0,96},{1,97},{2,98},{3,99},{4,100},{5,101},{6,102},{7,103},{8,104... | collective-permute-start | bytes 6152 | tf_op jit(solution)/shard_map/ppermute | solution.py:88
  (47 other events, 191.8 us)

commit v4 on v3

--- a/solution.py
+++ b/solution.py
@@ -103,11 +103,14 @@
     following = shifted(decay[:1], -1)
     upcoming = jnp.concatenate([decay[1:], following], 0)
     backward_scale = upcoming[::-1]
+    decay_pairs = decay.reshape((-1, 2) + decay.shape[1:])
+    scale_pairs = backward_scale.reshape((-1, 2) + backward_scale.shape[1:])
+    adds_pairs = forward_adds.reshape((-1, 2) + forward_adds.shape[1:])
     maps = jnp.stack([
-        pair_maps(decay[0::2], decay[1::2], closed_rows),
-        pair_maps(backward_scale[0::2], backward_scale[1::2], smoother_gain.T),
+        pair_maps(decay_pairs[:, 0], decay_pairs[:, 1], closed_rows),
+        pair_maps(scale_pairs[:, 0], scale_pairs[:, 1], smoother_gain.T),
     ])
-    adds = step_right(forward_adds[0::2], decay[1::2], closed_rows) + forward_adds[1::2]
+    adds = step_right(adds_pairs[:, 0], decay_pairs[:, 1], closed_rows) + adds_pairs[:, 1]
     tree = [(maps, adds)]
     while maps.shape[1] > 1:
         pairs = maps.reshape((2, -1, 2) + maps.shape[2:])

time: 110 us -> 116 us (1.055)
  other arithmetic: 2.22 us -> 5.16 us
  matrix products: 29.1 us -> 31.7 us
  local copies, waits for them, and re-layouts: 14.9 us -> 16.5 us
    dot_general x18, matrix products: 4.94 us -> 6.64 us  [batched(): jnp.einsum('kij,kjl->kil', jnp.stack(lhs), jnp.stack(rhs), precision=HIGH...]
    unnamed x130 -> x122, local copies, waits for them, and re-layouts: 5.84 us -> 5.31 us
  transfers between devices with their start and end apart: 15 -> 15, of which waited for: 13 -> 13; matrix products, arithmetic and copies ran while one was open for 16% -> 17% of each run, Pallas kernels for 0% -> 0%
where the time goes in v4:
time: 116 us; the launch traced here: 115 us
  waiting for transfers between devices  48.9 us (42%)
  matrix products  31.7 us (27%)
  local copies, waits for them, and re-layouts  16.5 us (14%)
  starting transfers between devices  10.9 us (9%)
  other arithmetic  5.16 us (4%)
  between operations  2.19 us (2%)
    ppermute x14, waiting for transfers between devices, exchanged(): return lax.ppermute(x, 'tm', [(i, partner(i, bit)) for i in range(count)])  48.8 us
    ppermute x1, starting transfers between devices, shifted(): return lax.ppermute(x, 'tm', pairs)  8.09 us
    dot_general x18, matrix products, batched(): jnp.einsum('kij,kjl->kil', jnp.stack(lhs), jnp.stack(rhs), precision=HIGH...  6.64 us
    unnamed x122, local copies, waits for them, and re-layouts  5.31 us
    dot_general x6, matrix products, step_right(): jnp.einsum('tbs,sr->tbr', x * scale[:, None, :], weights, precision=HIGHEST)  4.35 us
    dot_general x4, matrix products, dot(): return jnp.dot(a, b, precision=HIGHEST)  3.67 us
    dot_general x6, matrix products, down_sweep_maps(): odd = jnp.einsum('tij,tjk->tik', excl, left, precision=HIGHEST)  3.56 us
    ppermute x14, starting transfers between devices, exchanged(): return lax.ppermute(x, 'tm', [(i, partner(i, bit)) for i in range(count)])  2.85 us
  transfers between devices with their start and end apart: 15, of which 13 were waited for; matrix products, arithmetic and copies ran while one was open for 17% of the time, Pallas kernels for 0%

profile of v4, /device:TPU:6, one launch (start us, length us, event | category | flops | bytes accessed | tf_op | source)
XLA Modules:
  0.0 115.3 jit_solution(7776340920846024811)
XLA Ops:
  1.4 8.1 %collective-permute-start = (f32[1,128]{1,0:T(1,128)S(1)}, f32[1,128]{1,0:T(1,128)S(1)}, u32[]{:S(2)}, u32[]{:S(2)}) collective-permute-start(f32[1,128]{1,0:T(1,128)S(1)} %slice.435), channel_id=1, source_target_pairs={{1,0},{2,1},{3,2},{4,3},{5,4},{6,5},{7,6},{8,7},{9,8},{10,9},{11,1... | collective-permute-start | bytes 1544 | tf_op jit(solution)/shard_map/ppermute | solution.py:16
  10.2 1.3 %slice.469 = f32[16,128]{1,0:T(8,128)} slice(f32[32,128]{1,0:T(8,128)} %param.7), slice={[0:32:2], [0:128:1]} | slice | bytes 16384 | tf_op jit(solution)/shard_map/slice | solution.py:168
  12.2 1.2 %fusion.219 = f32[128,128]{1,0:T(8,128)S(1)} fusion(f32[64,128]{1,0:T(8,128)} %param.9, f32[64]{0:T(128)} %param.10), kind=kOutput, calls=%fused_computation.365 | convolution fusion | flops 12591104 | bytes 98560 | tf_op jit(solution)/shard_map/dot_general | solution.py:10
  13.4 1.0 fusion.203
  15.9 1.1 convolution_subtract_fusion
  18.4 1.0 convolution_multiply_fusion.1
  20.0 1.0 convolution_multiply_fusion
  21.0 1.1 fusion.13
  22.2 1.3 %fusion.325 = (f32[1,8,128,128]{3,2,1,0:T(8,128)}, f32[8,128,128]{2,1,0:T(8,128)}, f32[8,128,128]{2,1,0:T(8,128)}) fusion(f32[2,8,128,128]{3,2,1,0:T(8,128)S(1)} %fusion.13), kind=kLoop, calls=%fused_computation.555 | loop fusion | bytes 2621440 | tf_op jit(solution)/shard_map/slice | solution.py:126
  28.7 0.9 select_bitcast_fusion.21
  30.9 1.3 %convolution_bitcast_fusion.5 = f32[4,1,128,128]{3,2,0,1:T(8,128)S(1)} fusion(f32[4,128,128]{2,1,0:T(8,128)S(1)} %bitcast.787, f32[4,2,128,128]{3,2,1,0:T(8,128)} %bitcast.793), kind=kOutput, calls=%fused_computation.11 | convolution fusion | flops 100663296 | bytes 786432 | tf_op jit(solution)/shard_map/tij,tjk->tik/dot_general | solution.py:38
  35.8 5.1 %collective-permute-done.2 = f32[260,128]{1,0:T(8,128)S(1)} collective-permute-done((f32[260,128]{1,0:T(8,128)S(1)}, f32[260,128]{1,0:T(8,128)S(1)}, u32[]{:S(2)}, u32[]{:S(2)}) %collective-permute-start.2) | collective-permute-done | bytes 133152 | tf_op jit(solution)/shard_map/ppermute | solution.py:88
  43.0 5.6 %collective-permute-done.3 = f32[260,128]{1,0:T(8,128)S(1)} collective-permute-done((f32[260,128]{1,0:T(8,128)S(1)}, f32[260,128]{1,0:T(8,128)S(1)}, u32[]{:S(2)}, u32[]{:S(2)}) %collective-permute-start.3) | collective-permute-done | bytes 133152 | tf_op jit(solution)/shard_map/ppermute | solution.py:88
  50.6 4.7 %collective-permute-done.4 = f32[260,128]{1,0:T(8,128)S(1)} collective-permute-done((f32[260,128]{1,0:T(8,128)S(1)}, f32[260,128]{1,0:T(8,128)S(1)}, u32[]{:S(2)}, u32[]{:S(2)}) %collective-permute-start.4) | collective-permute-done | bytes 133152 | tf_op jit(solution)/shard_map/ppermute | solution.py:88
  57.2 1.0 convolution_bitcast_fusion.1
  58.2 4.7 %collective-permute-done.5 = f32[260,128]{1,0:T(8,128)S(1)} collective-permute-done((f32[260,128]{1,0:T(8,128)S(1)}, f32[260,128]{1,0:T(8,128)S(1)}, u32[]{:S(2)}, u32[]{:S(2)}) %collective-permute-start.5) | collective-permute-done | bytes 133152 | tf_op jit(solution)/shard_map/ppermute | solution.py:88
  64.8 4.0 %collective-permute-done.6 = f32[260,128]{1,0:T(8,128)S(1)} collective-permute-done((f32[260,128]{1,0:T(8,128)S(1)}, f32[260,128]{1,0:T(8,128)S(1)}, u32[]{:S(2)}, u32[]{:S(2)}) %collective-permute-start.6) | collective-permute-done | bytes 133152 | tf_op jit(solution)/shard_map/ppermute | solution.py:88
  69.6 4.4 %collective-permute-done.7 = f32[4,128]{1,0:T(4,128)S(1)} collective-permute-done((f32[4,128]{1,0:T(4,128)S(1)}, f32[4,128]{1,0:T(4,128)S(1)}, u32[]{:S(2)}, u32[]{:S(2)}) %collective-permute-start.7) | collective-permute-done | bytes 2080 | tf_op jit(solution)/shard_map/ppermute | solution.py:88
  74.2 1.2 %fusion.332 = f32[32,128,4]{1,2,0:T(4,128)S(1)} fusion(f32[32,128,128]{2,1,0:T(8,128)S(1)} %bitcast.775, f32[4,128,1]{1,0,2:T(4,128)S(1)} %fusion.10), kind=kOutput, calls=%fused_computation.562 | convolution fusion | flops 25165824 | bytes 2164736 | tf_op jit(solution)/shard_map/bs,tsr->tbr/dot_general | solution.py:170
  76.3 0.9 convolution_add_fusion.2
  82.0 1.0 convolution_bitcast_fusion
  85.2 1.7 %collective-permute-done.9 = f32[4,128]{1,0:T(4,128)S(1)} collective-permute-done((f32[4,128]{1,0:T(4,128)S(1)}, f32[4,128]{1,0:T(4,128)S(1)}, u32[]{:S(2)}, u32[]{:S(2)}) %collective-permute-start.9) | collective-permute-done | bytes 2080 | tf_op jit(solution)/shard_map/ppermute | solution.py:88
  87.4 4.7 %collective-permute-done.10 = f32[4,128]{1,0:T(4,128)S(1)} collective-permute-done((f32[4,128]{1,0:T(4,128)S(1)}, f32[4,128]{1,0:T(4,128)S(1)}, u32[]{:S(2)}, u32[]{:S(2)}) %collective-permute-start.10) | collective-permute-done | bytes 2080 | tf_op jit(solution)/shard_map/ppermute | solution.py:88
  93.2 3.0 %collective-permute-done.11 = f32[4,128]{1,0:T(4,128)S(1)} collective-permute-done((f32[4,128]{1,0:T(4,128)S(1)}, f32[4,128]{1,0:T(4,128)S(1)}, u32[]{:S(2)}, u32[]{:S(2)}) %collective-permute-start.11) | collective-permute-done | bytes 2080 | tf_op jit(solution)/shard_map/ppermute | solution.py:88
  97.9 3.4 %collective-permute-done.12 = f32[4,128]{1,0:T(4,128)S(1)} collective-permute-done((f32[4,128]{1,0:T(4,128)S(1)}, f32[4,128]{1,0:T(4,128)S(1)}, u32[]{:S(2)}, u32[]{:S(2)}) %collective-permute-start.12) | collective-permute-done | bytes 2080 | tf_op jit(solution)/shard_map/ppermute | solution.py:88
  101.3 1.0 fusion.153
  102.4 0.9 add_bitcast_fusion
  103.4 2.6 %collective-permute-done.13 = f32[4,128]{1,0:T(4,128)S(1)} collective-permute-done((f32[4,128]{1,0:T(4,128)S(1)}, f32[4,128]{1,0:T(4,128)S(1)}, u32[]{:S(2)}, u32[]{:S(2)}) %collective-permute-start.13) | collective-permute-done | bytes 2080 | tf_op jit(solution)/shard_map/ppermute | solution.py:88
  106.0 1.1 fusion.157
  107.5 4.4 %collective-permute-done.14 = f32[4,128]{1,0:T(4,128)S(1)} collective-permute-done((f32[4,128]{1,0:T(4,128)S(1)}, f32[4,128]{1,0:T(4,128)S(1)}, u32[]{:S(2)}, u32[]{:S(2)}) %collective-permute-start.14) | collective-permute-done | bytes 2080 | tf_op jit(solution)/shard_map/ppermute | solution.py:88
  111.9 1.2 %fusion.8 = f32[4,128,1]{1,0,2:T(4,128)S(1)} fusion(f32[4,128]{1,0:T(4,128)S(1)} %collective-permute-done.14, f32[4,128,128]{2,1,0:T(8,128)} %copy-done.47, f32[4,128,128]{2,1,0:T(8,128)} %copy-done.10, f32[4,128,128]{2,1,0:T(8,128)} %copy-done.9, f32[4,128,128]{2,1,0:T(8,128)} %copy-done.8, f32[4,128,128]{2,1,0:T(8,128)} %copy-done.7, ...), kind=kOutput, calls=%fused_computation.43 | convolution fusion | flops 924160 | bytes 416256 | tf_op jit(solution)/shard_map/dot_general | solution.py:10
  113.1 1.2 %fusion.333 = f32[32,128,4]{1,2,0:T(4,128)S(1)} fusion(f32[32,128,128]{2,1,0:T(8,128)S(1)} %bitcast.776, f32[4,128,1]{1,0,2:T(4,128)S(1)} %fusion.8), kind=kOutput, calls=%fused_computation.563 | convolution fusion | flops 25165824 | bytes 2164736 | tf_op jit(solution)/shard_map/bs,tsr->tbr/dot_general | solution.py:206
  (299 shorter events, 35.7 us)
Async XLA Ops:
  0.6 12.7 %copy-start = (f32[32,4,64]{2,1,0:T(4,128)S(1)}, f32[32,4,64]{2,1,0:T(4,128)}, u32[]{:S(2)}) copy-start(f32[32,4,64]{2,1,0:T(4,128)} %param.6) | copy-start | bytes 98308
  0.6 19.4 %copy-start.1 = (f32[128,128]{1,0:T(8,128)S(1)}, f32[128,128]{1,0:T(8,128)}, u32[]{:S(2)}) copy-start(f32[128,128]{1,0:T(8,128)} %param.11) | copy-start | bytes 196612
  1.4 18.5 %collective-permute-start = (f32[1,128]{1,0:T(1,128)S(1)}, f32[1,128]{1,0:T(1,128)S(1)}, u32[]{:S(2)}, u32[]{:S(2)}) collective-permute-start(f32[1,128]{1,0:T(1,128)S(1)} %slice.435), channel_id=1, source_target_pairs={{1,0},{2,1},{3,2},{4,3},{5,4},{6,5},{7,6},{8,7},{9,8},{10,9},{11,1... | collective-permute-start | bytes 1544 | tf_op jit(solution)/shard_map/ppermute | solution.py:16
  27.0 1.7 %collective-permute-start.1 = (f32[260,128]{1,0:T(8,128)}, f32[260,128]{1,0:T(8,128)}, u32[]{:S(2)}, u32[]{:S(2)}) collective-permute-start(f32[260,128]{1,0:T(8,128)} %pad_maximum_fusion.13), channel_id=1, source_target_pairs={{0,1},{1,0},{2,3},{3,2},{4,5},{5,4},{6,7},{7,6},{8,9},{9,8},{10,11... | collective-permute-start | bytes 399368 | tf_op jit(solution)/shard_map/ppermute | solution.py:88
  34.2 39.7 %copy-start.6 = (f32[4,128,128]{2,1,0:T(8,128)}, f32[4,128,128]{2,1,0:T(8,128)S(1)}, u32[]{:S(2)}) copy-start(f32[4,128,128]{2,1,0:T(8,128)S(1)} %fusion.26) | copy-start | bytes 786436
  35.2 5.7 %collective-permute-start.2 = (f32[260,128]{1,0:T(8,128)S(1)}, f32[260,128]{1,0:T(8,128)S(1)}, u32[]{:S(2)}, u32[]{:S(2)}) collective-permute-start(f32[260,128]{1,0:T(8,128)S(1)} %pad_maximum_fusion.14), channel_id=1, source_target_pairs={{0,2},{1,3},{2,0},{3,1},{4,6},{5,7},{6,4},{7,5},{8,10},{9,11},{10,... | collective-permute-start | bytes 399368 | tf_op jit(solution)/shard_map/ppermute | solution.py:88
  42.0 32.0 %copy-start.7 = (f32[4,128,128]{2,1,0:T(8,128)}, f32[4,128,128]{2,1,0:T(8,128)S(1)}, u32[]{:S(2)}) copy-start(f32[4,128,128]{2,1,0:T(8,128)S(1)} %fusion.41) | copy-start | bytes 786436
  42.1 8.6 %copy-start.18 = (f32[1,128,128]{2,1,0:T(8,128)}, f32[1,128,128]{2,1,0:T(8,128)S(1)}, u32[]{:S(2)}) copy-start(f32[1,128,128]{2,1,0:T(8,128)S(1)} %get-tuple-element.88) | copy-start | bytes 196612
  42.3 6.3 %collective-permute-start.3 = (f32[260,128]{1,0:T(8,128)S(1)}, f32[260,128]{1,0:T(8,128)S(1)}, u32[]{:S(2)}, u32[]{:S(2)}) collective-permute-start(f32[260,128]{1,0:T(8,128)S(1)} %pad_maximum_fusion.15), channel_id=1, source_target_pairs={{0,6},{1,7},{2,4},{3,5},{4,2},{5,3},{6,0},{7,1},{8,14},{9,15},{10,... | collective-permute-start | bytes 399368 | tf_op jit(solution)/shard_map/ppermute | solution.py:88
  49.7 24.3 %copy-start.8 = (f32[4,128,128]{2,1,0:T(8,128)}, f32[4,128,128]{2,1,0:T(8,128)S(1)}, u32[]{:S(2)}) copy-start(f32[4,128,128]{2,1,0:T(8,128)S(1)} %fusion.56) | copy-start | bytes 786436
  49.7 8.5 %copy-start.20 = (f32[1,128,128]{2,1,0:T(8,128)}, f32[1,128,128]{2,1,0:T(8,128)S(1)}, u32[]{:S(2)}) copy-start(f32[1,128,128]{2,1,0:T(8,128)S(1)} %get-tuple-element.84) | copy-start | bytes 196612
  50.0 5.3 %collective-permute-start.4 = (f32[260,128]{1,0:T(8,128)S(1)}, f32[260,128]{1,0:T(8,128)S(1)}, u32[]{:S(2)}, u32[]{:S(2)}) collective-permute-start(f32[260,128]{1,0:T(8,128)S(1)} %pad_maximum_fusion.16), channel_id=1, source_target_pairs={{0,8},{1,9},{2,10},{3,11},{4,12},{5,13},{6,14},{7,15},{8,0},{9,1},... | collective-permute-start | bytes 399368 | tf_op jit(solution)/shard_map/ppermute | solution.py:88
  56.3 17.6 %copy-start.9 = (f32[4,128,128]{2,1,0:T(8,128)}, f32[4,128,128]{2,1,0:T(8,128)S(1)}, u32[]{:S(2)}) copy-start(f32[4,128,128]{2,1,0:T(8,128)S(1)} %fusion.71) | copy-start | bytes 786436
  56.6 6.3 %collective-permute-start.5 = (f32[260,128]{1,0:T(8,128)S(1)}, f32[260,128]{1,0:T(8,128)S(1)}, u32[]{:S(2)}, u32[]{:S(2)}) collective-permute-start(f32[260,128]{1,0:T(8,128)S(1)} %pad_maximum_fusion.17), channel_id=1, source_target_pairs={{0,24},{1,25},{2,26},{3,27},{4,28},{5,29},{6,30},{7,31},{8,16},{9,... | collective-permute-start | bytes 399368 | tf_op jit(solution)/shard_map/ppermute | solution.py:88
  63.0 12.4 %copy-start.37 = (f32[1,128,128]{2,1,0:T(8,128)}, f32[1,128,128]{2,1,0:T(8,128)S(1)}, u32[]{:S(2)}) copy-start(f32[1,128,128]{2,1,0:T(8,128)S(1)} %get-tuple-element.55) | copy-start | bytes 196612
  63.4 10.6 %copy-start.10 = (f32[4,128,128]{2,1,0:T(8,128)}, f32[4,128,128]{2,1,0:T(8,128)S(1)}, u32[]{:S(2)}) copy-start(f32[4,128,128]{2,1,0:T(8,128)S(1)} %fusion.86) | copy-start | bytes 786436
  63.5 12.0 %copy-start.36 = (f32[1,128,128]{2,1,0:T(8,128)}, f32[1,128,128]{2,1,0:T(8,128)S(1)}, u32[]{:S(2)}) copy-start(f32[1,128,128]{2,1,0:T(8,128)S(1)} %get-tuple-element.76) | copy-start | bytes 196612
  63.7 5.1 %collective-permute-start.6 = (f32[260,128]{1,0:T(8,128)S(1)}, f32[260,128]{1,0:T(8,128)S(1)}, u32[]{:S(2)}, u32[]{:S(2)}) collective-permute-start(f32[260,128]{1,0:T(8,128)S(1)} %pad_maximum_fusion.18), channel_id=1, source_target_pairs={{0,32},{1,33},{2,34},{3,35},{4,36},{5,37},{6,38},{7,39},{8,40},{9,... | collective-permute-start | bytes 399368 | tf_op jit(solution)/shard_map/ppermute | solution.py:88
  64.8 10.6 %copy-start.14 = (f32[128,32,4]{0,1,2:T(8,128)S(1)}, f32[128,32,4]{0,1,2:T(8,128)}, u32[]{:S(2)}) copy-start(f32[128,32,4]{0,1,2:T(8,128)} %copy-done.13) | copy-start | bytes 196612
  64.8 10.6 %copy-start.43 = (f32[32,128]{1,0:T(8,128)S(1)}, f32[32,128]{1,0:T(8,128)}, u32[]{:S(2)}) copy-start(f32[32,128]{1,0:T(8,128)} %param.7) | copy-start | bytes 49156
  69.1 4.9 %collective-permute-start.7 = (f32[4,128]{1,0:T(4,128)S(1)}, f32[4,128]{1,0:T(4,128)S(1)}, u32[]{:S(2)}, u32[]{:S(2)}) collective-permute-start(f32[4,128]{1,0:T(4,128)S(1)} %fusion.296), channel_id=1, source_target_pairs={{0,96},{1,97},{2,98},{3,99},{4,100},{5,101},{6,102},{7,103},{8,104... | collective-permute-start | bytes 6152 | tf_op jit(solution)/shard_map/ppermute | solution.py:88
  78.6 1.4 %collective-permute-start.8 = (f32[4,128]{1,0:T(4,128)S(1)}, f32[4,128]{1,0:T(4,128)S(1)}, u32[]{:S(2)}, u32[]{:S(2)}) collective-permute-start(f32[4,128]{1,0:T(4,128)S(1)} %convolution_add_fusion.18), channel_id=1, source_target_pairs={{0,1},{1,0},{2,3},{3,2},{4,5},{5,4},{6,7},{7,6},{8,9},{9,8},{10,11... | collective-permute-start | bytes 6152 | tf_op jit(solution)/shard_map/ppermute | solution.py:88
  83.3 3.7 %collective-permute-start.9 = (f32[4,128]{1,0:T(4,128)S(1)}, f32[4,128]{1,0:T(4,128)S(1)}, u32[]{:S(2)}, u32[]{:S(2)}) collective-permute-start(f32[4,128]{1,0:T(4,128)S(1)} %fusion.293), channel_id=1, source_target_pairs={{0,2},{1,3},{2,0},{3,1},{4,6},{5,7},{6,4},{7,5},{8,10},{9,11},{10,... | collective-permute-start | bytes 6152 | tf_op jit(solution)/shard_map/ppermute | solution.py:88
  83.9 12.3 %copy-start.21 = (f32[1,128,128]{2,1,0:T(8,128)S(1)}, f32[1,128,128]{2,1,0:T(8,128)}, u32[]{:S(2)}) copy-start(f32[1,128,128]{2,1,0:T(8,128)} %copy-done.20) | copy-start | bytes 196612
  83.9 12.3 %copy-start.35 = (f32[1,128,128]{2,1,0:T(8,128)S(1)}, f32[1,128,128]{2,1,0:T(8,128)}, u32[]{:S(2)}) copy-start(f32[1,128,128]{2,1,0:T(8,128)} %copy-done.34) | copy-start | bytes 196612
  83.9 17.4 %copy-start.23 = (f32[1,128,128]{2,1,0:T(8,128)S(1)}, f32[1,128,128]{2,1,0:T(8,128)}, u32[]{:S(2)}) copy-start(f32[1,128,128]{2,1,0:T(8,128)} %copy-done.22) | copy-start | bytes 196612
  87.2 9.8 %copy-start.56 = (f32[2,4,128]{2,1,0:T(4,128)}, f32[2,4,128]{2,1,0:T(4,128)S(1)}, u32[]{:S(2)}) copy-start(f32[2,4,128]{2,1,0:T(4,128)S(1)} %fusion.141) | copy-start | bytes 12292
  87.2 4.9 %collective-permute-start.10 = (f32[4,128]{1,0:T(4,128)S(1)}, f32[4,128]{1,0:T(4,128)S(1)}, u32[]{:S(2)}, u32[]{:S(2)}) collective-permute-start(f32[4,128]{1,0:T(4,128)S(1)} %fusion.292), channel_id=1, source_target_pairs={{0,6},{1,7},{2,4},{3,5},{4,2},{5,3},{6,0},{7,1},{8,14},{9,15},{10,... | collective-permute-start | bytes 6152 | tf_op jit(solution)/shard_map/ppermute | solution.py:88
  92.3 3.9 %collective-permute-start.11 = (f32[4,128]{1,0:T(4,128)S(1)}, f32[4,128]{1,0:T(4,128)S(1)}, u32[]{:S(2)}, u32[]{:S(2)}) collective-permute-start(f32[4,128]{1,0:T(4,128)S(1)} %fusion.291), channel_id=1, source_target_pairs={{0,8},{1,9},{2,10},{3,11},{4,12},{5,13},{6,14},{7,15},{8,0},{9,1},... | collective-permute-start | bytes 6152 | tf_op jit(solution)/shard_map/ppermute | solution.py:88
  96.4 4.9 %collective-permute-start.12 = (f32[4,128]{1,0:T(4,128)S(1)}, f32[4,128]{1,0:T(4,128)S(1)}, u32[]{:S(2)}, u32[]{:S(2)}) collective-permute-start(f32[4,128]{1,0:T(4,128)S(1)} %fusion.290), channel_id=1, source_target_pairs={{0,24},{1,25},{2,26},{3,27},{4,28},{5,29},{6,30},{7,31},{8,16},{9,... | collective-permute-start | bytes 6152 | tf_op jit(solution)/shard_map/ppermute | solution.py:88
  102.4 3.6 %collective-permute-start.13 = (f32[4,128]{1,0:T(4,128)S(1)}, f32[4,128]{1,0:T(4,128)S(1)}, u32[]{:S(2)}, u32[]{:S(2)}) collective-permute-start(f32[4,128]{1,0:T(4,128)S(1)} %fusion.289), channel_id=1, source_target_pairs={{0,32},{1,33},{2,34},{3,35},{4,36},{5,37},{6,38},{7,39},{8,40},{9,... | collective-permute-start | bytes 6152 | tf_op jit(solution)/shard_map/ppermute | solution.py:88
  107.1 4.8 %collective-permute-start.14 = (f32[4,128]{1,0:T(4,128)S(1)}, f32[4,128]{1,0:T(4,128)S(1)}, u32[]{:S(2)}, u32[]{:S(2)}) collective-permute-start(f32[4,128]{1,0:T(4,128)S(1)} %fusion.288), channel_id=1, source_target_pairs={{0,96},{1,97},{2,98},{3,99},{4,100},{5,101},{6,102},{7,103},{8,104... | collective-permute-start | bytes 6152 | tf_op jit(solution)/shard_map/ppermute | solution.py:88
  (43 other events, 167.5 us)

commit v5 on v3

--- a/solution.py
+++ b/solution.py
@@ -69,6 +69,28 @@
         )
         out.append(adds)
     return out
+
+
+def down_level(state, maps, adds):
+    left_map = maps.reshape((-1, 2) + maps.shape[1:])[:, 0]
+    left_add = adds.reshape((-1, 2) + adds.shape[1:])[:, 0]
+    if state is None:
+        size = maps.shape[-1]
+        excl_map = jnp.eye(size, dtype=jnp.float32)[None]
+        excl_add = jnp.zeros_like(left_add[:1])
+        odd_map, odd_add = left_map, left_add
+    else:
+        excl_map, excl_add = state
+        odd_map = jnp.einsum("tij,tjk->tik", excl_map, left_map, precision=HIGHEST)
+        odd_add = jnp.einsum("tbj,tjk->tbk", excl_add, left_map, precision=HIGHEST) + left_add
+    return interleave(excl_map, odd_map), interleave(excl_add, odd_add)
+
+
+def down_steps(state, step_adds, even_scale, weights):
+    excl_map, excl_add = state
+    odd_map = step_right(excl_map, even_scale, weights)
+    odd_add = step_right(excl_add, even_scale, weights) + step_adds[0::2]
+    return interleave(excl_map, odd_map), interleave(excl_add, odd_add)
 
 
 def interleave(even, odd):
@@ -131,7 +153,11 @@
     total_map, total_add, before_map, before_add = maps[0, 0], adds[0], eye, jnp.zeros_like(adds[0])
     back_total, back_before = maps[1, 0], eye
     stored = []
-    late = forward_tree
+    sweep = [
+        (forward_tree[0][j], forward_tree[1][j])
+        for j in reversed(range(len(forward_tree[0]) - 1))
+    ]
+    state = None
     for k, bit in enumerate(rounds):
         upper = (index & bit) != 0
         if k == len(rounds) - 1:
@@ -140,9 +166,13 @@
             stored.append((back_total, back_total, back_before))
             break
         message = jnp.concatenate([total_map, total_add, back_total], 0)
+        if 1 <= k <= len(sweep):
+            (state, level), message = lax.optimization_barrier(((state, sweep[k - 1]), message))
+            state = down_level(state, *level)
+        elif k == len(sweep) + 1:
+            state, message = lax.optimization_barrier((state, message))
+            state = down_steps(state, forward_adds, decay[0::2], closed_rows)
         got = exchanged(message, bit)
-        if k == 0:
-            late, got = lax.optimization_barrier((late, got))
         got_map, got_add, got_back = got[:size], got[size:-size], got[-size:]
         first_map = jnp.where(upper, got_map, total_map)
         second_map = jnp.where(upper, total_map, got_map)
@@ -162,8 +192,11 @@
         back_total = products[2]
         back_before = jnp.where(upper, back_before, products[3])
 
-    excl_maps = down_sweep_maps(late[0], decay[0::2], closed_rows)
-    excl_adds = down_sweep_adds(late[0], late[1], forward_adds, decay[0::2], closed_rows)
+    for level in sweep[max(0, len(rounds) - 2):]:
+        state = down_level(state, *level)
+    if len(sweep) + 1 > len(rounds) - 2:
+        state = down_steps(state, forward_adds, decay[0::2], closed_rows)
+    excl_maps, excl_adds = state
     previous = jnp.einsum("bs,tsr->tbr", entering, excl_maps, precision=HIGHEST) + excl_adds
     filtered = (
         jnp.einsum("tbs,sr->tbr", previous * decay[:, None, :], closed_rows, precision=HIGHEST)

time: 110 us -> 106 us (0.964)
  local copies, waits for them, and re-layouts: 14.9 us -> 13.1 us
    dot_general x0 -> x6, matrix products: none -> 2.36 us  [the longest x3 1.3 us: down_level(): odd_map = jnp.einsum('tij,tjk->tik', excl_map, left_map, precision=HIGHEST)]
    unnamed x130, local copies, waits for them, and re-layouts: 5.84 us -> 4.01 us
    dot_general x6 -> x3, matrix products: 2.61 us -> 1.31 us  [down_sweep_maps(): odd = jnp.einsum('tij,tjk->tik', excl, left, precision=HIGHEST)]
where the time goes in v5:
time: 106 us
  waiting for transfers between devices  48.6 us (46%)
  matrix products  29.1 us (27%)
  local copies, waits for them, and re-layouts  13.1 us (12%)
  starting transfers between devices  11.1 us (10%)
  between operations  2.27 us (2%)
  other arithmetic  1.51 us (1%)
    ppermute x14, waiting for transfers between devices, exchanged(): return lax.ppermute(x, 'tm', [(i, partner(i, bit)) for i in range(count)])  48.6 us
    ppermute x1, starting transfers between devices, shifted(): return lax.ppermute(x, 'tm', pairs)  8.09 us
    dot_general x18, matrix products, batched(): jnp.einsum('kij,kjl->kil', jnp.stack(lhs), jnp.stack(rhs), precision=HIGH...  4.95 us
    dot_general x6, matrix products, step_right(): jnp.einsum('tbs,sr->tbr', x * scale[:, None, :], weights, precision=HIGHEST)  4.35 us
    unnamed x130, local copies, waits for them, and re-layouts  4.01 us
    dot_general x4, matrix products, dot(): return jnp.dot(a, b, precision=HIGHEST)  3.67 us
    ppermute x14, starting transfers between devices, exchanged(): return lax.ppermute(x, 'tm', [(i, partner(i, bit)) for i in range(count)])  2.97 us
    dot_general x4, matrix products, local(): jnp.einsum('dtij,dtjk->dtik', pairs[:, :, 0], pairs[:, :, 1], precision=H...  2.46 us
  transfers between devices with their start and end apart: 15, of which 13 were waited for; matrix products, arithmetic and copies ran while one was open for 16% of the time, Pallas kernels for 0%

profile of v5, /device:TPU:6, one launch (start us, length us, event | category | flops | bytes accessed | tf_op | source)
XLA Modules:
  0.0 105.7 jit_solution(10697405862340545961)
XLA Ops:
  1.4 8.1 %collective-permute-start = (f32[1,128]{1,0:T(1,128)S(1)}, f32[1,128]{1,0:T(1,128)S(1)}, u32[]{:S(2)}, u32[]{:S(2)}) collective-permute-start(f32[1,128]{1,0:T(1,128)S(1)} %slice.422), channel_id=1, source_target_pairs={{1,0},{2,1},{3,2},{4,3},{5,4},{6,5},{7,6},{8,7},{9,8},{10,9},{11,1... | collective-permute-start | bytes 1544 | tf_op jit(solution)/shard_map/ppermute | solution.py:16
  10.9 0.7 slice.421
  11.7 1.2 %fusion.224 = f32[128,128]{1,0:T(8,128)S(1)} fusion(f32[64,128]{1,0:T(8,128)} %param.9, f32[64]{0:T(128)} %param.10), kind=kOutput, calls=%fused_computation.366 | convolution fusion | flops 12591104 | bytes 98560 | tf_op jit(solution)/shard_map/dot_general | solution.py:10
  12.9 1.0 convolution_bitcast_fusion.8
  14.0 1.1 %convolution_subtract_fusion = f32[128,128]{1,0:T(8,128)S(1)} fusion(f32[128,128]{1,0:T(8,128)} %param.8, f32[128,128]{1,0:T(8,128)S(1)} %fusion.224), kind=kOutput, calls=%fused_computation.13 | convolution fusion | flops 25182208 | bytes 196608 | tf_op jit(solution)/shard_map/dot_general | solution.py:10
  15.2 0.9 copy.49
  16.5 1.0 convolution_multiply_fusion
  18.1 1.0 broadcast_multiply_fusion
  19.1 1.1 %fusion.13 = f32[2,8,128,128]{3,2,1,0:T(8,128)S(1)} fusion(f32[1,8,2,128,128]{4,3,2,1,0:T(8,128)S(1)} %bitcast.750, f32[1,8,2,128,128]{4,3,2,1,0:T(8,128)S(1)} %bitcast.745), kind=kOutput, calls=%fused_computation.51 | convolution fusion | flops 403177472 | bytes 5242880 | tf_op jit(solution)/shard_map/dtij,dtjk->dtik/dot_general | solution.py:141
  20.3 1.2 %fusion.328 = (f32[1,8,128,128]{3,2,1,0:T(8,128)}, f32[8,128,128]{2,1,0:T(8,128)}, f32[8,128,128]{2,1,0:T(8,128)S(1)}) fusion(f32[2,8,128,128]{3,2,1,0:T(8,128)S(1)} %fusion.13), kind=kLoop, calls=%fused_computation.554 | loop fusion | bytes 2621440 | tf_op jit(solution)/shard_map/slice | solution.py:145
  22.1 0.8 fusion.329
  26.7 5.6 %collective-permute-done.2 = f32[260,128]{1,0:T(8,128)S(1)} collective-permute-done((f32[260,128]{1,0:T(8,128)S(1)}, f32[260,128]{1,0:T(8,128)S(1)}, u32[]{:S(2)}, u32[]{:S(2)}) %collective-permute-start.2) | collective-permute-done | bytes 133152 | tf_op jit(solution)/shard_map/ppermute | solution.py:110
  33.7 5.6 %collective-permute-done.3 = f32[260,128]{1,0:T(8,128)S(1)} collective-permute-done((f32[260,128]{1,0:T(8,128)S(1)}, f32[260,128]{1,0:T(8,128)S(1)}, u32[]{:S(2)}, u32[]{:S(2)}) %collective-permute-start.3) | collective-permute-done | bytes 133152 | tf_op jit(solution)/shard_map/ppermute | solution.py:110
  41.1 4.1 %collective-permute-done.4 = f32[260,128]{1,0:T(8,128)S(1)} collective-permute-done((f32[260,128]{1,0:T(8,128)S(1)}, f32[260,128]{1,0:T(8,128)S(1)}, u32[]{:S(2)}, u32[]{:S(2)}) %collective-permute-start.4) | collective-permute-done | bytes 133152 | tf_op jit(solution)/shard_map/ppermute | solution.py:110
  46.6 0.7 collective-permute-start.5
  48.8 4.3 %collective-permute-done.5 = f32[260,128]{1,0:T(8,128)S(1)} collective-permute-done((f32[260,128]{1,0:T(8,128)S(1)}, f32[260,128]{1,0:T(8,128)S(1)}, u32[]{:S(2)}, u32[]{:S(2)}) %collective-permute-start.5) | collective-permute-done | bytes 133152 | tf_op jit(solution)/shard_map/ppermute | solution.py:110
  54.2 1.0 convolution_bitcast_fusion.1
  56.3 4.0 %collective-permute-done.6 = f32[260,128]{1,0:T(8,128)S(1)} collective-permute-done((f32[260,128]{1,0:T(8,128)S(1)}, f32[260,128]{1,0:T(8,128)S(1)}, u32[]{:S(2)}, u32[]{:S(2)}) %collective-permute-start.6) | collective-permute-done | bytes 133152 | tf_op jit(solution)/shard_map/ppermute | solution.py:110
  61.1 4.4 %collective-permute-done.7 = f32[4,128]{1,0:T(4,128)S(1)} collective-permute-done((f32[4,128]{1,0:T(4,128)S(1)}, f32[4,128]{1,0:T(4,128)S(1)}, u32[]{:S(2)}, u32[]{:S(2)}) %collective-permute-start.7) | collective-permute-done | bytes 2080 | tf_op jit(solution)/shard_map/ppermute | solution.py:110
  65.8 1.2 %fusion.332 = f32[32,128,4]{1,2,0:T(4,128)S(1)} fusion(f32[32,128,128]{2,1,0:T(8,128)S(1)} %bitcast.758, f32[4,128,1]{1,0,2:T(4,128)S(1)} %fusion.10), kind=kOutput, calls=%fused_computation.558 | convolution fusion | flops 25165824 | bytes 2164736 | tf_op jit(solution)/shard_map/bs,tsr->tbr/dot_general | solution.py:200
  67.9 0.9 convolution_add_fusion.2
  74.0 1.0 convolution_bitcast_fusion
  77.3 1.7 %collective-permute-done.9 = f32[4,128]{1,0:T(4,128)S(1)} collective-permute-done((f32[4,128]{1,0:T(4,128)S(1)}, f32[4,128]{1,0:T(4,128)S(1)}, u32[]{:S(2)}, u32[]{:S(2)}) %collective-permute-start.9) | collective-permute-done | bytes 2080 | tf_op jit(solution)/shard_map/ppermute | solution.py:110
  79.4 4.7 %collective-permute-done.10 = f32[4,128]{1,0:T(4,128)S(1)} collective-permute-done((f32[4,128]{1,0:T(4,128)S(1)}, f32[4,128]{1,0:T(4,128)S(1)}, u32[]{:S(2)}, u32[]{:S(2)}) %collective-permute-start.10) | collective-permute-done | bytes 2080 | tf_op jit(solution)/shard_map/ppermute | solution.py:110
  85.2 3.0 %collective-permute-done.11 = f32[4,128]{1,0:T(4,128)S(1)} collective-permute-done((f32[4,128]{1,0:T(4,128)S(1)}, f32[4,128]{1,0:T(4,128)S(1)}, u32[]{:S(2)}, u32[]{:S(2)}) %collective-permute-start.11) | collective-permute-done | bytes 2080 | tf_op jit(solution)/shard_map/ppermute | solution.py:110
  89.0 0.8 slice.553
  89.9 3.4 %collective-permute-done.12 = f32[4,128]{1,0:T(4,128)S(1)} collective-permute-done((f32[4,128]{1,0:T(4,128)S(1)}, f32[4,128]{1,0:T(4,128)S(1)}, u32[]{:S(2)}, u32[]{:S(2)}) %collective-permute-start.12) | collective-permute-done | bytes 2080 | tf_op jit(solution)/shard_map/ppermute | solution.py:110
  93.6 0.9 add_bitcast_fusion
  94.6 2.6 %collective-permute-done.13 = f32[4,128]{1,0:T(4,128)S(1)} collective-permute-done((f32[4,128]{1,0:T(4,128)S(1)}, f32[4,128]{1,0:T(4,128)S(1)}, u32[]{:S(2)}, u32[]{:S(2)}) %collective-permute-start.13) | collective-permute-done | bytes 2080 | tf_op jit(solution)/shard_map/ppermute | solution.py:110
  97.8 4.4 %collective-permute-done.14 = f32[4,128]{1,0:T(4,128)S(1)} collective-permute-done((f32[4,128]{1,0:T(4,128)S(1)}, f32[4,128]{1,0:T(4,128)S(1)}, u32[]{:S(2)}, u32[]{:S(2)}) %collective-permute-start.14) | collective-permute-done | bytes 2080 | tf_op jit(solution)/shard_map/ppermute | solution.py:110
  102.3 1.2 %fusion.8 = f32[4,128,1]{1,0,2:T(4,128)S(1)} fusion(f32[4,128]{1,0:T(4,128)S(1)} %collective-permute-done.14, f32[4,128,128]{2,1,0:T(8,128)} %copy-done.53, f32[4,128,128]{2,1,0:T(8,128)} %copy-done.9, f32[4,128,128]{2,1,0:T(8,128)} %copy-done.8, f32[4,128,128]{2,1,0:T(8,128)} %copy-done.7, f32[4,128,128]{2,1,0:T(8,128)} %copy-done.6, ...), kind=kOutput, calls=%fused_computation.43 | convolution fusion | flops 924160 | bytes 416256 | tf_op jit(solution)/shard_map/dot_general | solution.py:10
  103.5 1.2 %fusion.333 = f32[32,128,4]{1,2,0:T(4,128)S(1)} fusion(f32[32,128,128]{2,1,0:T(8,128)S(1)} %bitcast.759, f32[4,128,1]{1,0,2:T(4,128)S(1)} %fusion.8), kind=kOutput, calls=%fused_computation.559 | convolution fusion | flops 25165824 | bytes 2164736 | tf_op jit(solution)/shard_map/bs,tsr->tbr/dot_general | solution.py:236
  (304 shorter events, 28.3 us)
Async XLA Ops:
  0.6 12.2 %copy-start = (f32[32,4,64]{2,1,0:T(4,128)S(1)}, f32[32,4,64]{2,1,0:T(4,128)}, u32[]{:S(2)}) copy-start(f32[32,4,64]{2,1,0:T(4,128)} %param.6) | copy-start | bytes 98308
  0.6 17.5 %copy-start.1 = (f32[128,128]{1,0:T(8,128)S(1)}, f32[128,128]{1,0:T(8,128)}, u32[]{:S(2)}) copy-start(f32[128,128]{1,0:T(8,128)} %param.11) | copy-start | bytes 196612
  1.4 16.6 %collective-permute-start = (f32[1,128]{1,0:T(1,128)S(1)}, f32[1,128]{1,0:T(1,128)S(1)}, u32[]{:S(2)}, u32[]{:S(2)}) collective-permute-start(f32[1,128]{1,0:T(1,128)S(1)} %slice.422), channel_id=1, source_target_pairs={{1,0},{2,1},{3,2},{4,3},{5,4},{6,5},{7,6},{8,7},{9,8},{10,9},{11,1... | collective-permute-start | bytes 1544 | tf_op jit(solution)/shard_map/ppermute | solution.py:16
  14.0 12.3 %copy-start.21 = (f32[1,128,128]{2,1,0:T(8,128)}, f32[1,128,128]{2,1,0:T(8,128)S(1)}, u32[]{:S(2)}) copy-start(f32[1,128,128]{2,1,0:T(8,128)S(1)} %fusion.213) | copy-start | bytes 196612
  24.3 1.4 %collective-permute-start.1 = (f32[260,128]{1,0:T(8,128)S(1)}, f32[260,128]{1,0:T(8,128)S(1)}, u32[]{:S(2)}, u32[]{:S(2)}) collective-permute-start(f32[260,128]{1,0:T(8,128)S(1)} %pad_maximum_fusion.13), channel_id=1, source_target_pairs={{0,1},{1,0},{2,3},{3,2},{4,5},{5,4},{6,7},{7,6},{8,9},{9,8},{10,11... | collective-permute-start | bytes 399368 | tf_op jit(solution)/shard_map/ppermute | solution.py:110
  26.2 39.3 %copy-start.5 = (f32[4,128,128]{2,1,0:T(8,128)}, f32[4,128,128]{2,1,0:T(8,128)S(1)}, u32[]{:S(2)}) copy-start(f32[4,128,128]{2,1,0:T(8,128)S(1)} %fusion.29) | copy-start | bytes 786436
  26.6 5.7 %collective-permute-start.2 = (f32[260,128]{1,0:T(8,128)S(1)}, f32[260,128]{1,0:T(8,128)S(1)}, u32[]{:S(2)}, u32[]{:S(2)}) collective-permute-start(f32[260,128]{1,0:T(8,128)S(1)} %pad_maximum_fusion.14), channel_id=1, source_target_pairs={{0,2},{1,3},{2,0},{3,1},{4,6},{5,7},{6,4},{7,5},{8,10},{9,11},{10,... | collective-permute-start | bytes 399368 | tf_op jit(solution)/shard_map/ppermute | solution.py:110
  32.7 32.8 %copy-start.6 = (f32[4,128,128]{2,1,0:T(8,128)}, f32[4,128,128]{2,1,0:T(8,128)S(1)}, u32[]{:S(2)}) copy-start(f32[4,128,128]{2,1,0:T(8,128)S(1)} %fusion.44) | copy-start | bytes 786436
  33.0 6.3 %collective-permute-start.3 = (f32[260,128]{1,0:T(8,128)S(1)}, f32[260,128]{1,0:T(8,128)S(1)}, u32[]{:S(2)}, u32[]{:S(2)}) collective-permute-start(f32[260,128]{1,0:T(8,128)S(1)} %pad_maximum_fusion.15), channel_id=1, source_target_pairs={{0,6},{1,7},{2,4},{3,5},{4,2},{5,3},{6,0},{7,1},{8,14},{9,15},{10,... | collective-permute-start | bytes 399368 | tf_op jit(solution)/shard_map/ppermute | solution.py:110
  39.8 25.7 %copy-start.7 = (f32[4,128,128]{2,1,0:T(8,128)}, f32[4,128,128]{2,1,0:T(8,128)S(1)}, u32[]{:S(2)}) copy-start(f32[4,128,128]{2,1,0:T(8,128)S(1)} %fusion.59) | copy-start | bytes 786436
  40.1 5.1 %collective-permute-start.4 = (f32[260,128]{1,0:T(8,128)S(1)}, f32[260,128]{1,0:T(8,128)S(1)}, u32[]{:S(2)}, u32[]{:S(2)}) collective-permute-start(f32[260,128]{1,0:T(8,128)S(1)} %pad_maximum_fusion.16), channel_id=1, source_target_pairs={{0,8},{1,9},{2,10},{3,11},{4,12},{5,13},{6,14},{7,15},{8,0},{9,1},... | collective-permute-start | bytes 399368 | tf_op jit(solution)/shard_map/ppermute | solution.py:110
  46.3 19.2 %copy-start.8 = (f32[4,128,128]{2,1,0:T(8,128)}, f32[4,128,128]{2,1,0:T(8,128)S(1)}, u32[]{:S(2)}) copy-start(f32[4,128,128]{2,1,0:T(8,128)S(1)} %fusion.74) | copy-start | bytes 786436
  46.6 6.5 %collective-permute-start.5 = (f32[260,128]{1,0:T(8,128)S(1)}, f32[260,128]{1,0:T(8,128)S(1)}, u32[]{:S(2)}, u32[]{:S(2)}) collective-permute-start(f32[260,128]{1,0:T(8,128)S(1)} %pad_maximum_fusion.17), channel_id=1, source_target_pairs={{0,24},{1,25},{2,26},{3,27},{4,28},{5,29},{6,30},{7,31},{8,16},{9,... | collective-permute-start | bytes 399368 | tf_op jit(solution)/shard_map/ppermute | solution.py:110
  53.6 11.9 %copy-start.9 = (f32[4,128,128]{2,1,0:T(8,128)}, f32[4,128,128]{2,1,0:T(8,128)S(1)}, u32[]{:S(2)}) copy-start(f32[4,128,128]{2,1,0:T(8,128)S(1)} %fusion.89) | copy-start | bytes 786436
  55.3 5.1 %collective-permute-start.6 = (f32[260,128]{1,0:T(8,128)S(1)}, f32[260,128]{1,0:T(8,128)S(1)}, u32[]{:S(2)}, u32[]{:S(2)}) collective-permute-start(f32[260,128]{1,0:T(8,128)S(1)} %pad_maximum_fusion.18), channel_id=1, source_target_pairs={{0,32},{1,33},{2,34},{3,35},{4,36},{5,37},{6,38},{7,39},{8,40},{9,... | collective-permute-start | bytes 399368 | tf_op jit(solution)/shard_map/ppermute | solution.py:110
  56.3 10.6 %copy-start.24 = (f32[32,4,128]{2,0,1:T(8,128)S(1)}, f32[32,4,128]{2,0,1:T(8,128)}, u32[]{:S(2)}) copy-start(f32[32,4,128]{2,0,1:T(8,128)} %copy-done.23) | copy-start | bytes 196612
  56.3 10.6 %copy-start.47 = (f32[32,128]{1,0:T(8,128)S(1)}, f32[32,128]{1,0:T(8,128)}, u32[]{:S(2)}) copy-start(f32[32,128]{1,0:T(8,128)} %param.7) | copy-start | bytes 49156
  60.6 4.9 %collective-permute-start.7 = (f32[4,128]{1,0:T(4,128)S(1)}, f32[4,128]{1,0:T(4,128)S(1)}, u32[]{:S(2)}, u32[]{:S(2)}) collective-permute-start(f32[4,128]{1,0:T(4,128)S(1)} %fusion.301), channel_id=1, source_target_pairs={{0,96},{1,97},{2,98},{3,99},{4,100},{5,101},{6,102},{7,103},{8,104... | collective-permute-start | bytes 6152 | tf_op jit(solution)/shard_map/ppermute | solution.py:110
  70.1 1.3 %collective-permute-start.8 = (f32[4,128]{1,0:T(4,128)S(1)}, f32[4,128]{1,0:T(4,128)S(1)}, u32[]{:S(2)}, u32[]{:S(2)}) collective-permute-start(f32[4,128]{1,0:T(4,128)S(1)} %convolution_add_fusion.18), channel_id=1, source_target_pairs={{0,1},{1,0},{2,3},{3,2},{4,5},{5,4},{6,7},{7,6},{8,9},{9,8},{10,11... | collective-permute-start | bytes 6152 | tf_op jit(solution)/shard_map/ppermute | solution.py:110
  75.3 3.7 %collective-permute-start.9 = (f32[4,128]{1,0:T(4,128)S(1)}, f32[4,128]{1,0:T(4,128)S(1)}, u32[]{:S(2)}, u32[]{:S(2)}) collective-permute-start(f32[4,128]{1,0:T(4,128)S(1)} %fusion.298), channel_id=1, source_target_pairs={{0,2},{1,3},{2,0},{3,1},{4,6},{5,7},{6,4},{7,5},{8,10},{9,11},{10,... | collective-permute-start | bytes 6152 | tf_op jit(solution)/shard_map/ppermute | solution.py:110
  75.9 12.3 %copy-start.18 = (f32[1,128,128]{2,1,0:T(8,128)S(1)}, f32[1,128,128]{2,1,0:T(8,128)}, u32[]{:S(2)}) copy-start(f32[1,128,128]{2,1,0:T(8,128)} %copy-done.17) | copy-start | bytes 196612
  75.9 12.3 %copy-start.36 = (f32[1,128,128]{2,1,0:T(8,128)S(1)}, f32[1,128,128]{2,1,0:T(8,128)}, u32[]{:S(2)}) copy-start(f32[1,128,128]{2,1,0:T(8,128)} %copy-done.35) | copy-start | bytes 196612
  76.0 17.3 %copy-start.20 = (f32[1,128,128]{2,1,0:T(8,128)S(1)}, f32[1,128,128]{2,1,0:T(8,128)}, u32[]{:S(2)}) copy-start(f32[1,128,128]{2,1,0:T(8,128)} %copy-done.19) | copy-start | bytes 196612
  76.0 17.3 %copy-start.40 = (f32[1,128,128]{2,1,0:T(8,128)S(1)}, f32[1,128,128]{2,1,0:T(8,128)}, u32[]{:S(2)}) copy-start(f32[1,128,128]{2,1,0:T(8,128)} %copy-done.39) | copy-start | bytes 196612
  76.0 21.2 %copy-start.38 = (f32[1,128,128]{2,1,0:T(8,128)S(1)}, f32[1,128,128]{2,1,0:T(8,128)}, u32[]{:S(2)}) copy-start(f32[1,128,128]{2,1,0:T(8,128)} %copy-done.37) | copy-start | bytes 196612
  76.0 21.2 %copy-start.42 = (f32[1,128,128]{2,1,0:T(8,128)S(1)}, f32[1,128,128]{2,1,0:T(8,128)}, u32[]{:S(2)}) copy-start(f32[1,128,128]{2,1,0:T(8,128)} %copy-done.41) | copy-start | bytes 196612
  79.2 9.8 %copy-start.60 = (f32[2,4,128]{2,1,0:T(4,128)}, f32[2,4,128]{2,1,0:T(4,128)S(1)}, u32[]{:S(2)}) copy-start(f32[2,4,128]{2,1,0:T(4,128)S(1)} %fusion.145) | copy-start | bytes 12292
  79.2 4.9 %collective-permute-start.10 = (f32[4,128]{1,0:T(4,128)S(1)}, f32[4,128]{1,0:T(4,128)S(1)}, u32[]{:S(2)}, u32[]{:S(2)}) collective-permute-start(f32[4,128]{1,0:T(4,128)S(1)} %fusion.297), channel_id=1, source_target_pairs={{0,6},{1,7},{2,4},{3,5},{4,2},{5,3},{6,0},{7,1},{8,14},{9,15},{10,... | collective-permute-start | bytes 6152 | tf_op jit(solution)/shard_map/ppermute | solution.py:110
  84.3 3.9 %collective-permute-start.11 = (f32[4,128]{1,0:T(4,128)S(1)}, f32[4,128]{1,0:T(4,128)S(1)}, u32[]{:S(2)}, u32[]{:S(2)}) collective-permute-start(f32[4,128]{1,0:T(4,128)S(1)} %fusion.296), channel_id=1, source_target_pairs={{0,8},{1,9},{2,10},{3,11},{4,12},{5,13},{6,14},{7,15},{8,0},{9,1},... | collective-permute-start | bytes 6152 | tf_op jit(solution)/shard_map/ppermute | solution.py:110
  88.4 4.9 %collective-permute-start.12 = (f32[4,128]{1,0:T(4,128)S(1)}, f32[4,128]{1,0:T(4,128)S(1)}, u32[]{:S(2)}, u32[]{:S(2)}) collective-permute-start(f32[4,128]{1,0:T(4,128)S(1)} %fusion.295), channel_id=1, source_target_pairs={{0,24},{1,25},{2,26},{3,27},{4,28},{5,29},{6,30},{7,31},{8,16},{9,... | collective-permute-start | bytes 6152 | tf_op jit(solution)/shard_map/ppermute | solution.py:110
  93.5 3.6 %collective-permute-start.13 = (f32[4,128]{1,0:T(4,128)S(1)}, f32[4,128]{1,0:T(4,128)S(1)}, u32[]{:S(2)}, u32[]{:S(2)}) collective-permute-start(f32[4,128]{1,0:T(4,128)S(1)} %fusion.294), channel_id=1, source_target_pairs={{0,32},{1,33},{2,34},{3,35},{4,36},{5,37},{6,38},{7,39},{8,40},{9,... | collective-permute-start | bytes 6152 | tf_op jit(solution)/shard_map/ppermute | solution.py:110
  97.4 4.9 %collective-permute-start.14 = (f32[4,128]{1,0:T(4,128)S(1)}, f32[4,128]{1,0:T(4,128)S(1)}, u32[]{:S(2)}, u32[]{:S(2)}) collective-permute-start(f32[4,128]{1,0:T(4,128)S(1)} %fusion.293), channel_id=1, source_target_pairs={{0,96},{1,97},{2,98},{3,99},{4,100},{5,101},{6,102},{7,103},{8,104... | collective-permute-start | bytes 6152 | tf_op jit(solution)/shard_map/ppermute | solution.py:110
  (47 other events, 205.0 us)

commit v6 on v5

--- a/solution.py
+++ b/solution.py
@@ -212,13 +212,22 @@
 
     total_add = back_adds[-1][0]
     before_add = jnp.zeros_like(total_add)
-    late_b = (backward_maps, back_adds)
+    back_sweep = [
+        (backward_maps[j], back_adds[j + 1]) for j in reversed(range(len(backward_maps) - 1))
+    ]
+    back_state = None
     for k, bit in enumerate(rounds):
         upper = (index & bit) != 0
         own_map, second_map, own_before = stored[k]
+        if 1 <= k <= len(back_sweep):
+            (back_state, level), total_add = lax.optimization_barrier(
+                ((back_state, back_sweep[k - 1]), total_add)
+            )
+            back_state = down_level(back_state, *level)
+        elif k == len(back_sweep) + 1:
+            back_state, total_add = lax.optimization_barrier((back_state, total_add))
+            back_state = down_steps(back_state, back_adds[0], backward_scale[0::2], smoother_gain.T)
         got_add = exchanged(total_add, bit)
-        if k == 0:
-            late_b, got_add = lax.optimization_barrier((late_b, got_add))
         if k == len(rounds) - 1:
             before_add = jnp.where(upper, before_add, dot(got_add, own_before) + before_add)
             break
@@ -228,10 +237,12 @@
         total_add = offsets[0] + second_add
         before_add = jnp.where(upper, before_add, offsets[1] + before_add)
     arriving = before_add
-    back_excl_maps = down_sweep_maps(late_b[0], backward_scale[0::2], smoother_gain.T)
-    back_excl_adds = down_sweep_adds(
-        late_b[0], late_b[1][1:], late_b[1][0], backward_scale[0::2], smoother_gain.T
-    )
+    done = min(len(back_sweep), len(rounds) - 1)
+    for level in back_sweep[done:]:
+        back_state = down_level(back_state, *level)
+    if len(back_sweep) + 1 > len(rounds) - 1:
+        back_state = down_steps(back_state, back_adds[0], backward_scale[0::2], smoother_gain.T)
+    back_excl_maps, back_excl_adds = back_state
     following_state = (
         jnp.einsum("bs,tsr->tbr", arriving, back_excl_maps, precision=HIGHEST) + back_excl_adds
     )[::-1]

time: 106 us -> 114 us (1.075)
  local copies, waits for them, and re-layouts: 13.1 us -> 16.9 us
  waiting for transfers between devices: 48.6 us -> 50.8 us
    slice x4, local copies, waits for them, and re-layouts: 0.05 us -> 4 us  [up_sweep_adds(): adds = step_right(step_adds[0::2], odd_scale, weights) + step_adds[1::2]]
    slice x6 -> x0, local copies, waits for them, and re-layouts: 2.81 us -> none  [the longest x2 1.95 us: local(): backward_maps = [m[1] for m, _ in tree]]
    dot_general x6 -> x0, matrix products: 2.36 us -> none  [the longest x3 1.31 us: down_sweep_maps(): odd = jnp.einsum('tij,tjk->tik', excl, left, precision=HIGHEST)]
    ppermute x14, waiting for transfers between devices: 48.6 us -> 50.8 us  [exchanged(): return lax.ppermute(x, 'tm', [(i, partner(i, bit)) for i in range(count)])]
    squeeze x1 -> x3, local copies, waits for them, and re-layouts: 0.67 us -> 2.47 us  [local(): backward_maps = [m[1] for m, _ in tree]]
    dot_general x18, matrix products: 4.95 us -> 6.64 us  [batched(): jnp.einsum('kij,kjl->kil', jnp.stack(lhs), jnp.stack(rhs), precision=HIGH...]
    dot_general x3 -> x6, matrix products: 1.3 us -> 2.61 us  [down_level(): odd_map = jnp.einsum('tij,tjk->tik', excl_map, left_map, precision=HIGHEST)]
    unnamed x130 -> x92, local copies, waits for them, and re-layouts: 4.01 us -> 4.62 us
  transfers between devices with their start and end apart: 15 -> 15, of which waited for: 13 -> 14; matrix products, arithmetic and copies ran while one was open for 16% -> 14% of each run, Pallas kernels for 0% -> 0%
where the time goes in v6:
time: 114 us; the launch traced here: 113 us
  waiting for transfers between devices  50.8 us (45%)
  matrix products  30.1 us (26%)
  local copies, waits for them, and re-layouts  16.9 us (15%)
  starting transfers between devices  11 us (10%)
  other arithmetic  2.23 us (2%)
  between operations  2.06 us (2%)
    ppermute x14, waiting for transfers between devices, exchanged(): return lax.ppermute(x, 'tm', [(i, partner(i, bit)) for i in range(count)])  50.8 us
    ppermute x1, starting transfers between devices, shifted(): return lax.ppermute(x, 'tm', pairs)  8.09 us
    dot_general x18, matrix products, batched(): jnp.einsum('kij,kjl->kil', jnp.stack(lhs), jnp.stack(rhs), precision=HIGH...  6.64 us
    unnamed x92, local copies, waits for them, and re-layouts  4.62 us
    slice x4, local copies, waits for them, and re-layouts, up_sweep_adds(): adds = step_right(step_adds[0::2], odd_scale, weights) + step_adds[1::2]  4 us
    dot_general x6, matrix products, step_right(): jnp.einsum('tbs,sr->tbr', x * scale[:, None, :], weights, precision=HIGHEST)  3.76 us
    dot_general x4, matrix products, dot(): return jnp.dot(a, b, precision=HIGHEST)  3.62 us
    ppermute x14, starting transfers between devices, exchanged(): return lax.ppermute(x, 'tm', [(i, partner(i, bit)) for i in range(count)])  2.92 us
  transfers between devices with their start and end apart: 15, of which 14 were waited for; matrix products, arithmetic and copies ran while one was open for 14% of the time, Pallas kernels for 0%

profile of v6, /device:TPU:6, one launch (start us, length us, event | category | flops | bytes accessed | tf_op | source)
XLA Modules:
  0.0 113.1 jit_solution(7061760487695397077)
XLA Ops:
  1.4 8.1 %collective-permute-start = (f32[1,128]{1,0:T(1,128)S(1)}, f32[1,128]{1,0:T(1,128)S(1)}, u32[]{:S(2)}, u32[]{:S(2)}) collective-permute-start(f32[1,128]{1,0:T(1,128)S(1)} %slice.415), channel_id=1, source_target_pairs={{1,0},{2,1},{3,2},{4,3},{5,4},{6,5},{7,6},{8,7},{9,8},{10,9},{11,1... | collective-permute-start | bytes 1544 | tf_op jit(solution)/shard_map/ppermute | solution.py:16
  11.7 1.2 %fusion.225 = f32[128,128]{1,0:T(8,128)S(1)} fusion(f32[64,128]{1,0:T(8,128)} %param.9, f32[64]{0:T(128)} %param.10), kind=kOutput, calls=%fused_computation.367 | convolution fusion | flops 12591104 | bytes 98560 | tf_op jit(solution)/shard_map/dot_general | solution.py:10
  12.9 1.0 convolution_bitcast_fusion.8
  14.0 1.1 convolution_subtract_fusion
  15.2 0.9 copy.49
  16.5 1.0 convolution_multiply_fusion
  18.1 1.0 broadcast_multiply_fusion
  19.2 1.1 %fusion.14 = f32[2,8,128,128]{3,2,1,0:T(8,128)S(1)} fusion(f32[1,8,2,128,128]{4,3,2,1,0:T(8,128)S(1)} %bitcast.746, f32[1,8,2,128,128]{4,3,2,1,0:T(8,128)S(1)} %bitcast.741), kind=kOutput, calls=%fused_computation.53 | convolution fusion | flops 403177472 | bytes 5242880 | tf_op jit(solution)/shard_map/dtij,dtjk->dtik/dot_general | solution.py:141
  20.3 1.0 slice_bitcast_fusion.129
  27.2 5.6 %collective-permute-done.2 = f32[260,128]{1,0:T(8,128)S(1)} collective-permute-done((f32[260,128]{1,0:T(8,128)S(1)}, f32[260,128]{1,0:T(8,128)S(1)}, u32[]{:S(2)}, u32[]{:S(2)}) %collective-permute-start.2) | collective-permute-done | bytes 133152 | tf_op jit(solution)/shard_map/ppermute | solution.py:110
  34.8 5.6 %collective-permute-done.3 = f32[260,128]{1,0:T(8,128)S(1)} collective-permute-done((f32[260,128]{1,0:T(8,128)S(1)}, f32[260,128]{1,0:T(8,128)S(1)}, u32[]{:S(2)}, u32[]{:S(2)}) %collective-permute-start.3) | collective-permute-done | bytes 133152 | tf_op jit(solution)/shard_map/ppermute | solution.py:110
  42.8 4.1 %collective-permute-done.4 = f32[260,128]{1,0:T(8,128)S(1)} collective-permute-done((f32[260,128]{1,0:T(8,128)S(1)}, f32[260,128]{1,0:T(8,128)S(1)}, u32[]{:S(2)}, u32[]{:S(2)}) %collective-permute-start.4) | collective-permute-done | bytes 133152 | tf_op jit(solution)/shard_map/ppermute | solution.py:110
  50.5 4.3 %collective-permute-done.5 = f32[260,128]{1,0:T(8,128)S(1)} collective-permute-done((f32[260,128]{1,0:T(8,128)S(1)}, f32[260,128]{1,0:T(8,128)S(1)}, u32[]{:S(2)}, u32[]{:S(2)}) %collective-permute-start.5) | collective-permute-done | bytes 133152 | tf_op jit(solution)/shard_map/ppermute | solution.py:110
  55.9 1.0 convolution_bitcast_fusion.1
  58.0 4.0 %collective-permute-done.6 = f32[260,128]{1,0:T(8,128)S(1)} collective-permute-done((f32[260,128]{1,0:T(8,128)S(1)}, f32[260,128]{1,0:T(8,128)S(1)}, u32[]{:S(2)}, u32[]{:S(2)}) %collective-permute-start.6) | collective-permute-done | bytes 133152 | tf_op jit(solution)/shard_map/ppermute | solution.py:110
  62.8 4.4 %collective-permute-done.7 = f32[4,128]{1,0:T(4,128)S(1)} collective-permute-done((f32[4,128]{1,0:T(4,128)S(1)}, f32[4,128]{1,0:T(4,128)S(1)}, u32[]{:S(2)}, u32[]{:S(2)}) %collective-permute-start.7) | collective-permute-done | bytes 2080 | tf_op jit(solution)/shard_map/ppermute | solution.py:110
  67.4 1.2 %fusion.325 = f32[32,128,4]{1,2,0:T(4,128)S(1)} fusion(f32[32,128,128]{2,1,0:T(8,128)S(1)} %bitcast.755, f32[4,128,1]{1,0,2:T(4,128)S(1)} %fusion.11), kind=kOutput, calls=%fused_computation.554 | convolution fusion | flops 25165824 | bytes 2164736 | tf_op jit(solution)/shard_map/bs,tsr->tbr/dot_general | solution.py:200
  70.7 1.4 %slice.508 = f32[16,4,128]{2,0,1:T(8,128)} reverse(f32[16,4,128]{2,0,1:T(8,128)} %slice.507), dimensions={0} | reverse | bytes 65536 | tf_op jit(solution)/shard_map/slice | solution.py:61
  72.1 1.4 %slice.510 = f32[16,4,128]{2,0,1:T(8,128)} reverse(f32[16,4,128]{2,0,1:T(8,128)} %slice.509), dimensions={0} | reverse | bytes 65536 | tf_op jit(solution)/shard_map/slice | solution.py:61
  73.5 1.1 convolution_add_fusion.3
  77.0 1.1 fusion.125
  78.9 0.9 fusion.123
  79.9 3.6 %collective-permute-done.9 = f32[4,128]{1,0:T(4,128)S(1)} collective-permute-done((f32[4,128]{1,0:T(4,128)S(1)}, f32[4,128]{1,0:T(4,128)S(1)}, u32[]{:S(2)}, u32[]{:S(2)}) %collective-permute-start.9) | collective-permute-done | bytes 2080 | tf_op jit(solution)/shard_map/ppermute | solution.py:110
  83.5 1.0 fusion.149
  85.2 4.2 %collective-permute-done.10 = f32[4,128]{1,0:T(4,128)S(1)} collective-permute-done((f32[4,128]{1,0:T(4,128)S(1)}, f32[4,128]{1,0:T(4,128)S(1)}, u32[]{:S(2)}, u32[]{:S(2)}) %collective-permute-start.10) | collective-permute-done | bytes 2080 | tf_op jit(solution)/shard_map/ppermute | solution.py:110
  90.5 2.7 %collective-permute-done.11 = f32[4,128]{1,0:T(4,128)S(1)} collective-permute-done((f32[4,128]{1,0:T(4,128)S(1)}, f32[4,128]{1,0:T(4,128)S(1)}, u32[]{:S(2)}, u32[]{:S(2)}) %collective-permute-start.11) | collective-permute-done | bytes 2080 | tf_op jit(solution)/shard_map/ppermute | solution.py:110
  95.7 4.1 %collective-permute-done.12 = f32[4,128]{1,0:T(4,128)S(1)} collective-permute-done((f32[4,128]{1,0:T(4,128)S(1)}, f32[4,128]{1,0:T(4,128)S(1)}, u32[]{:S(2)}, u32[]{:S(2)}) %collective-permute-start.12) | collective-permute-done | bytes 2080 | tf_op jit(solution)/shard_map/ppermute | solution.py:110
  100.0 1.0 convolution_bitcast_fusion
  102.1 2.6 %collective-permute-done.13 = f32[4,128]{1,0:T(4,128)S(1)} collective-permute-done((f32[4,128]{1,0:T(4,128)S(1)}, f32[4,128]{1,0:T(4,128)S(1)}, u32[]{:S(2)}, u32[]{:S(2)}) %collective-permute-start.13) | collective-permute-done | bytes 2080 | tf_op jit(solution)/shard_map/ppermute | solution.py:110
  105.2 4.5 %collective-permute-done.14 = f32[4,128]{1,0:T(4,128)S(1)} collective-permute-done((f32[4,128]{1,0:T(4,128)S(1)}, f32[4,128]{1,0:T(4,128)S(1)}, u32[]{:S(2)}, u32[]{:S(2)}) %collective-permute-start.14) | collective-permute-done | bytes 2080 | tf_op jit(solution)/shard_map/ppermute | solution.py:110
  109.8 1.1 %fusion.9 = f32[4,128,1]{1,0,2:T(4,128)S(1)} fusion(f32[4,128]{1,0:T(4,128)S(1)} %collective-permute-done.14, f32[4,128,128]{2,1,0:T(8,128)} %copy-done.42, f32[4,128,128]{2,1,0:T(8,128)S(1)} %fusion.92, f32[4,128,128]{2,1,0:T(8,128)} %copy-done.6, f32[4,128,128]{2,1,0:T(8,128)} %copy-done.5, f32[4,128,128]{2,1,0:T(8,128)} %copy-done.4, ...), kind=kOutput, calls=%fused_computation.45 | convolution fusion | flops 924160 | bytes 416256 | tf_op jit(solution)/shard_map/dot_general | solution.py:10
  110.9 1.2 %fusion.326 = f32[32,128,4]{1,2,0:T(4,128)S(1)} fusion(f32[32,128,128]{2,1,0:T(8,128)S(1)} %bitcast.756, f32[4,128,1]{1,0,2:T(4,128)S(1)} %fusion.9), kind=kOutput, calls=%fused_computation.555 | convolution fusion | flops 25165824 | bytes 2164736 | tf_op jit(solution)/shard_map/bs,tsr->tbr/dot_general | solution.py:247
  (263 shorter events, 32.6 us)
Async XLA Ops:
  0.6 12.3 %copy-start = (f32[32,4,64]{2,1,0:T(4,128)S(1)}, f32[32,4,64]{2,1,0:T(4,128)}, u32[]{:S(2)}) copy-start(f32[32,4,64]{2,1,0:T(4,128)} %param.6) | copy-start | bytes 98308
  0.6 17.5 %copy-start.1 = (f32[128,128]{1,0:T(8,128)S(1)}, f32[128,128]{1,0:T(8,128)}, u32[]{:S(2)}) copy-start(f32[128,128]{1,0:T(8,128)} %param.11) | copy-start | bytes 196612
  1.4 16.7 %collective-permute-start = (f32[1,128]{1,0:T(1,128)S(1)}, f32[1,128]{1,0:T(1,128)S(1)}, u32[]{:S(2)}, u32[]{:S(2)}) collective-permute-start(f32[1,128]{1,0:T(1,128)S(1)} %slice.415), channel_id=1, source_target_pairs={{1,0},{2,1},{3,2},{4,3},{5,4},{6,5},{7,6},{8,7},{9,8},{10,9},{11,1... | collective-permute-start | bytes 1544 | tf_op jit(solution)/shard_map/ppermute | solution.py:16
  9.5 17.7 %copy-start.17 = (f32[1,1,128,128]{3,2,1,0:T(8,128)}, f32[1,1,128,128]{3,2,1,0:T(8,128)S(1)}, u32[]{:S(2)}) copy-start(f32[1,1,128,128]{3,2,1,0:T(8,128)S(1)} %fusion.213) | copy-start | bytes 196612
  11.0 8.2 %copy-start.39 = (f32[16,128]{1,0:T(8,128)}, f32[16,128]{1,0:T(8,128)S(1)}, u32[]{:S(2)}) copy-start(f32[16,128]{1,0:T(8,128)S(1)} %slice.412) | copy-start | bytes 24580
  14.0 12.8 %copy-start.12 = (f32[1,128,128]{2,1,0:T(8,128)}, f32[1,128,128]{2,1,0:T(8,128)S(1)}, u32[]{:S(2)}) copy-start(f32[1,128,128]{2,1,0:T(8,128)S(1)} %fusion.214) | copy-start | bytes 196612
  24.2 1.4 %collective-permute-start.1 = (f32[260,128]{1,0:T(8,128)S(1)}, f32[260,128]{1,0:T(8,128)S(1)}, u32[]{:S(2)}, u32[]{:S(2)}) collective-permute-start(f32[260,128]{1,0:T(8,128)S(1)} %pad_maximum_fusion.13), channel_id=1, source_target_pairs={{0,1},{1,0},{2,3},{3,2},{4,5},{5,4},{6,7},{7,6},{8,9},{9,8},{10,11... | collective-permute-start | bytes 399368 | tf_op jit(solution)/shard_map/ppermute | solution.py:110
  26.7 40.5 %copy-start.3 = (f32[4,128,128]{2,1,0:T(8,128)}, f32[4,128,128]{2,1,0:T(8,128)S(1)}, u32[]{:S(2)}) copy-start(f32[4,128,128]{2,1,0:T(8,128)S(1)} %fusion.32) | copy-start | bytes 786436
  27.0 5.7 %collective-permute-start.2 = (f32[260,128]{1,0:T(8,128)S(1)}, f32[260,128]{1,0:T(8,128)S(1)}, u32[]{:S(2)}, u32[]{:S(2)}) collective-permute-start(f32[260,128]{1,0:T(8,128)S(1)} %pad_maximum_fusion.14), channel_id=1, source_target_pairs={{0,2},{1,3},{2,0},{3,1},{4,6},{5,7},{6,4},{7,5},{8,10},{9,11},{10,... | collective-permute-start | bytes 399368 | tf_op jit(solution)/shard_map/ppermute | solution.py:110
  33.8 33.4 %copy-start.4 = (f32[4,128,128]{2,1,0:T(8,128)}, f32[4,128,128]{2,1,0:T(8,128)S(1)}, u32[]{:S(2)}) copy-start(f32[4,128,128]{2,1,0:T(8,128)S(1)} %fusion.47) | copy-start | bytes 786436
  34.1 6.3 %collective-permute-start.3 = (f32[260,128]{1,0:T(8,128)S(1)}, f32[260,128]{1,0:T(8,128)S(1)}, u32[]{:S(2)}, u32[]{:S(2)}) collective-permute-start(f32[260,128]{1,0:T(8,128)S(1)} %pad_maximum_fusion.15), channel_id=1, source_target_pairs={{0,6},{1,7},{2,4},{3,5},{4,2},{5,3},{6,0},{7,1},{8,14},{9,15},{10,... | collective-permute-start | bytes 399368 | tf_op jit(solution)/shard_map/ppermute | solution.py:110
  41.5 25.7 %copy-start.5 = (f32[4,128,128]{2,1,0:T(8,128)}, f32[4,128,128]{2,1,0:T(8,128)S(1)}, u32[]{:S(2)}) copy-start(f32[4,128,128]{2,1,0:T(8,128)S(1)} %fusion.62) | copy-start | bytes 786436
  41.8 5.1 %collective-permute-start.4 = (f32[260,128]{1,0:T(8,128)S(1)}, f32[260,128]{1,0:T(8,128)S(1)}, u32[]{:S(2)}, u32[]{:S(2)}) collective-permute-start(f32[260,128]{1,0:T(8,128)S(1)} %pad_maximum_fusion.16), channel_id=1, source_target_pairs={{0,8},{1,9},{2,10},{3,11},{4,12},{5,13},{6,14},{7,15},{8,0},{9,1},... | collective-permute-start | bytes 399368 | tf_op jit(solution)/shard_map/ppermute | solution.py:110
  48.0 19.2 %copy-start.6 = (f32[4,128,128]{2,1,0:T(8,128)}, f32[4,128,128]{2,1,0:T(8,128)S(1)}, u32[]{:S(2)}) copy-start(f32[4,128,128]{2,1,0:T(8,128)S(1)} %fusion.77) | copy-start | bytes 786436
  48.3 6.5 %collective-permute-start.5 = (f32[260,128]{1,0:T(8,128)S(1)}, f32[260,128]{1,0:T(8,128)S(1)}, u32[]{:S(2)}, u32[]{:S(2)}) collective-permute-start(f32[260,128]{1,0:T(8,128)S(1)} %pad_maximum_fusion.17), channel_id=1, source_target_pairs={{0,24},{1,25},{2,26},{3,27},{4,28},{5,29},{6,30},{7,31},{8,16},{9,... | collective-permute-start | bytes 399368 | tf_op jit(solution)/shard_map/ppermute | solution.py:110
  56.9 5.1 %collective-permute-start.6 = (f32[260,128]{1,0:T(8,128)S(1)}, f32[260,128]{1,0:T(8,128)S(1)}, u32[]{:S(2)}, u32[]{:S(2)}) collective-permute-start(f32[260,128]{1,0:T(8,128)S(1)} %pad_maximum_fusion.18), channel_id=1, source_target_pairs={{0,32},{1,33},{2,34},{3,35},{4,36},{5,37},{6,38},{7,39},{8,40},{9,... | collective-permute-start | bytes 399368 | tf_op jit(solution)/shard_map/ppermute | solution.py:110
  58.0 10.6 %copy-start.16 = (f32[32,4,128]{2,0,1:T(8,128)S(1)}, f32[32,4,128]{2,0,1:T(8,128)}, u32[]{:S(2)}) copy-start(f32[32,4,128]{2,0,1:T(8,128)} %copy-done.15) | copy-start | bytes 196612
  58.0 10.6 %copy-start.36 = (f32[32,128]{1,0:T(8,128)S(1)}, f32[32,128]{1,0:T(8,128)}, u32[]{:S(2)}) copy-start(f32[32,128]{1,0:T(8,128)} %param.7) | copy-start | bytes 49156
  62.3 4.9 %collective-permute-start.7 = (f32[4,128]{1,0:T(4,128)S(1)}, f32[4,128]{1,0:T(4,128)S(1)}, u32[]{:S(2)}, u32[]{:S(2)}) collective-permute-start(f32[4,128]{1,0:T(4,128)S(1)} %fusion.298), channel_id=1, source_target_pairs={{0,96},{1,97},{2,98},{3,99},{4,100},{5,101},{6,102},{7,103},{8,104... | collective-permute-start | bytes 6152 | tf_op jit(solution)/shard_map/ppermute | solution.py:110
  67.4 7.7 %copy-start.2 = (f32[1,8,128,128]{3,2,1,0:T(8,128)S(1)}, f32[1,8,128,128]{3,2,1,0:T(8,128)}, u32[]{:S(2)}) copy-start(f32[1,8,128,128]{3,2,1,0:T(8,128)} %get-tuple-element.91) | copy-start | bytes 1572868
  67.4 8.0 %copy-start.7 = (f32[1,4,128,128]{3,2,1,0:T(8,128)S(1)}, f32[1,4,128,128]{3,2,1,0:T(8,128)}, u32[]{:S(2)}) copy-start(f32[1,4,128,128]{3,2,1,0:T(8,128)} %get-tuple-element.94) | copy-start | bytes 786436
  69.4 8.6 %copy-start.13 = (f32[32,4,128]{2,0,1:T(8,128)}, f32[32,4,128]{2,0,1:T(8,128)S(1)}, u32[]{:S(2)}) copy-start(f32[32,4,128]{2,0,1:T(8,128)S(1)} %convolution_subtract_fusion.1) | copy-start | bytes 196612
  73.5 15.9 %copy-start.25 = (f32[1,128,128]{2,1,0:T(8,128)S(1)}, f32[1,128,128]{2,1,0:T(8,128)}, u32[]{:S(2)}) copy-start(f32[1,128,128]{2,1,0:T(8,128)} %copy-done.24) | copy-start | bytes 196612
  75.8 1.2 %collective-permute-start.8 = (f32[4,128]{1,0:T(4,128)S(1)}, f32[4,128]{1,0:T(4,128)S(1)}, u32[]{:S(2)}, u32[]{:S(2)}) collective-permute-start(f32[4,128]{1,0:T(4,128)S(1)} %convolution_add_fusion.19), channel_id=1, source_target_pairs={{0,1},{1,0},{2,3},{3,2},{4,5},{5,4},{6,7},{7,6},{8,9},{9,8},{10,11... | collective-permute-start | bytes 6152 | tf_op jit(solution)/shard_map/ppermute | solution.py:110
  79.8 3.7 %collective-permute-start.9 = (f32[4,128]{1,0:T(4,128)S(1)}, f32[4,128]{1,0:T(4,128)S(1)}, u32[]{:S(2)}, u32[]{:S(2)}) collective-permute-start(f32[4,128]{1,0:T(4,128)S(1)} %fusion.296), channel_id=1, source_target_pairs={{0,2},{1,3},{2,0},{3,1},{4,6},{5,7},{6,4},{7,5},{8,10},{9,11},{10,... | collective-permute-start | bytes 6152 | tf_op jit(solution)/shard_map/ppermute | solution.py:110
  84.5 4.8 %collective-permute-start.10 = (f32[4,128]{1,0:T(4,128)S(1)}, f32[4,128]{1,0:T(4,128)S(1)}, u32[]{:S(2)}, u32[]{:S(2)}) collective-permute-start(f32[4,128]{1,0:T(4,128)S(1)} %fusion.295), channel_id=1, source_target_pairs={{0,6},{1,7},{2,4},{3,5},{4,2},{5,3},{6,0},{7,1},{8,14},{9,15},{10,... | collective-permute-start | bytes 6152 | tf_op jit(solution)/shard_map/ppermute | solution.py:110
  84.9 8.3 %copy-start.9 = (f32[1,128,128]{2,1,0:T(8,128)S(1)}, f32[1,128,128]{2,1,0:T(8,128)}, u32[]{:S(2)}) copy-start(f32[1,128,128]{2,1,0:T(8,128)} %copy-done.8) | copy-start | bytes 196612
  84.9 8.3 %copy-start.27 = (f32[1,128,128]{2,1,0:T(8,128)S(1)}, f32[1,128,128]{2,1,0:T(8,128)}, u32[]{:S(2)}) copy-start(f32[1,128,128]{2,1,0:T(8,128)} %copy-done.26) | copy-start | bytes 196612
  89.6 3.6 %collective-permute-start.11 = (f32[4,128]{1,0:T(4,128)S(1)}, f32[4,128]{1,0:T(4,128)S(1)}, u32[]{:S(2)}, u32[]{:S(2)}) collective-permute-start(f32[4,128]{1,0:T(4,128)S(1)} %fusion.294), channel_id=1, source_target_pairs={{0,8},{1,9},{2,10},{3,11},{4,12},{5,13},{6,14},{7,15},{8,0},{9,1},... | collective-permute-start | bytes 6152 | tf_op jit(solution)/shard_map/ppermute | solution.py:110
  94.7 5.1 %collective-permute-start.12 = (f32[4,128]{1,0:T(4,128)S(1)}, f32[4,128]{1,0:T(4,128)S(1)}, u32[]{:S(2)}, u32[]{:S(2)}) collective-permute-start(f32[4,128]{1,0:T(4,128)S(1)} %fusion.293), channel_id=1, source_target_pairs={{0,24},{1,25},{2,26},{3,27},{4,28},{5,29},{6,30},{7,31},{8,16},{9,... | collective-permute-start | bytes 6152 | tf_op jit(solution)/shard_map/ppermute | solution.py:110
  101.0 3.7 %collective-permute-start.13 = (f32[4,128]{1,0:T(4,128)S(1)}, f32[4,128]{1,0:T(4,128)S(1)}, u32[]{:S(2)}, u32[]{:S(2)}) collective-permute-start(f32[4,128]{1,0:T(4,128)S(1)} %fusion.292), channel_id=1, source_target_pairs={{0,32},{1,33},{2,34},{3,35},{4,36},{5,37},{6,38},{7,39},{8,40},{9,... | collective-permute-start | bytes 6152 | tf_op jit(solution)/shard_map/ppermute | solution.py:110
  104.9 4.9 %collective-permute-start.14 = (f32[4,128]{1,0:T(4,128)S(1)}, f32[4,128]{1,0:T(4,128)S(1)}, u32[]{:S(2)}, u32[]{:S(2)}) collective-permute-start(f32[4,128]{1,0:T(4,128)S(1)} %fusion.290), channel_id=1, source_target_pairs={{0,96},{1,97},{2,98},{3,99},{4,100},{5,101},{6,102},{7,103},{8,104... | collective-permute-start | bytes 6152 | tf_op jit(solution)/shard_map/ppermute | solution.py:110
  (28 other events, 113.1 us)

commit v7 on v5

--- a/solution.py
+++ b/solution.py
@@ -122,14 +122,16 @@
     closed_rows = transition.T - dot(transition.T, dot(obs_map.T, gain_rows))
     forward_adds = jnp.einsum("wyn,nx->wyx", observations, gain_rows, precision=HIGHEST)
 
-    following = shifted(decay[:1], -1)
-    upcoming = jnp.concatenate([decay[1:], following], 0)
+    split = jnp.transpose(decay.reshape((-1, 2) + decay.shape[1:]), (1, 0, 2))
+    decay_even, decay_odd = split[0], split[1]
+    following = shifted(decay_even[:1], -1)
+    upcoming = interleave(decay_odd, jnp.concatenate([decay_even[1:], following], 0))
     backward_scale = upcoming[::-1]
     maps = jnp.stack([
-        pair_maps(decay[0::2], decay[1::2], closed_rows),
+        pair_maps(decay_even, decay_odd, closed_rows),
         pair_maps(backward_scale[0::2], backward_scale[1::2], smoother_gain.T),
     ])
-    adds = step_right(forward_adds[0::2], decay[1::2], closed_rows) + forward_adds[1::2]
+    adds = step_right(forward_adds[0::2], decay_odd, closed_rows) + forward_adds[1::2]
     tree = [(maps, adds)]
     while maps.shape[1] > 1:
         pairs = maps.reshape((2, -1, 2) + maps.shape[2:])
@@ -171,7 +173,7 @@
             state = down_level(state, *level)
         elif k == len(sweep) + 1:
             state, message = lax.optimization_barrier((state, message))
-            state = down_steps(state, forward_adds, decay[0::2], closed_rows)
+            state = down_steps(state, forward_adds, decay_even, closed_rows)
         got = exchanged(message, bit)
         got_map, got_add, got_back = got[:size], got[size:-size], got[-size:]
         first_map = jnp.where(upper, got_map, total_map)
@@ -195,7 +197,7 @@
     for level in sweep[max(0, len(rounds) - 2):]:
         state = down_level(state, *level)
     if len(sweep) + 1 > len(rounds) - 2:
-        state = down_steps(state, forward_adds, decay[0::2], closed_rows)
+        state = down_steps(state, forward_adds, decay_even, closed_rows)
     excl_maps, excl_adds = state
     previous = jnp.einsum("bs,tsr->tbr", entering, excl_maps, precision=HIGHEST) + excl_adds
     filtered = (

time: 106 us -> 107 us (level)
  local copies, waits for them, and re-layouts: 13.1 us -> 10.2 us
  matrix products: 29.1 us -> 31.7 us
    dot_general x18, matrix products: 4.95 us -> 8.27 us  [batched(): jnp.einsum('kij,kjl->kil', jnp.stack(lhs), jnp.stack(rhs), precision=HIGH...]
    slice x4 -> x3, local copies, waits for them, and re-layouts: 2.89 us -> 0.01 us  [the longest x1 0.01 us: local(): following = shifted(decay_even[:1], -1)]
    unnamed x130 -> x116, local copies, waits for them, and re-layouts: 4.01 us -> 3.16 us
  transfers between devices with their start and end apart: 15 -> 15, of which waited for: 13 -> 13; matrix products, arithmetic and copies ran while one was open for 16% -> 14% of each run, Pallas kernels for 0% -> 0%
where the time goes in v7:
time: 107 us; the launch traced here: 106 us
  waiting for transfers between devices  49 us (46%)
  matrix products  31.7 us (30%)
  starting transfers between devices  11 us (10%)
  local copies, waits for them, and re-layouts  10.2 us (10%)
  between operations  2.32 us (2%)
  other arithmetic  2.14 us (2%)
    ppermute x14, waiting for transfers between devices, exchanged(): return lax.ppermute(x, 'tm', [(i, partner(i, bit)) for i in range(count)])  49 us
    dot_general x18, matrix products, batched(): jnp.einsum('kij,kjl->kil', jnp.stack(lhs), jnp.stack(rhs), precision=HIGH...  8.27 us
    ppermute x1, starting transfers between devices, shifted(): return lax.ppermute(x, 'tm', pairs)  8.09 us
    dot_general x4, matrix products, dot(): return jnp.dot(a, b, precision=HIGHEST)  3.66 us
    dot_general x6, matrix products, step_right(): jnp.einsum('tbs,sr->tbr', x * scale[:, None, :], weights, precision=HIGHEST)  3.64 us
    unnamed x116, local copies, waits for them, and re-layouts  3.16 us
    ppermute x14, starting transfers between devices, exchanged(): return lax.ppermute(x, 'tm', [(i, partner(i, bit)) for i in range(count)])  2.88 us
    dot_general x4, matrix products, local(): jnp.einsum('dtij,dtjk->dtik', pairs[:, :, 0], pairs[:, :, 1], precision=H...  2.46 us
  transfers between devices with their start and end apart: 15, of which 13 were waited for; matrix products, arithmetic and copies ran while one was open for 14% of the time, Pallas kernels for 0%

profile of v7, /device:TPU:6, one launch (start us, length us, event | category | flops | bytes accessed | tf_op | source)
XLA Modules:
  0.0 106.3 jit_solution(7703811591245862090)
XLA Ops:
  1.4 8.1 %collective-permute-start = (f32[1,128]{1,0:T(1,128)S(1)}, f32[1,128]{1,0:T(1,128)S(1)}, u32[]{:S(2)}, u32[]{:S(2)}) collective-permute-start(f32[1,128]{1,0:T(1,128)S(1)} %slice_bitcast_fusion.130), channel_id=1, source_target_pairs={{1,0},{2,1},{3,2},{4,3},{5,4},{6,5},{7,6},{8,7},{9,8},{10,9},{11,1... | collective-permute-start | bytes 1544 | tf_op jit(solution)/shard_map/ppermute | solution.py:16
  9.6 1.2 %fusion.219 = f32[128,128]{1,0:T(8,128)S(1)} fusion(f32[64,128]{1,0:T(8,128)} %param.9, f32[64]{0:T(128)} %param.10), kind=kOutput, calls=%fused_computation.365 | convolution fusion | flops 12591104 | bytes 98560 | tf_op jit(solution)/shard_map/dot_general | solution.py:10
  10.8 1.0 convolution_bitcast_fusion.8
  11.9 1.1 %convolution_subtract_fusion = f32[128,128]{1,0:T(8,128)S(1)} fusion(f32[128,128]{1,0:T(8,128)} %param.8, f32[128,128]{1,0:T(8,128)S(1)} %fusion.219), kind=kOutput, calls=%fused_computation.14 | convolution fusion | flops 25182208 | bytes 196608 | tf_op jit(solution)/shard_map/dot_general | solution.py:10
  13.1 0.9 copy.52
  14.4 1.0 convolution_multiply_fusion.1
  16.0 1.0 convolution_multiply_fusion
  17.0 1.1 %fusion.13 = f32[2,8,128,128]{3,2,1,0:T(8,128)S(1)} fusion(f32[1,8,2,128,128]{4,3,2,1,0:T(8,128)S(1)} %bitcast.763, f32[1,8,2,128,128]{4,3,2,1,0:T(8,128)S(1)} %bitcast.758), kind=kOutput, calls=%fused_computation.52 | convolution fusion | flops 403177472 | bytes 5242880 | tf_op jit(solution)/shard_map/dtij,dtjk->dtik/dot_general | solution.py:143
  18.2 1.2 %fusion.319 = (f32[1,8,128,128]{3,2,1,0:T(8,128)}, f32[8,128,128]{2,1,0:T(8,128)}, f32[8,128,128]{2,1,0:T(8,128)S(1)}) fusion(f32[2,8,128,128]{3,2,1,0:T(8,128)S(1)} %fusion.13), kind=kLoop, calls=%fused_computation.559 | loop fusion | bytes 2621440 | tf_op jit(solution)/shard_map/slice | solution.py:147
  24.6 5.6 %collective-permute-done.2 = f32[260,128]{1,0:T(8,128)S(1)} collective-permute-done((f32[260,128]{1,0:T(8,128)S(1)}, f32[260,128]{1,0:T(8,128)S(1)}, u32[]{:S(2)}, u32[]{:S(2)}) %collective-permute-start.2) | collective-permute-done | bytes 133152 | tf_op jit(solution)/shard_map/ppermute | solution.py:110
  31.7 5.6 %collective-permute-done.3 = f32[260,128]{1,0:T(8,128)S(1)} collective-permute-done((f32[260,128]{1,0:T(8,128)S(1)}, f32[260,128]{1,0:T(8,128)S(1)}, u32[]{:S(2)}, u32[]{:S(2)}) %collective-permute-start.3) | collective-permute-done | bytes 133152 | tf_op jit(solution)/shard_map/ppermute | solution.py:110
  39.0 4.1 %collective-permute-done.4 = f32[260,128]{1,0:T(8,128)S(1)} collective-permute-done((f32[260,128]{1,0:T(8,128)S(1)}, f32[260,128]{1,0:T(8,128)S(1)}, u32[]{:S(2)}, u32[]{:S(2)}) %collective-permute-start.4) | collective-permute-done | bytes 133152 | tf_op jit(solution)/shard_map/ppermute | solution.py:110
  43.8 1.2 %fusion.73 = f32[4,128,128]{2,1,0:T(8,128)S(1)} fusion(f32[1,128,128]{2,1,0:T(8,128)S(1)} %get-tuple-element.131, f32[1,128,128]{2,1,0:T(8,128)S(1)} %get-tuple-element.84, f32[1,128,128]{2,1,0:T(8,128)S(1)} %get-tuple-element.130, f32[1,128,128]{2,1,0:T(8,128)S(1)} %get-tuple-element.85, f32[1,128,128]{2,1,0:T(8,128)S(1)} %get-tuple-element.109, ...), kind=kOutput, calls=%fused_computation.131 | convolution fusion | flops 101056512 | bytes 786432 | tf_op jit(solution)/shard_map/kij,kjl->kil/dot_general | solution.py:114
  47.6 4.3 %collective-permute-done.5 = f32[260,128]{1,0:T(8,128)S(1)} collective-permute-done((f32[260,128]{1,0:T(8,128)S(1)}, f32[260,128]{1,0:T(8,128)S(1)}, u32[]{:S(2)}, u32[]{:S(2)}) %collective-permute-start.5) | collective-permute-done | bytes 133152 | tf_op jit(solution)/shard_map/ppermute | solution.py:110
  53.0 1.0 convolution_bitcast_fusion.1
  55.1 4.0 %collective-permute-done.6 = f32[260,128]{1,0:T(8,128)S(1)} collective-permute-done((f32[260,128]{1,0:T(8,128)S(1)}, f32[260,128]{1,0:T(8,128)S(1)}, u32[]{:S(2)}, u32[]{:S(2)}) %collective-permute-start.6) | collective-permute-done | bytes 133152 | tf_op jit(solution)/shard_map/ppermute | solution.py:110
  59.9 4.4 %collective-permute-done.7 = f32[4,128]{1,0:T(4,128)S(1)} collective-permute-done((f32[4,128]{1,0:T(4,128)S(1)}, f32[4,128]{1,0:T(4,128)S(1)}, u32[]{:S(2)}, u32[]{:S(2)}) %collective-permute-start.7) | collective-permute-done | bytes 2080 | tf_op jit(solution)/shard_map/ppermute | solution.py:110
  64.5 1.2 %fusion.324 = f32[32,128,4]{1,2,0:T(4,128)S(1)} fusion(f32[32,128,128]{2,1,0:T(8,128)S(1)} %bitcast.771, f32[4,128,1]{1,0,2:T(4,128)S(1)} %fusion.10), kind=kOutput, calls=%fused_computation.564 | convolution fusion | flops 25165824 | bytes 2164736 | tf_op jit(solution)/shard_map/bs,tsr->tbr/dot_general | solution.py:202
  66.6 0.9 convolution_add_fusion.2
  74.8 2.5 %collective-permute-done.9 = f32[4,128]{1,0:T(4,128)S(1)} collective-permute-done((f32[4,128]{1,0:T(4,128)S(1)}, f32[4,128]{1,0:T(4,128)S(1)}, u32[]{:S(2)}, u32[]{:S(2)}) %collective-permute-start.9) | collective-permute-done | bytes 2080 | tf_op jit(solution)/shard_map/ppermute | solution.py:110
  78.3 0.8 slice.561
  79.2 3.2 %collective-permute-done.10 = f32[4,128]{1,0:T(4,128)S(1)} collective-permute-done((f32[4,128]{1,0:T(4,128)S(1)}, f32[4,128]{1,0:T(4,128)S(1)}, u32[]{:S(2)}, u32[]{:S(2)}) %collective-permute-start.10) | collective-permute-done | bytes 2080 | tf_op jit(solution)/shard_map/ppermute | solution.py:110
  82.4 1.0 fusion.148
  83.5 3.6 %collective-permute-done.11 = f32[4,128]{1,0:T(4,128)S(1)} collective-permute-done((f32[4,128]{1,0:T(4,128)S(1)}, f32[4,128]{1,0:T(4,128)S(1)}, u32[]{:S(2)}, u32[]{:S(2)}) %collective-permute-start.11) | collective-permute-done | bytes 2080 | tf_op jit(solution)/shard_map/ppermute | solution.py:110
  87.1 1.0 fusion.152
  88.8 1.0 convolution_bitcast_fusion
  89.8 3.3 %collective-permute-done.12 = f32[4,128]{1,0:T(4,128)S(1)} collective-permute-done((f32[4,128]{1,0:T(4,128)S(1)}, f32[4,128]{1,0:T(4,128)S(1)}, u32[]{:S(2)}, u32[]{:S(2)}) %collective-permute-start.12) | collective-permute-done | bytes 2080 | tf_op jit(solution)/shard_map/ppermute | solution.py:110
  93.2 1.0 fusion.156
  94.5 3.3 %collective-permute-done.13 = f32[4,128]{1,0:T(4,128)S(1)} collective-permute-done((f32[4,128]{1,0:T(4,128)S(1)}, f32[4,128]{1,0:T(4,128)S(1)}, u32[]{:S(2)}, u32[]{:S(2)}) %collective-permute-start.13) | collective-permute-done | bytes 2080 | tf_op jit(solution)/shard_map/ppermute | solution.py:110
  98.5 4.5 %collective-permute-done.14 = f32[4,128]{1,0:T(4,128)S(1)} collective-permute-done((f32[4,128]{1,0:T(4,128)S(1)}, f32[4,128]{1,0:T(4,128)S(1)}, u32[]{:S(2)}, u32[]{:S(2)}) %collective-permute-start.14) | collective-permute-done | bytes 2080 | tf_op jit(solution)/shard_map/ppermute | solution.py:110
  102.9 1.2 %fusion.8 = f32[4,128,1]{1,0,2:T(4,128)S(1)} fusion(f32[4,128]{1,0:T(4,128)S(1)} %collective-permute-done.14, f32[4,128,128]{2,1,0:T(8,128)} %copy-done.45, f32[4,128,128]{2,1,0:T(8,128)} %copy-done.8, f32[4,128,128]{2,1,0:T(8,128)} %copy-done.7, f32[4,128,128]{2,1,0:T(8,128)} %copy-done.6, f32[4,128,128]{2,1,0:T(8,128)} %copy-done.5, ...), kind=kOutput, calls=%fused_computation.44 | convolution fusion | flops 924160 | bytes 416256 | tf_op jit(solution)/shard_map/dot_general | solution.py:10
  104.1 1.2 %fusion.325 = f32[32,128,4]{1,2,0:T(4,128)S(1)} fusion(f32[32,128,128]{2,1,0:T(8,128)S(1)} %bitcast.772, f32[4,128,1]{1,0,2:T(4,128)S(1)} %fusion.8), kind=kOutput, calls=%fused_computation.565 | convolution fusion | flops 25165824 | bytes 2164736 | tf_op jit(solution)/shard_map/bs,tsr->tbr/dot_general | solution.py:238
  (292 shorter events, 27.3 us)
Async XLA Ops:
  0.6 10.1 %copy-start = (f32[32,4,64]{2,1,0:T(4,128)S(1)}, f32[32,4,64]{2,1,0:T(4,128)}, u32[]{:S(2)}) copy-start(f32[32,4,64]{2,1,0:T(4,128)} %param.6) | copy-start | bytes 98308
  0.6 15.4 %copy-start.1 = (f32[128,128]{1,0:T(8,128)S(1)}, f32[128,128]{1,0:T(8,128)}, u32[]{:S(2)}) copy-start(f32[128,128]{1,0:T(8,128)} %param.11) | copy-start | bytes 196612
  1.4 14.5 %collective-permute-start = (f32[1,128]{1,0:T(1,128)S(1)}, f32[1,128]{1,0:T(1,128)S(1)}, u32[]{:S(2)}, u32[]{:S(2)}) collective-permute-start(f32[1,128]{1,0:T(1,128)S(1)} %slice_bitcast_fusion.130), channel_id=1, source_target_pairs={{1,0},{2,1},{3,2},{4,3},{5,4},{6,5},{7,6},{8,7},{9,8},{10,9},{11,1... | collective-permute-start | bytes 1544 | tf_op jit(solution)/shard_map/ppermute | solution.py:16
  9.5 7.5 %copy-start.42 = (f32[16,128]{1,0:T(8,128)}, f32[16,128]{1,0:T(8,128)S(1)}, u32[]{:S(2)}) copy-start(f32[16,128]{1,0:T(8,128)S(1)} %get-tuple-element.152) | copy-start | bytes 24580
  11.9 12.3 %copy-start.20 = (f32[1,128,128]{2,1,0:T(8,128)}, f32[1,128,128]{2,1,0:T(8,128)S(1)}, u32[]{:S(2)}) copy-start(f32[1,128,128]{2,1,0:T(8,128)S(1)} %fusion.208) | copy-start | bytes 196612
  22.3 1.4 %collective-permute-start.1 = (f32[260,128]{1,0:T(8,128)S(1)}, f32[260,128]{1,0:T(8,128)S(1)}, u32[]{:S(2)}, u32[]{:S(2)}) collective-permute-start(f32[260,128]{1,0:T(8,128)S(1)} %pad_maximum_fusion.13), channel_id=1, source_target_pairs={{0,1},{1,0},{2,3},{3,2},{4,5},{5,4},{6,7},{7,6},{8,9},{9,8},{10,11... | collective-permute-start | bytes 399368 | tf_op jit(solution)/shard_map/ppermute | solution.py:110
  24.2 40.1 %copy-start.4 = (f32[4,128,128]{2,1,0:T(8,128)}, f32[4,128,128]{2,1,0:T(8,128)S(1)}, u32[]{:S(2)}) copy-start(f32[4,128,128]{2,1,0:T(8,128)S(1)} %fusion.28) | copy-start | bytes 786436
  24.2 7.1 %copy-start.12 = (f32[1,128,128]{2,1,0:T(8,128)}, f32[1,128,128]{2,1,0:T(8,128)S(1)}, u32[]{:S(2)}) copy-start(f32[1,128,128]{2,1,0:T(8,128)S(1)} %get-tuple-element.117) | copy-start | bytes 196612
  24.5 5.7 %collective-permute-start.2 = (f32[260,128]{1,0:T(8,128)S(1)}, f32[260,128]{1,0:T(8,128)S(1)}, u32[]{:S(2)}, u32[]{:S(2)}) collective-permute-start(f32[260,128]{1,0:T(8,128)S(1)} %pad_maximum_fusion.14), channel_id=1, source_target_pairs={{0,2},{1,3},{2,0},{3,1},{4,6},{5,7},{6,4},{7,5},{8,10},{9,11},{10,... | collective-permute-start | bytes 399368 | tf_op jit(solution)/shard_map/ppermute | solution.py:110
  30.6 33.6 %copy-start.5 = (f32[4,128,128]{2,1,0:T(8,128)}, f32[4,128,128]{2,1,0:T(8,128)S(1)}, u32[]{:S(2)}) copy-start(f32[4,128,128]{2,1,0:T(8,128)S(1)} %fusion.43) | copy-start | bytes 786436
  31.0 6.3 %collective-permute-start.3 = (f32[260,128]{1,0:T(8,128)S(1)}, f32[260,128]{1,0:T(8,128)S(1)}, u32[]{:S(2)}, u32[]{:S(2)}) collective-permute-start(f32[260,128]{1,0:T(8,128)S(1)} %pad_maximum_fusion.15), channel_id=1, source_target_pairs={{0,6},{1,7},{2,4},{3,5},{4,2},{5,3},{6,0},{7,1},{8,14},{9,15},{10,... | collective-permute-start | bytes 399368 | tf_op jit(solution)/shard_map/ppermute | solution.py:110
  37.7 26.5 %copy-start.6 = (f32[4,128,128]{2,1,0:T(8,128)}, f32[4,128,128]{2,1,0:T(8,128)S(1)}, u32[]{:S(2)}) copy-start(f32[4,128,128]{2,1,0:T(8,128)S(1)} %fusion.58) | copy-start | bytes 786436
  37.8 7.3 %copy-start.16 = (f32[1,128,128]{2,1,0:T(8,128)}, f32[1,128,128]{2,1,0:T(8,128)S(1)}, u32[]{:S(2)}) copy-start(f32[1,128,128]{2,1,0:T(8,128)S(1)} %get-tuple-element.109) | copy-start | bytes 196612
  38.1 5.1 %collective-permute-start.4 = (f32[260,128]{1,0:T(8,128)S(1)}, f32[260,128]{1,0:T(8,128)S(1)}, u32[]{:S(2)}, u32[]{:S(2)}) collective-permute-start(f32[260,128]{1,0:T(8,128)S(1)} %pad_maximum_fusion.16), channel_id=1, source_target_pairs={{0,8},{1,9},{2,10},{3,11},{4,12},{5,13},{6,14},{7,15},{8,0},{9,1},... | collective-permute-start | bytes 399368 | tf_op jit(solution)/shard_map/ppermute | solution.py:110
  45.1 19.2 %copy-start.7 = (f32[4,128,128]{2,1,0:T(8,128)}, f32[4,128,128]{2,1,0:T(8,128)S(1)}, u32[]{:S(2)}) copy-start(f32[4,128,128]{2,1,0:T(8,128)S(1)} %fusion.73) | copy-start | bytes 786436
  45.1 7.2 %copy-start.18 = (f32[1,128,128]{2,1,0:T(8,128)}, f32[1,128,128]{2,1,0:T(8,128)S(1)}, u32[]{:S(2)}) copy-start(f32[1,128,128]{2,1,0:T(8,128)S(1)} %get-tuple-element.105) | copy-start | bytes 196612
  45.4 6.5 %collective-permute-start.5 = (f32[260,128]{1,0:T(8,128)S(1)}, f32[260,128]{1,0:T(8,128)S(1)}, u32[]{:S(2)}, u32[]{:S(2)}) collective-permute-start(f32[260,128]{1,0:T(8,128)S(1)} %pad_maximum_fusion.17), channel_id=1, source_target_pairs={{0,24},{1,25},{2,26},{3,27},{4,28},{5,29},{6,30},{7,31},{8,16},{9,... | collective-permute-start | bytes 399368 | tf_op jit(solution)/shard_map/ppermute | solution.py:110
  52.3 11.9 %copy-start.8 = (f32[4,128,128]{2,1,0:T(8,128)}, f32[4,128,128]{2,1,0:T(8,128)S(1)}, u32[]{:S(2)}) copy-start(f32[4,128,128]{2,1,0:T(8,128)S(1)} %fusion.88) | copy-start | bytes 786436
  54.0 5.1 %collective-permute-start.6 = (f32[260,128]{1,0:T(8,128)S(1)}, f32[260,128]{1,0:T(8,128)S(1)}, u32[]{:S(2)}, u32[]{:S(2)}) collective-permute-start(f32[260,128]{1,0:T(8,128)S(1)} %pad_maximum_fusion.18), channel_id=1, source_target_pairs={{0,32},{1,33},{2,34},{3,35},{4,36},{5,37},{6,38},{7,39},{8,40},{9,... | collective-permute-start | bytes 399368 | tf_op jit(solution)/shard_map/ppermute | solution.py:110
  55.1 10.6 %copy-start.23 = (f32[32,4,128]{2,0,1:T(8,128)S(1)}, f32[32,4,128]{2,0,1:T(8,128)}, u32[]{:S(2)}) copy-start(f32[32,4,128]{2,0,1:T(8,128)} %copy-done.22) | copy-start | bytes 196612
  55.1 10.6 %copy-start.48 = (f32[32,128]{1,0:T(8,128)S(1)}, f32[32,128]{1,0:T(8,128)}, u32[]{:S(2)}) copy-start(f32[32,128]{1,0:T(8,128)} %param.7) | copy-start | bytes 49156
  59.4 4.9 %collective-permute-start.7 = (f32[4,128]{1,0:T(4,128)S(1)}, f32[4,128]{1,0:T(4,128)S(1)}, u32[]{:S(2)}, u32[]{:S(2)}) collective-permute-start(f32[4,128]{1,0:T(4,128)S(1)} %fusion.292), channel_id=1, source_target_pairs={{0,96},{1,97},{2,98},{3,99},{4,100},{5,101},{6,102},{7,103},{8,104... | collective-permute-start | bytes 6152 | tf_op jit(solution)/shard_map/ppermute | solution.py:110
  68.8 1.4 %collective-permute-start.8 = (f32[4,128]{1,0:T(4,128)S(1)}, f32[4,128]{1,0:T(4,128)S(1)}, u32[]{:S(2)}, u32[]{:S(2)}) collective-permute-start(f32[4,128]{1,0:T(4,128)S(1)} %convolution_add_fusion.18), channel_id=1, source_target_pairs={{0,1},{1,0},{2,3},{3,2},{4,5},{5,4},{6,7},{7,6},{8,9},{9,8},{10,11... | collective-permute-start | bytes 6152 | tf_op jit(solution)/shard_map/ppermute | solution.py:110
  73.1 9.3 %copy-start.15 = (f32[1,128,128]{2,1,0:T(8,128)S(1)}, f32[1,128,128]{2,1,0:T(8,128)}, u32[]{:S(2)}) copy-start(f32[1,128,128]{2,1,0:T(8,128)} %copy-done.14) | copy-start | bytes 196612
  73.1 14.0 %copy-start.17 = (f32[1,128,128]{2,1,0:T(8,128)S(1)}, f32[1,128,128]{2,1,0:T(8,128)}, u32[]{:S(2)}) copy-start(f32[1,128,128]{2,1,0:T(8,128)} %copy-done.16) | copy-start | bytes 196612
  73.2 19.9 %copy-start.19 = (f32[1,128,128]{2,1,0:T(8,128)S(1)}, f32[1,128,128]{2,1,0:T(8,128)}, u32[]{:S(2)}) copy-start(f32[1,128,128]{2,1,0:T(8,128)} %copy-done.18) | copy-start | bytes 196612
  73.6 3.7 %collective-permute-start.9 = (f32[4,128]{1,0:T(4,128)S(1)}, f32[4,128]{1,0:T(4,128)S(1)}, u32[]{:S(2)}, u32[]{:S(2)}) collective-permute-start(f32[4,128]{1,0:T(4,128)S(1)} %fusion.289), channel_id=1, source_target_pairs={{0,2},{1,3},{2,0},{3,1},{4,6},{5,7},{6,4},{7,5},{8,10},{9,11},{10,... | collective-permute-start | bytes 6152 | tf_op jit(solution)/shard_map/ppermute | solution.py:110
  77.5 4.9 %collective-permute-start.10 = (f32[4,128]{1,0:T(4,128)S(1)}, f32[4,128]{1,0:T(4,128)S(1)}, u32[]{:S(2)}, u32[]{:S(2)}) collective-permute-start(f32[4,128]{1,0:T(4,128)S(1)} %fusion.288), channel_id=1, source_target_pairs={{0,6},{1,7},{2,4},{3,5},{4,2},{5,3},{6,0},{7,1},{8,14},{9,15},{10,... | collective-permute-start | bytes 6152 | tf_op jit(solution)/shard_map/ppermute | solution.py:110
  83.4 3.6 %collective-permute-start.11 = (f32[4,128]{1,0:T(4,128)S(1)}, f32[4,128]{1,0:T(4,128)S(1)}, u32[]{:S(2)}, u32[]{:S(2)}) collective-permute-start(f32[4,128]{1,0:T(4,128)S(1)} %fusion.287), channel_id=1, source_target_pairs={{0,8},{1,9},{2,10},{3,11},{4,12},{5,13},{6,14},{7,15},{8,0},{9,1},... | collective-permute-start | bytes 6152 | tf_op jit(solution)/shard_map/ppermute | solution.py:110
  88.1 5.0 %collective-permute-start.12 = (f32[4,128]{1,0:T(4,128)S(1)}, f32[4,128]{1,0:T(4,128)S(1)}, u32[]{:S(2)}, u32[]{:S(2)}) collective-permute-start(f32[4,128]{1,0:T(4,128)S(1)} %fusion.286), channel_id=1, source_target_pairs={{0,24},{1,25},{2,26},{3,27},{4,28},{5,29},{6,30},{7,31},{8,16},{9,... | collective-permute-start | bytes 6152 | tf_op jit(solution)/shard_map/ppermute | solution.py:110
  94.2 3.6 %collective-permute-start.13 = (f32[4,128]{1,0:T(4,128)S(1)}, f32[4,128]{1,0:T(4,128)S(1)}, u32[]{:S(2)}, u32[]{:S(2)}) collective-permute-start(f32[4,128]{1,0:T(4,128)S(1)} %fusion.285), channel_id=1, source_target_pairs={{0,32},{1,33},{2,34},{3,35},{4,36},{5,37},{6,38},{7,39},{8,40},{9,... | collective-permute-start | bytes 6152 | tf_op jit(solution)/shard_map/ppermute | solution.py:110
  98.1 4.9 %collective-permute-start.14 = (f32[4,128]{1,0:T(4,128)S(1)}, f32[4,128]{1,0:T(4,128)S(1)}, u32[]{:S(2)}, u32[]{:S(2)}) collective-permute-start(f32[4,128]{1,0:T(4,128)S(1)} %fusion.284), channel_id=1, source_target_pairs={{0,96},{1,97},{2,98},{3,99},{4,100},{5,101},{6,102},{7,103},{8,104... | collective-permute-start | bytes 6152 | tf_op jit(solution)/shard_map/ppermute | solution.py:110
  (40 other events, 149.7 us)

commit v8 on v5

--- a/solution.py
+++ b/solution.py
@@ -166,12 +166,6 @@
             stored.append((back_total, back_total, back_before))
             break
         message = jnp.concatenate([total_map, total_add, back_total], 0)
-        if 1 <= k <= len(sweep):
-            (state, level), message = lax.optimization_barrier(((state, sweep[k - 1]), message))
-            state = down_level(state, *level)
-        elif k == len(sweep) + 1:
-            state, message = lax.optimization_barrier((state, message))
-            state = down_steps(state, forward_adds, decay[0::2], closed_rows)
         got = exchanged(message, bit)
         got_map, got_add, got_back = got[:size], got[size:-size], got[-size:]
         first_map = jnp.where(upper, got_map, total_map)
@@ -181,16 +175,19 @@
         back_first = jnp.where(upper, back_total, got_back)
         back_second = jnp.where(upper, got_back, back_total)
         stored.append((back_total, back_second, back_before))
-        products = batched(
-            [first_map, got_map, back_first, got_back],
-            [second_map, before_map, back_second, back_before],
-        )
-        offsets = batched([first_add, got_add], [second_map, before_map])
-        total_map, total_add = products[0], offsets[0] + second_add
-        before_map = jnp.where(upper, products[1], before_map)
-        before_add = jnp.where(upper, offsets[1] + before_add, before_add)
-        back_total = products[2]
-        back_before = jnp.where(upper, back_before, products[3])
+        totals = batched([first_map, back_first], [second_map, back_second])
+        total_add = dot(first_add, second_map) + second_add
+        spans = batched([got_map, got_back], [before_map, back_before])
+        if 1 <= k <= len(sweep):
+            (state, level), spans = lax.optimization_barrier(((state, sweep[k - 1]), spans))
+            state = down_level(state, *level)
+        elif k == len(sweep) + 1:
+            state, spans = lax.optimization_barrier((state, spans))
+            state = down_steps(state, forward_adds, decay[0::2], closed_rows)
+        before_add = jnp.where(upper, dot(got_add, before_map) + before_add, before_add)
+        total_map, back_total = totals[0], totals[1]
+        before_map = jnp.where(upper, spans[0], before_map)
+        back_before = jnp.where(upper, back_before, spans[1])
 
     for level in sweep[max(0, len(rounds) - 2):]:
         state = down_level(state, *level)

time: 106 us -> 106 us (level); the launches traced: 106 us -> 104 us
  waiting for transfers between devices: 48.6 us -> 41.4 us
  matrix products: 29.1 us -> 31.7 us
  starting transfers between devices: 11.1 us -> 12.4 us
    ppermute x14, waiting for transfers between devices: 48.6 us -> 41.4 us  [exchanged(): return lax.ppermute(x, 'tm', [(i, partner(i, bit)) for i in range(count)])]
    ppermute x14, starting transfers between devices: 2.97 us -> 4.27 us  [exchanged(): return lax.ppermute(x, 'tm', [(i, partner(i, bit)) for i in range(count)])]
    dot_general x18 -> x17, matrix products: 4.95 us -> 5.95 us  [batched(): jnp.einsum('kij,kjl->kil', jnp.stack(lhs), jnp.stack(rhs), precision=HIGH...]
    dot_general x4 -> x16, matrix products: 3.67 us -> 4.51 us  [dot(): return jnp.dot(a, b, precision=HIGHEST)]
  transfers between devices with their start and end apart: 15 -> 15, of which waited for: 13 -> 12; matrix products, arithmetic and copies ran while one was open for 16% -> 21% of each run, Pallas kernels for 0% -> 0%
where the time goes in v8:
time: 106 us; the launch traced here: 104 us
  waiting for transfers between devices  41.4 us (39%)
  matrix products  31.7 us (30%)
  local copies, waits for them, and re-layouts  13.6 us (13%)
  starting transfers between devices  12.4 us (12%)
  between operations  2.37 us (2%)
  other arithmetic  2.13 us (2%)
    ppermute x14, waiting for transfers between devices, exchanged(): return lax.ppermute(x, 'tm', [(i, partner(i, bit)) for i in range(count)])  41.4 us
    ppermute x1, starting transfers between devices, shifted(): return lax.ppermute(x, 'tm', pairs)  8.09 us
    dot_general x17, matrix products, batched(): jnp.einsum('kij,kjl->kil', jnp.stack(lhs), jnp.stack(rhs), precision=HIGH...  5.95 us
    dot_general x16, matrix products, dot(): return jnp.dot(a, b, precision=HIGHEST)  4.51 us
    dot_general x6, matrix products, step_right(): jnp.einsum('tbs,sr->tbr', x * scale[:, None, :], weights, precision=HIGHEST)  4.42 us
    ppermute x14, starting transfers between devices, exchanged(): return lax.ppermute(x, 'tm', [(i, partner(i, bit)) for i in range(count)])  4.27 us
    unnamed x130, local copies, waits for them, and re-layouts  3.74 us
    dot_general x4, matrix products, local(): jnp.einsum('dtij,dtjk->dtik', pairs[:, :, 0], pairs[:, :, 1], precision=H...  2.46 us
  transfers between devices with their start and end apart: 15, of which 12 were waited for; matrix products, arithmetic and copies ran while one was open for 21% of the time, Pallas kernels for 0%

profile of v8, /device:TPU:6, one launch (start us, length us, event | category | flops | bytes accessed | tf_op | source)
XLA Modules:
  0.0 103.6 jit_solution(7758013968549401258)
XLA Ops:
  1.4 8.1 %collective-permute-start = (f32[1,128]{1,0:T(1,128)S(1)}, f32[1,128]{1,0:T(1,128)S(1)}, u32[]{:S(2)}, u32[]{:S(2)}) collective-permute-start(f32[1,128]{1,0:T(1,128)S(1)} %slice.386), channel_id=1, source_target_pairs={{1,0},{2,1},{3,2},{4,3},{5,4},{6,5},{7,6},{8,7},{9,8},{10,9},{11,1... | collective-permute-start | bytes 1544 | tf_op jit(solution)/shard_map/ppermute | solution.py:16
  11.7 1.0 convolution_bitcast_fusion.8
  12.8 1.2 %fusion.161 = f32[128,128]{1,0:T(8,128)S(1)} fusion(f32[64,128]{1,0:T(8,128)} %param.9, f32[64]{0:T(128)} %param.10), kind=kOutput, calls=%fused_computation.326 | convolution fusion | flops 12591104 | bytes 98560 | tf_op jit(solution)/shard_map/dot_general | solution.py:10
  14.0 1.1 %convolution_subtract_fusion = f32[128,128]{1,0:T(8,128)S(1)} fusion(f32[128,128]{1,0:T(8,128)} %param.8, f32[128,128]{1,0:T(8,128)S(1)} %fusion.161), kind=kOutput, calls=%fused_computation.13 | convolution fusion | flops 25182208 | bytes 196608 | tf_op jit(solution)/shard_map/dot_general | solution.py:10
  16.1 1.0 convolution_multiply_fusion
  17.8 1.0 broadcast_multiply_fusion
  18.8 1.1 %fusion.18 = f32[2,8,128,128]{3,2,1,0:T(8,128)S(1)} fusion(f32[1,8,2,128,128]{4,3,2,1,0:T(8,128)S(1)} %bitcast.681, f32[1,8,2,128,128]{4,3,2,1,0:T(8,128)S(1)} %bitcast.676), kind=kOutput, calls=%fused_computation.68 | convolution fusion | flops 403177472 | bytes 5242880 | tf_op jit(solution)/shard_map/dtij,dtjk->dtik/dot_general | solution.py:141
  20.0 1.2 %fusion.265 = (f32[1,8,128,128]{3,2,1,0:T(8,128)}, f32[8,128,128]{2,1,0:T(8,128)}, f32[8,128,128]{2,1,0:T(8,128)S(1)}) fusion(f32[2,8,128,128]{3,2,1,0:T(8,128)S(1)} %fusion.18), kind=kLoop, calls=%fused_computation.485 | loop fusion | bytes 2621440 | tf_op jit(solution)/shard_map/slice | solution.py:145
  22.2 0.9 fusion.266
  26.7 5.5 %collective-permute-done.2 = f32[260,128]{1,0:T(8,128)S(1)} collective-permute-done((f32[260,128]{1,0:T(8,128)S(1)}, f32[260,128]{1,0:T(8,128)S(1)}, u32[]{:S(2)}, u32[]{:S(2)}) %collective-permute-start.2) | collective-permute-done | bytes 133152 | tf_op jit(solution)/shard_map/ppermute | solution.py:110
  33.4 5.6 %collective-permute-done.3 = f32[260,128]{1,0:T(8,128)S(1)} collective-permute-done((f32[260,128]{1,0:T(8,128)S(1)}, f32[260,128]{1,0:T(8,128)S(1)}, u32[]{:S(2)}, u32[]{:S(2)}) %collective-permute-start.3) | collective-permute-done | bytes 133152 | tf_op jit(solution)/shard_map/ppermute | solution.py:110
  40.6 4.1 %collective-permute-done.4 = f32[260,128]{1,0:T(8,128)S(1)} collective-permute-done((f32[260,128]{1,0:T(8,128)S(1)}, f32[260,128]{1,0:T(8,128)S(1)}, u32[]{:S(2)}, u32[]{:S(2)}) %collective-permute-start.4) | collective-permute-done | bytes 133152 | tf_op jit(solution)/shard_map/ppermute | solution.py:110
  47.4 4.5 %collective-permute-done.5 = f32[260,128]{1,0:T(8,128)S(1)} collective-permute-done((f32[260,128]{1,0:T(8,128)S(1)}, f32[260,128]{1,0:T(8,128)S(1)}, u32[]{:S(2)}, u32[]{:S(2)}) %collective-permute-start.5) | collective-permute-done | bytes 133152 | tf_op jit(solution)/shard_map/ppermute | solution.py:110
  55.2 2.5 %collective-permute-done.6 = f32[260,128]{1,0:T(8,128)S(1)} collective-permute-done((f32[260,128]{1,0:T(8,128)S(1)}, f32[260,128]{1,0:T(8,128)S(1)}, u32[]{:S(2)}, u32[]{:S(2)}) %collective-permute-start.6) | collective-permute-done | bytes 133152 | tf_op jit(solution)/shard_map/ppermute | solution.py:110
  59.1 1.0 convolution_bitcast_fusion.1
  60.8 1.8 %collective-permute-done.7 = f32[4,128]{1,0:T(4,128)S(1)} collective-permute-done((f32[4,128]{1,0:T(4,128)S(1)}, f32[4,128]{1,0:T(4,128)S(1)}, u32[]{:S(2)}, u32[]{:S(2)}) %collective-permute-start.7) | collective-permute-done | bytes 2080 | tf_op jit(solution)/shard_map/ppermute | solution.py:110
  62.9 1.2 %fusion.269 = f32[32,128,4]{1,2,0:T(4,128)S(1)} fusion(f32[32,128,128]{2,1,0:T(8,128)S(1)} %bitcast.690, f32[4,128,1]{1,0,2:T(4,128)S(1)} %fusion.15), kind=kOutput, calls=%fused_computation.489 | convolution fusion | flops 25165824 | bytes 2164736 | tf_op jit(solution)/shard_map/bs,tsr->tbr/dot_general | solution.py:197
  65.6 1.0 convolution_add_fusion.2
  69.2 0.8 slice.584
  70.4 0.9 fusion.5
  73.7 1.0 convolution_bitcast_fusion
  76.6 4.7 %collective-permute-done.10 = f32[4,128]{1,0:T(4,128)S(1)} collective-permute-done((f32[4,128]{1,0:T(4,128)S(1)}, f32[4,128]{1,0:T(4,128)S(1)}, u32[]{:S(2)}, u32[]{:S(2)}) %collective-permute-start.10) | collective-permute-done | bytes 2080 | tf_op jit(solution)/shard_map/ppermute | solution.py:110
  82.6 2.8 %collective-permute-done.11 = f32[4,128]{1,0:T(4,128)S(1)} collective-permute-done((f32[4,128]{1,0:T(4,128)S(1)}, f32[4,128]{1,0:T(4,128)S(1)}, u32[]{:S(2)}, u32[]{:S(2)}) %collective-permute-start.11) | collective-permute-done | bytes 2080 | tf_op jit(solution)/shard_map/ppermute | solution.py:110
  86.2 0.8 slice.505
  87.0 3.4 %collective-permute-done.12 = f32[4,128]{1,0:T(4,128)S(1)} collective-permute-done((f32[4,128]{1,0:T(4,128)S(1)}, f32[4,128]{1,0:T(4,128)S(1)}, u32[]{:S(2)}, u32[]{:S(2)}) %collective-permute-start.12) | collective-permute-done | bytes 2080 | tf_op jit(solution)/shard_map/ppermute | solution.py:110
  90.5 1.1 %fusion.37 = f32[2,4,128]{2,1,0:T(4,128)S(1)} fusion(f32[1,128,128]{2,1,0:T(8,128)} %copy-done.20, f32[1,128,128]{2,1,0:T(8,128)} %copy-done.34, f32[1,4,128]{2,1,0:T(4,128)S(1)} %bitcast.749, f32[1,4,128]{2,1,0:T(4,128)S(1)} %select_bitcast_fusion.17), kind=kOutput, calls=%fused_computation.128 | convolution fusion | flops 1606656 | bytes 139264 | tf_op jit(solution)/shard_map/kij,kjl->kil/dot_general | solution.py:114
  91.6 0.9 add_bitcast_fusion
  92.6 2.6 %collective-permute-done.13 = f32[4,128]{1,0:T(4,128)S(1)} collective-permute-done((f32[4,128]{1,0:T(4,128)S(1)}, f32[4,128]{1,0:T(4,128)S(1)}, u32[]{:S(2)}, u32[]{:S(2)}) %collective-permute-start.13) | collective-permute-done | bytes 2080 | tf_op jit(solution)/shard_map/ppermute | solution.py:110
  95.2 1.1 %fusion.35 = f32[2,4,128]{2,1,0:T(4,128)S(1)} fusion(f32[1,128,128]{2,1,0:T(8,128)} %copy-done.37, f32[1,128,128]{2,1,0:T(8,128)} %get-tuple-element.98, f32[1,4,128]{2,1,0:T(4,128)S(1)} %bitcast.751, f32[1,4,128]{2,1,0:T(4,128)S(1)} %select_bitcast_fusion.16), kind=kOutput, calls=%fused_computation.126 | convolution fusion | flops 1606656 | bytes 139264 | tf_op jit(solution)/shard_map/kij,kjl->kil/dot_general | solution.py:114
  96.3 1.5 %collective-permute-start.14 = (f32[4,128]{1,0:T(4,128)S(1)}, f32[4,128]{1,0:T(4,128)S(1)}, u32[]{:S(2)}, u32[]{:S(2)}) collective-permute-start(f32[4,128]{1,0:T(4,128)S(1)} %fusion.214), channel_id=1, source_target_pairs={{0,96},{1,97},{2,98},{3,99},{4,100},{5,101},{6,102},{7,103},{8,104... | collective-permute-start | bytes 6152 | tf_op jit(solution)/shard_map/ppermute | solution.py:110
  98.1 3.0 %collective-permute-done.14 = f32[4,128]{1,0:T(4,128)S(1)} collective-permute-done((f32[4,128]{1,0:T(4,128)S(1)}, f32[4,128]{1,0:T(4,128)S(1)}, u32[]{:S(2)}, u32[]{:S(2)}) %collective-permute-start.14) | collective-permute-done | bytes 2080 | tf_op jit(solution)/shard_map/ppermute | solution.py:110
  101.3 1.2 %fusion.270 = f32[32,128,4]{1,2,0:T(4,128)S(1)} fusion(f32[32,128,128]{2,1,0:T(8,128)S(1)} %bitcast.689, f32[4,128,1]{1,0,2:T(4,128)S(1)} %fusion.8), kind=kOutput, calls=%fused_computation.490 | convolution fusion | flops 25165824 | bytes 2164736 | tf_op jit(solution)/shard_map/bs,tsr->tbr/dot_general | solution.py:233
  (309 shorter events, 31.3 us)
Async XLA Ops:
  0.6 11.0 %copy-start = (f32[32,4,64]{2,1,0:T(4,128)S(1)}, f32[32,4,64]{2,1,0:T(4,128)}, u32[]{:S(2)}) copy-start(f32[32,4,64]{2,1,0:T(4,128)} %param.6) | copy-start | bytes 98308
  0.6 17.0 %copy-start.1 = (f32[128,128]{1,0:T(8,128)S(1)}, f32[128,128]{1,0:T(8,128)}, u32[]{:S(2)}) copy-start(f32[128,128]{1,0:T(8,128)} %param.11) | copy-start | bytes 196612
  1.4 16.3 %collective-permute-start = (f32[1,128]{1,0:T(1,128)S(1)}, f32[1,128]{1,0:T(1,128)S(1)}, u32[]{:S(2)}, u32[]{:S(2)}) collective-permute-start(f32[1,128]{1,0:T(1,128)S(1)} %slice.386), channel_id=1, source_target_pairs={{1,0},{2,1},{3,2},{4,3},{5,4},{6,5},{7,6},{8,7},{9,8},{10,9},{11,1... | collective-permute-start | bytes 1544 | tf_op jit(solution)/shard_map/ppermute | solution.py:16
  10.2 7.6 %copy-start.50 = (f32[16,128]{1,0:T(8,128)}, f32[16,128]{1,0:T(8,128)S(1)}, u32[]{:S(2)}) copy-start(f32[16,128]{1,0:T(8,128)S(1)} %slice.383) | copy-start | bytes 24580
  12.7 7.3 %copy-start.40 = (f32[16,4,128]{2,0,1:T(8,128)}, f32[16,4,128]{2,0,1:T(8,128)S(1)}, u32[]{:S(2)}) copy-start(f32[16,4,128]{2,0,1:T(8,128)S(1)} %slice.398) | copy-start | bytes 98308
  12.8 20.6 %copy-start.14 = (f32[1,1,128,128]{3,2,1,0:T(8,128)}, f32[1,1,128,128]{3,2,1,0:T(8,128)S(1)}, u32[]{:S(2)}) copy-start(f32[1,1,128,128]{3,2,1,0:T(8,128)S(1)} %fusion.153) | copy-start | bytes 196612
  12.8 12.9 %copy-start.24 = (f32[1,128,128]{2,1,0:T(8,128)}, f32[1,128,128]{2,1,0:T(8,128)S(1)}, u32[]{:S(2)}) copy-start(f32[1,128,128]{2,1,0:T(8,128)S(1)} %fusion.154) | copy-start | bytes 196612
  24.2 1.4 %collective-permute-start.1 = (f32[260,128]{1,0:T(8,128)S(1)}, f32[260,128]{1,0:T(8,128)S(1)}, u32[]{:S(2)}, u32[]{:S(2)}) collective-permute-start(f32[260,128]{1,0:T(8,128)S(1)} %pad_maximum_fusion.23), channel_id=1, source_target_pairs={{0,1},{1,0},{2,3},{3,2},{4,5},{5,4},{6,7},{7,6},{8,9},{9,8},{10,11... | collective-permute-start | bytes 399368 | tf_op jit(solution)/shard_map/ppermute | solution.py:110
  25.6 7.5 %copy-start.26 = (f32[1,128,128]{2,1,0:T(8,128)}, f32[1,128,128]{2,1,0:T(8,128)S(1)}, u32[]{:S(2)}) copy-start(f32[1,128,128]{2,1,0:T(8,128)S(1)} %get-tuple-element.93) | copy-start | bytes 196612
  25.9 19.1 %copy-start.4 = (f32[2,128,128]{2,1,0:T(8,128)}, f32[2,128,128]{2,1,0:T(8,128)S(1)}, u32[]{:S(2)}) copy-start(f32[2,128,128]{2,1,0:T(8,128)S(1)} %fusion.45) | copy-start | bytes 393220
  26.0 13.1 %copy-start.16 = (f32[1,128,128]{2,1,0:T(8,128)}, f32[1,128,128]{2,1,0:T(8,128)S(1)}, u32[]{:S(2)}) copy-start(f32[1,128,128]{2,1,0:T(8,128)S(1)} %get-tuple-element.128) | copy-start | bytes 196612
  26.5 5.7 %collective-permute-start.2 = (f32[260,128]{1,0:T(8,128)S(1)}, f32[260,128]{1,0:T(8,128)S(1)}, u32[]{:S(2)}, u32[]{:S(2)}) collective-permute-start(f32[260,128]{1,0:T(8,128)S(1)} %pad_maximum_fusion.24), channel_id=1, source_target_pairs={{0,2},{1,3},{2,0},{3,1},{4,6},{5,7},{6,4},{7,5},{8,10},{9,11},{10,... | collective-permute-start | bytes 399368 | tf_op jit(solution)/shard_map/ppermute | solution.py:110
  32.7 6.3 %collective-permute-start.3 = (f32[260,128]{1,0:T(8,128)S(1)}, f32[260,128]{1,0:T(8,128)S(1)}, u32[]{:S(2)}, u32[]{:S(2)}) collective-permute-start(f32[260,128]{1,0:T(8,128)S(1)} %pad_maximum_fusion.25), channel_id=1, source_target_pairs={{0,6},{1,7},{2,4},{3,5},{4,2},{5,3},{6,0},{7,1},{8,14},{9,15},{10,... | collective-permute-start | bytes 399368 | tf_op jit(solution)/shard_map/ppermute | solution.py:110
  33.1 11.9 %copy-start.7 = (f32[2,128,128]{2,1,0:T(8,128)}, f32[2,128,128]{2,1,0:T(8,128)S(1)}, u32[]{:S(2)}) copy-start(f32[2,128,128]{2,1,0:T(8,128)S(1)} %fusion.43) | copy-start | bytes 393220
  33.1 7.4 %copy-start.18 = (f32[1,128,128]{2,1,0:T(8,128)}, f32[1,128,128]{2,1,0:T(8,128)S(1)}, u32[]{:S(2)}) copy-start(f32[1,128,128]{2,1,0:T(8,128)S(1)} %get-tuple-element.124) | copy-start | bytes 196612
  39.6 5.1 %collective-permute-start.4 = (f32[260,128]{1,0:T(8,128)S(1)}, f32[260,128]{1,0:T(8,128)S(1)}, u32[]{:S(2)}, u32[]{:S(2)}) collective-permute-start(f32[260,128]{1,0:T(8,128)S(1)} %pad_maximum_fusion.26), channel_id=1, source_target_pairs={{0,8},{1,9},{2,10},{3,11},{4,12},{5,13},{6,14},{7,15},{8,0},{9,1},... | collective-permute-start | bytes 399368 | tf_op jit(solution)/shard_map/ppermute | solution.py:110
  45.1 9.9 %copy-start.20 = (f32[1,128,128]{2,1,0:T(8,128)}, f32[1,128,128]{2,1,0:T(8,128)S(1)}, u32[]{:S(2)}) copy-start(f32[1,128,128]{2,1,0:T(8,128)S(1)} %get-tuple-element.116) | copy-start | bytes 196612
  45.6 6.3 %collective-permute-start.5 = (f32[260,128]{1,0:T(8,128)S(1)}, f32[260,128]{1,0:T(8,128)S(1)}, u32[]{:S(2)}, u32[]{:S(2)}) collective-permute-start(f32[260,128]{1,0:T(8,128)S(1)} %pad_maximum_fusion.27), channel_id=1, source_target_pairs={{0,24},{1,25},{2,26},{3,27},{4,28},{5,29},{6,30},{7,31},{8,16},{9,... | collective-permute-start | bytes 399368 | tf_op jit(solution)/shard_map/ppermute | solution.py:110
  52.4 5.3 %collective-permute-start.6 = (f32[260,128]{1,0:T(8,128)S(1)}, f32[260,128]{1,0:T(8,128)S(1)}, u32[]{:S(2)}, u32[]{:S(2)}) collective-permute-start(f32[260,128]{1,0:T(8,128)S(1)} %pad_maximum_fusion.28), channel_id=1, source_target_pairs={{0,32},{1,33},{2,34},{3,35},{4,36},{5,37},{6,38},{7,39},{8,40},{9,... | collective-permute-start | bytes 399368 | tf_op jit(solution)/shard_map/ppermute | solution.py:110
  57.9 4.8 %collective-permute-start.7 = (f32[4,128]{1,0:T(4,128)S(1)}, f32[4,128]{1,0:T(4,128)S(1)}, u32[]{:S(2)}, u32[]{:S(2)}) collective-permute-start(f32[4,128]{1,0:T(4,128)S(1)} %convolution_add_fusion.25), channel_id=1, source_target_pairs={{0,96},{1,97},{2,98},{3,99},{4,100},{5,101},{6,102},{7,103},{8,104... | collective-permute-start | bytes 6152 | tf_op jit(solution)/shard_map/ppermute | solution.py:110
  62.8 7.2 %copy-start.15 = (f32[1,1,128,128]{3,2,1,0:T(8,128)S(1)}, f32[1,1,128,128]{3,2,1,0:T(8,128)}, u32[]{:S(2)}) copy-start(f32[1,1,128,128]{3,2,1,0:T(8,128)} %copy-done.14) | copy-start | bytes 196612
  62.8 7.2 %copy-start.11 = (f32[4,128,128]{2,1,0:T(8,128)S(1)}, f32[4,128,128]{2,1,0:T(8,128)}, u32[]{:S(2)}) copy-start(f32[4,128,128]{2,1,0:T(8,128)} %get-tuple-element.55) | copy-start | bytes 786436
  67.9 1.3 %collective-permute-start.8 = (f32[4,128]{1,0:T(4,128)S(1)}, f32[4,128]{1,0:T(4,128)S(1)}, u32[]{:S(2)}, u32[]{:S(2)}) collective-permute-start(f32[4,128]{1,0:T(4,128)S(1)} %convolution_add_fusion.18), channel_id=1, source_target_pairs={{0,1},{1,0},{2,3},{3,2},{4,5},{5,4},{6,7},{7,6},{8,9},{9,8},{10,11... | collective-permute-start | bytes 6152 | tf_op jit(solution)/shard_map/ppermute | solution.py:110
  72.2 3.9 %collective-permute-start.9 = (f32[4,128]{1,0:T(4,128)S(1)}, f32[4,128]{1,0:T(4,128)S(1)}, u32[]{:S(2)}, u32[]{:S(2)}) collective-permute-start(f32[4,128]{1,0:T(4,128)S(1)} %fusion.219), channel_id=1, source_target_pairs={{0,2},{1,3},{2,0},{3,1},{4,6},{5,7},{6,4},{7,5},{8,10},{9,11},{10,... | collective-permute-start | bytes 6152 | tf_op jit(solution)/shard_map/ppermute | solution.py:110
  74.8 10.6 %copy-start.22 = (f32[1,128,128]{2,1,0:T(8,128)S(1)}, f32[1,128,128]{2,1,0:T(8,128)}, u32[]{:S(2)}) copy-start(f32[1,128,128]{2,1,0:T(8,128)} %copy-done.21) | copy-start | bytes 196612
  74.8 10.6 %copy-start.33 = (f32[1,128,128]{2,1,0:T(8,128)S(1)}, f32[1,128,128]{2,1,0:T(8,128)}, u32[]{:S(2)}) copy-start(f32[1,128,128]{2,1,0:T(8,128)} %copy-done.32) | copy-start | bytes 196612
  76.4 9.8 %copy-start.60 = (f32[2,4,128]{2,1,0:T(4,128)}, f32[2,4,128]{2,1,0:T(4,128)S(1)}, u32[]{:S(2)}) copy-start(f32[2,4,128]{2,1,0:T(4,128)S(1)} %fusion.44) | copy-start | bytes 12292
  76.4 4.9 %collective-permute-start.10 = (f32[4,128]{1,0:T(4,128)S(1)}, f32[4,128]{1,0:T(4,128)S(1)}, u32[]{:S(2)}, u32[]{:S(2)}) collective-permute-start(f32[4,128]{1,0:T(4,128)S(1)} %fusion.218), channel_id=1, source_target_pairs={{0,6},{1,7},{2,4},{3,5},{4,2},{5,3},{6,0},{7,1},{8,14},{9,15},{10,... | collective-permute-start | bytes 6152 | tf_op jit(solution)/shard_map/ppermute | solution.py:110
  81.5 3.9 %collective-permute-start.11 = (f32[4,128]{1,0:T(4,128)S(1)}, f32[4,128]{1,0:T(4,128)S(1)}, u32[]{:S(2)}, u32[]{:S(2)}) collective-permute-start(f32[4,128]{1,0:T(4,128)S(1)} %fusion.217), channel_id=1, source_target_pairs={{0,8},{1,9},{2,10},{3,11},{4,12},{5,13},{6,14},{7,15},{8,0},{9,1},... | collective-permute-start | bytes 6152 | tf_op jit(solution)/shard_map/ppermute | solution.py:110
  85.6 4.9 %collective-permute-start.12 = (f32[4,128]{1,0:T(4,128)S(1)}, f32[4,128]{1,0:T(4,128)S(1)}, u32[]{:S(2)}, u32[]{:S(2)}) collective-permute-start(f32[4,128]{1,0:T(4,128)S(1)} %fusion.216), channel_id=1, source_target_pairs={{0,24},{1,25},{2,26},{3,27},{4,28},{5,29},{6,30},{7,31},{8,16},{9,... | collective-permute-start | bytes 6152 | tf_op jit(solution)/shard_map/ppermute | solution.py:110
  91.6 3.6 %collective-permute-start.13 = (f32[4,128]{1,0:T(4,128)S(1)}, f32[4,128]{1,0:T(4,128)S(1)}, u32[]{:S(2)}, u32[]{:S(2)}) collective-permute-start(f32[4,128]{1,0:T(4,128)S(1)} %fusion.215), channel_id=1, source_target_pairs={{0,32},{1,33},{2,34},{3,35},{4,36},{5,37},{6,38},{7,39},{8,40},{9,... | collective-permute-start | bytes 6152 | tf_op jit(solution)/shard_map/ppermute | solution.py:110
  96.3 4.8 %collective-permute-start.14 = (f32[4,128]{1,0:T(4,128)S(1)}, f32[4,128]{1,0:T(4,128)S(1)}, u32[]{:S(2)}, u32[]{:S(2)}) collective-permute-start(f32[4,128]{1,0:T(4,128)S(1)} %fusion.214), channel_id=1, source_target_pairs={{0,96},{1,97},{2,98},{3,99},{4,100},{5,101},{6,102},{7,103},{8,104... | collective-permute-start | bytes 6152 | tf_op jit(solution)/shard_map/ppermute | solution.py:110
  (47 other events, 146.2 us)

commit v9 on v8

--- a/solution.py
+++ b/solution.py
@@ -221,9 +221,8 @@
             break
         first_add = jnp.where(upper, total_add, got_add)
         second_add = jnp.where(upper, got_add, total_add)
-        offsets = batched([first_add, got_add], [second_map, own_before])
-        total_add = offsets[0] + second_add
-        before_add = jnp.where(upper, before_add, offsets[1] + before_add)
+        before_add = jnp.where(upper, before_add, dot(got_add, own_before) + before_add)
+        total_add = dot(first_add, second_map) + second_add
     arriving = before_add
     back_excl_maps = down_sweep_maps(late_b[0], backward_scale[0::2], smoother_gain.T)
     back_excl_adds = down_sweep_adds(

time: 106 us -> 114 us (1.075)
  matrix products: 31.7 us -> 37.9 us
  waiting for transfers between devices: 41.4 us -> 45 us
    dot_general x16 -> x28, matrix products: 4.51 us -> 13.5 us  [dot(): return jnp.dot(a, b, precision=HIGHEST)]
    ppermute x14, waiting for transfers between devices: 41.4 us -> 45 us  [exchanged(): return lax.ppermute(x, 'tm', [(i, partner(i, bit)) for i in range(count)])]
    slice x4, local copies, waits for them, and re-layouts: 0.66 us -> 3.98 us  [up_sweep_adds(): adds = step_right(step_adds[0::2], odd_scale, weights) + step_adds[1::2]]
    dot_general x17 -> x11, matrix products: 5.95 us -> 2.94 us  [batched(): jnp.einsum('kij,kjl->kil', jnp.stack(lhs), jnp.stack(rhs), precision=HIGH...]
    unnamed x130 -> x102, local copies, waits for them, and re-layouts: 3.74 us -> 2.22 us
  transfers between devices with their start and end apart: 15 -> 15, of which waited for: 12 -> 13; matrix products, arithmetic and copies ran while one was open for 21% -> 18% of each run, Pallas kernels for 0% -> 0%
where the time goes in v9:
time: 114 us; the launch traced here: 112 us
  waiting for transfers between devices  45 us (39%)
  matrix products  37.9 us (33%)
  local copies, waits for them, and re-layouts  13.6 us (12%)
  starting transfers between devices  11.4 us (10%)
  between operations  2.11 us (2%)
  other arithmetic  2.06 us (2%)
    ppermute x14, waiting for transfers between devices, exchanged(): return lax.ppermute(x, 'tm', [(i, partner(i, bit)) for i in range(count)])  45 us
    dot_general x28, matrix products, dot(): return jnp.dot(a, b, precision=HIGHEST)  13.5 us
    ppermute x1, starting transfers between devices, shifted(): return lax.ppermute(x, 'tm', pairs)  8.09 us
    slice x4, local copies, waits for them, and re-layouts, up_sweep_adds(): adds = step_right(step_adds[0::2], odd_scale, weights) + step_adds[1::2]  3.98 us
    dot_general x6, matrix products, step_right(): jnp.einsum('tbs,sr->tbr', x * scale[:, None, :], weights, precision=HIGHEST)  3.73 us
    ppermute x14, starting transfers between devices, exchanged(): return lax.ppermute(x, 'tm', [(i, partner(i, bit)) for i in range(count)])  3.33 us
    dot_general x11, matrix products, batched(): jnp.einsum('kij,kjl->kil', jnp.stack(lhs), jnp.stack(rhs), precision=HIGH...  2.94 us
    dot_general x4, matrix products, local(): jnp.einsum('dtij,dtjk->dtik', pairs[:, :, 0], pairs[:, :, 1], precision=H...  2.46 us
  transfers between devices with their start and end apart: 15, of which 13 were waited for; matrix products, arithmetic and copies ran while one was open for 18% of the time, Pallas kernels for 0%

profile of v9, /device:TPU:6, one launch (start us, length us, event | category | flops | bytes accessed | tf_op | source)
XLA Modules:
  0.0 112.1 jit_solution(889737703430376057)
XLA Ops:
  1.4 8.1 %collective-permute-start = (f32[1,128]{1,0:T(1,128)S(1)}, f32[1,128]{1,0:T(1,128)S(1)}, u32[]{:S(2)}, u32[]{:S(2)}) collective-permute-start(f32[1,128]{1,0:T(1,128)S(1)} %slice.350), channel_id=1, source_target_pairs={{1,0},{2,1},{3,2},{4,3},{5,4},{6,5},{7,6},{8,7},{9,8},{10,9},{11,1... | collective-permute-start | bytes 1544 | tf_op jit(solution)/shard_map/ppermute | solution.py:16
  11.7 1.0 convolution_bitcast_fusion.8
  12.8 1.2 %fusion.151 = f32[128,128]{1,0:T(8,128)S(1)} fusion(f32[64,128]{1,0:T(8,128)} %param.9, f32[64]{0:T(128)} %param.10), kind=kOutput, calls=%fused_computation.321 | convolution fusion | flops 12591104 | bytes 98560 | tf_op jit(solution)/shard_map/dot_general | solution.py:10
  14.0 1.1 convolution_subtract_fusion
  16.1 1.0 convolution_multiply_fusion
  17.8 1.0 broadcast_multiply_fusion
  18.8 1.1 %fusion.23 = f32[2,8,128,128]{3,2,1,0:T(8,128)S(1)} fusion(f32[1,8,2,128,128]{4,3,2,1,0:T(8,128)S(1)} %bitcast.632, f32[1,8,2,128,128]{4,3,2,1,0:T(8,128)S(1)} %bitcast.627), kind=kOutput, calls=%fused_computation.85 | convolution fusion | flops 403177472 | bytes 5242880 | tf_op jit(solution)/shard_map/dtij,dtjk->dtik/dot_general | solution.py:141
  20.0 1.0 fusion.238
  26.4 5.5 %collective-permute-done.2 = f32[260,128]{1,0:T(8,128)S(1)} collective-permute-done((f32[260,128]{1,0:T(8,128)S(1)}, f32[260,128]{1,0:T(8,128)S(1)}, u32[]{:S(2)}, u32[]{:S(2)}) %collective-permute-start.2) | collective-permute-done | bytes 133152 | tf_op jit(solution)/shard_map/ppermute | solution.py:110
  33.1 6.0 %collective-permute-done.3 = f32[260,128]{1,0:T(8,128)S(1)} collective-permute-done((f32[260,128]{1,0:T(8,128)S(1)}, f32[260,128]{1,0:T(8,128)S(1)}, u32[]{:S(2)}, u32[]{:S(2)}) %collective-permute-start.3) | collective-permute-done | bytes 133152 | tf_op jit(solution)/shard_map/ppermute | solution.py:110
  40.6 4.1 %collective-permute-done.4 = f32[260,128]{1,0:T(8,128)S(1)} collective-permute-done((f32[260,128]{1,0:T(8,128)S(1)}, f32[260,128]{1,0:T(8,128)S(1)}, u32[]{:S(2)}, u32[]{:S(2)}) %collective-permute-start.4) | collective-permute-done | bytes 133152 | tf_op jit(solution)/shard_map/ppermute | solution.py:110
  48.0 4.5 %collective-permute-done.5 = f32[260,128]{1,0:T(8,128)S(1)} collective-permute-done((f32[260,128]{1,0:T(8,128)S(1)}, f32[260,128]{1,0:T(8,128)S(1)}, u32[]{:S(2)}, u32[]{:S(2)}) %collective-permute-start.5) | collective-permute-done | bytes 133152 | tf_op jit(solution)/shard_map/ppermute | solution.py:110
  55.8 2.5 %collective-permute-done.6 = f32[260,128]{1,0:T(8,128)S(1)} collective-permute-done((f32[260,128]{1,0:T(8,128)S(1)}, f32[260,128]{1,0:T(8,128)S(1)}, u32[]{:S(2)}, u32[]{:S(2)}) %collective-permute-start.6) | collective-permute-done | bytes 133152 | tf_op jit(solution)/shard_map/ppermute | solution.py:110
  60.9 2.5 %collective-permute-done.7 = f32[4,128]{1,0:T(4,128)S(1)} collective-permute-done((f32[4,128]{1,0:T(4,128)S(1)}, f32[4,128]{1,0:T(4,128)S(1)}, u32[]{:S(2)}, u32[]{:S(2)}) %collective-permute-start.7) | collective-permute-done | bytes 2080 | tf_op jit(solution)/shard_map/ppermute | solution.py:110
  63.5 1.2 %fusion.242 = f32[32,128,4]{1,2,0:T(4,128)S(1)} fusion(f32[32,128,128]{2,1,0:T(8,128)S(1)} %bitcast.641, f32[4,128,1]{1,0,2:T(4,128)S(1)} %fusion.20), kind=kOutput, calls=%fused_computation.444 | convolution fusion | flops 25165824 | bytes 2164736 | tf_op jit(solution)/shard_map/bs,tsr->tbr/dot_general | solution.py:197
  66.8 1.4 %slice.435 = f32[16,4,128]{2,0,1:T(8,128)} reverse(f32[16,4,128]{2,0,1:T(8,128)} %slice.434), dimensions={0} | reverse | bytes 65536 | tf_op jit(solution)/shard_map/slice | solution.py:61
  68.2 1.4 %slice.433 = f32[16,4,128]{2,0,1:T(8,128)} reverse(f32[16,4,128]{2,0,1:T(8,128)} %slice.432), dimensions={0} | reverse | bytes 65536 | tf_op jit(solution)/shard_map/slice | solution.py:61
  69.5 1.0 convolution_add_fusion.2
  71.5 1.1 %convolution_add_fusion.14 = f32[2,4,128]{2,1,0:T(4,128)S(1)} fusion(f32[2,2,128,128]{3,2,1,0:T(8,128)} %bitcast.666, f32[2,2,4,128]{3,2,1,0:T(4,128)S(1)} %bitcast.695), kind=kOutput, calls=%fused_computation.37 | convolution fusion | flops 1573888 | bytes 143360 | tf_op jit(solution)/shard_map/tbj,tjk->tbk/dot_general | solution.py:67
  77.1 1.6 %convolution_add_fusion.28 = f32[4,128]{1,0:T(4,128)} fusion(f32[260,128]{1,0:T(8,128)} %copy-done.28, pred[]{:T(512)S(6)} %ne.28, f32[4,128]{1,0:T(4,128)S(1)} %collective-permute-done.8, f32[4,128]{1,0:T(4,128)S(1)} %convolution_add_fusion.29, f32[2,128,128]{2,1,0:T(8,128)S(1)} %copy-done.3), kind=kOutput, calls=%fused_computation.59 | convolution fusion | flops 804352 | bytes 142848 | tf_op jit(solution)/shard_map/dot_general | solution.py:10
  80.4 1.0 convolution_bitcast_fusion
  82.7 1.1 convolution_add_fusion.26
  84.6 3.9 %collective-permute-done.10 = f32[4,128]{1,0:T(4,128)S(1)} collective-permute-done((f32[4,128]{1,0:T(4,128)S(1)}, f32[4,128]{1,0:T(4,128)S(1)}, u32[]{:S(2)}, u32[]{:S(2)}) %collective-permute-start.10) | collective-permute-done | bytes 2080 | tf_op jit(solution)/shard_map/ppermute | solution.py:110
  88.5 1.0 convolution_add_fusion.24
  89.9 3.4 %collective-permute-done.11 = f32[4,128]{1,0:T(4,128)S(1)} collective-permute-done((f32[4,128]{1,0:T(4,128)S(1)}, f32[4,128]{1,0:T(4,128)S(1)}, u32[]{:S(2)}, u32[]{:S(2)}) %collective-permute-start.11) | collective-permute-done | bytes 2080 | tf_op jit(solution)/shard_map/ppermute | solution.py:110
  93.4 1.0 convolution_add_fusion.22
  95.1 4.2 %collective-permute-done.12 = f32[4,128]{1,0:T(4,128)S(1)} collective-permute-done((f32[4,128]{1,0:T(4,128)S(1)}, f32[4,128]{1,0:T(4,128)S(1)}, u32[]{:S(2)}, u32[]{:S(2)}) %collective-permute-start.12) | collective-permute-done | bytes 2080 | tf_op jit(solution)/shard_map/ppermute | solution.py:110
  99.2 1.0 convolution_add_fusion.20
  100.4 3.4 %collective-permute-done.13 = f32[4,128]{1,0:T(4,128)S(1)} collective-permute-done((f32[4,128]{1,0:T(4,128)S(1)}, f32[4,128]{1,0:T(4,128)S(1)}, u32[]{:S(2)}, u32[]{:S(2)}) %collective-permute-start.13) | collective-permute-done | bytes 2080 | tf_op jit(solution)/shard_map/ppermute | solution.py:110
  103.9 1.0 convolution_add_fusion.18
  105.8 3.9 %collective-permute-done.14 = f32[4,128]{1,0:T(4,128)S(1)} collective-permute-done((f32[4,128]{1,0:T(4,128)S(1)}, f32[4,128]{1,0:T(4,128)S(1)}, u32[]{:S(2)}, u32[]{:S(2)}) %collective-permute-start.14) | collective-permute-done | bytes 2080 | tf_op jit(solution)/shard_map/ppermute | solution.py:110
  109.9 1.2 %fusion.243 = f32[32,128,4]{1,2,0:T(4,128)S(1)} fusion(f32[32,128,128]{2,1,0:T(8,128)S(1)} %bitcast.640, f32[4,128,1]{1,0,2:T(4,128)S(1)} %fusion.8), kind=kOutput, calls=%fused_computation.445 | convolution fusion | flops 25165824 | bytes 2164736 | tf_op jit(solution)/shard_map/bs,tsr->tbr/dot_general | solution.py:232
  (275 shorter events, 35.4 us)
Async XLA Ops:
  0.6 11.0 %copy-start = (f32[32,4,64]{2,1,0:T(4,128)S(1)}, f32[32,4,64]{2,1,0:T(4,128)}, u32[]{:S(2)}) copy-start(f32[32,4,64]{2,1,0:T(4,128)} %param.6) | copy-start | bytes 98308
  0.6 17.0 %copy-start.1 = (f32[128,128]{1,0:T(8,128)S(1)}, f32[128,128]{1,0:T(8,128)}, u32[]{:S(2)}) copy-start(f32[128,128]{1,0:T(8,128)} %param.11) | copy-start | bytes 196612
  1.4 16.3 %collective-permute-start = (f32[1,128]{1,0:T(1,128)S(1)}, f32[1,128]{1,0:T(1,128)S(1)}, u32[]{:S(2)}, u32[]{:S(2)}) collective-permute-start(f32[1,128]{1,0:T(1,128)S(1)} %slice.350), channel_id=1, source_target_pairs={{1,0},{2,1},{3,2},{4,3},{5,4},{6,5},{7,6},{8,7},{9,8},{10,9},{11,1... | collective-permute-start | bytes 1544 | tf_op jit(solution)/shard_map/ppermute | solution.py:16
  10.2 8.6 %copy-start.43 = (f32[16,128]{1,0:T(8,128)}, f32[16,128]{1,0:T(8,128)S(1)}, u32[]{:S(2)}) copy-start(f32[16,128]{1,0:T(8,128)S(1)} %slice.347) | copy-start | bytes 24580
  12.8 20.3 %copy-start.18 = (f32[1,1,128,128]{3,2,1,0:T(8,128)}, f32[1,1,128,128]{3,2,1,0:T(8,128)S(1)}, u32[]{:S(2)}) copy-start(f32[1,1,128,128]{3,2,1,0:T(8,128)S(1)} %fusion.147) | copy-start | bytes 196612
  23.7 8.5 %copy-start.2 = (f32[2,128,128]{2,1,0:T(8,128)}, f32[2,128,128]{2,1,0:T(8,128)S(1)}, u32[]{:S(2)}) copy-start(f32[2,128,128]{2,1,0:T(8,128)S(1)} %fusion.40) | copy-start | bytes 393220
  23.9 1.4 %collective-permute-start.1 = (f32[260,128]{1,0:T(8,128)S(1)}, f32[260,128]{1,0:T(8,128)S(1)}, u32[]{:S(2)}, u32[]{:S(2)}) collective-permute-start(f32[260,128]{1,0:T(8,128)S(1)} %pad_maximum_fusion.11), channel_id=1, source_target_pairs={{0,1},{1,0},{2,3},{3,2},{4,5},{5,4},{6,7},{7,6},{8,9},{9,8},{10,11... | collective-permute-start | bytes 399368 | tf_op jit(solution)/shard_map/ppermute | solution.py:110
  26.2 5.7 %collective-permute-start.2 = (f32[260,128]{1,0:T(8,128)S(1)}, f32[260,128]{1,0:T(8,128)S(1)}, u32[]{:S(2)}, u32[]{:S(2)}) collective-permute-start(f32[260,128]{1,0:T(8,128)S(1)} %pad_maximum_fusion.12), channel_id=1, source_target_pairs={{0,2},{1,3},{2,0},{3,1},{4,6},{5,7},{6,4},{7,5},{8,10},{9,11},{10,... | collective-permute-start | bytes 399368 | tf_op jit(solution)/shard_map/ppermute | solution.py:110
  32.8 6.3 %collective-permute-start.3 = (f32[260,128]{1,0:T(8,128)S(1)}, f32[260,128]{1,0:T(8,128)S(1)}, u32[]{:S(2)}, u32[]{:S(2)}) collective-permute-start(f32[260,128]{1,0:T(8,128)S(1)} %pad_maximum_fusion.13), channel_id=1, source_target_pairs={{0,6},{1,7},{2,4},{3,5},{4,2},{5,3},{6,0},{7,1},{8,14},{9,15},{10,... | collective-permute-start | bytes 399368 | tf_op jit(solution)/shard_map/ppermute | solution.py:110
  39.1 8.6 %copy-start.25 = (f32[260,128]{1,0:T(8,128)}, f32[260,128]{1,0:T(8,128)S(1)}, u32[]{:S(2)}) copy-start(f32[260,128]{1,0:T(8,128)S(1)} %collective-permute-done.3) | copy-start | bytes 399364
  39.6 5.1 %collective-permute-start.4 = (f32[260,128]{1,0:T(8,128)S(1)}, f32[260,128]{1,0:T(8,128)S(1)}, u32[]{:S(2)}, u32[]{:S(2)}) collective-permute-start(f32[260,128]{1,0:T(8,128)S(1)} %pad_maximum_fusion.14), channel_id=1, source_target_pairs={{0,8},{1,9},{2,10},{3,11},{4,12},{5,13},{6,14},{7,15},{8,0},{9,1},... | collective-permute-start | bytes 399368 | tf_op jit(solution)/shard_map/ppermute | solution.py:110
  46.2 6.3 %collective-permute-start.5 = (f32[260,128]{1,0:T(8,128)S(1)}, f32[260,128]{1,0:T(8,128)S(1)}, u32[]{:S(2)}, u32[]{:S(2)}) collective-permute-start(f32[260,128]{1,0:T(8,128)S(1)} %pad_maximum_fusion.15), channel_id=1, source_target_pairs={{0,24},{1,25},{2,26},{3,27},{4,28},{5,29},{6,30},{7,31},{8,16},{9,... | collective-permute-start | bytes 399368 | tf_op jit(solution)/shard_map/ppermute | solution.py:110
  53.1 5.3 %collective-permute-start.6 = (f32[260,128]{1,0:T(8,128)S(1)}, f32[260,128]{1,0:T(8,128)S(1)}, u32[]{:S(2)}, u32[]{:S(2)}) collective-permute-start(f32[260,128]{1,0:T(8,128)S(1)} %pad_maximum_fusion.16), channel_id=1, source_target_pairs={{0,32},{1,33},{2,34},{3,35},{4,36},{5,37},{6,38},{7,39},{8,40},{9,... | collective-permute-start | bytes 399368 | tf_op jit(solution)/shard_map/ppermute | solution.py:110
  58.5 4.8 %collective-permute-start.7 = (f32[4,128]{1,0:T(4,128)S(1)}, f32[4,128]{1,0:T(4,128)S(1)}, u32[]{:S(2)}, u32[]{:S(2)}) collective-permute-start(f32[4,128]{1,0:T(4,128)S(1)} %convolution_add_fusion.36), channel_id=1, source_target_pairs={{0,96},{1,97},{2,98},{3,99},{4,100},{5,101},{6,102},{7,103},{8,104... | collective-permute-start | bytes 6152 | tf_op jit(solution)/shard_map/ppermute | solution.py:110
  60.8 10.3 %copy-start.12 = (f32[1,8,128,128]{3,2,1,0:T(8,128)S(1)}, f32[1,8,128,128]{3,2,1,0:T(8,128)}, u32[]{:S(2)}) copy-start(f32[1,8,128,128]{3,2,1,0:T(8,128)} %get-tuple-element.72) | copy-start | bytes 1572868
  63.5 10.7 %copy-start.31 = (f32[2,128,128]{2,1,0:T(8,128)S(1)}, f32[2,128,128]{2,1,0:T(8,128)}, u32[]{:S(2)}) copy-start(f32[2,128,128]{2,1,0:T(8,128)} %get-tuple-element.54) | copy-start | bytes 393220
  63.5 10.7 %copy-start.19 = (f32[1,1,128,128]{3,2,1,0:T(8,128)S(1)}, f32[1,1,128,128]{3,2,1,0:T(8,128)}, u32[]{:S(2)}) copy-start(f32[1,1,128,128]{3,2,1,0:T(8,128)} %copy-done.18) | copy-start | bytes 196612
  63.5 10.7 %copy-start.15 = (f32[4,128,128]{2,1,0:T(8,128)S(1)}, f32[4,128,128]{2,1,0:T(8,128)}, u32[]{:S(2)}) copy-start(f32[4,128,128]{2,1,0:T(8,128)} %get-tuple-element.55) | copy-start | bytes 786436
  65.6 10.3 %copy-start.16 = (f32[32,4,128]{2,0,1:T(8,128)}, f32[32,4,128]{2,0,1:T(8,128)S(1)}, u32[]{:S(2)}) copy-start(f32[32,4,128]{2,0,1:T(8,128)S(1)} %convolution_subtract_fusion.1) | copy-start | bytes 196612
  72.8 1.4 %collective-permute-start.8 = (f32[4,128]{1,0:T(4,128)S(1)}, f32[4,128]{1,0:T(4,128)S(1)}, u32[]{:S(2)}, u32[]{:S(2)}) collective-permute-start(f32[4,128]{1,0:T(4,128)S(1)} %convolution_add_fusion.29), channel_id=1, source_target_pairs={{0,1},{1,0},{2,3},{3,2},{4,5},{5,4},{6,7},{7,6},{8,9},{9,8},{10,11... | collective-permute-start | bytes 6152 | tf_op jit(solution)/shard_map/ppermute | solution.py:110
  78.8 3.9 %collective-permute-start.9 = (f32[4,128]{1,0:T(4,128)}, f32[4,128]{1,0:T(4,128)}, u32[]{:S(2)}, u32[]{:S(2)}) collective-permute-start(f32[4,128]{1,0:T(4,128)} %convolution_add_fusion.28), channel_id=1, source_target_pairs={{0,2},{1,3},{2,0},{3,1},{4,6},{5,7},{6,4},{7,5},{8,10},{9,11},{10,... | collective-permute-start | bytes 6152 | tf_op jit(solution)/shard_map/ppermute | solution.py:110
  82.0 11.4 %copy-start.7 = (f32[2,128,128]{2,1,0:T(8,128)S(1)}, f32[2,128,128]{2,1,0:T(8,128)}, u32[]{:S(2)}) copy-start(f32[2,128,128]{2,1,0:T(8,128)} %copy-done.6) | copy-start | bytes 393220
  82.0 12.9 %copy-start.9 = (f32[2,128,128]{2,1,0:T(8,128)S(1)}, f32[2,128,128]{2,1,0:T(8,128)}, u32[]{:S(2)}) copy-start(f32[2,128,128]{2,1,0:T(8,128)} %copy-done.8) | copy-start | bytes 393220
  82.0 17.2 %copy-start.11 = (f32[2,128,128]{2,1,0:T(8,128)S(1)}, f32[2,128,128]{2,1,0:T(8,128)}, u32[]{:S(2)}) copy-start(f32[2,128,128]{2,1,0:T(8,128)} %copy-done.10) | copy-start | bytes 393220
  82.0 21.9 %copy-start.14 = (f32[2,128,128]{2,1,0:T(8,128)S(1)}, f32[2,128,128]{2,1,0:T(8,128)}, u32[]{:S(2)}) copy-start(f32[2,128,128]{2,1,0:T(8,128)} %copy-done.13) | copy-start | bytes 393220
  82.0 27.7 %copy-start.30 = (f32[2,128,128]{2,1,0:T(8,128)S(1)}, f32[2,128,128]{2,1,0:T(8,128)}, u32[]{:S(2)}) copy-start(f32[2,128,128]{2,1,0:T(8,128)} %copy-done.29) | copy-start | bytes 393220
  82.2 28.9 %copy-start.17 = (f32[32,4,128]{2,0,1:T(8,128)S(1)}, f32[32,4,128]{2,0,1:T(8,128)}, u32[]{:S(2)}) copy-start(f32[32,4,128]{2,0,1:T(8,128)} %copy-done.16) | copy-start | bytes 196612
  83.7 4.8 %collective-permute-start.10 = (f32[4,128]{1,0:T(4,128)S(1)}, f32[4,128]{1,0:T(4,128)S(1)}, u32[]{:S(2)}, u32[]{:S(2)}) collective-permute-start(f32[4,128]{1,0:T(4,128)S(1)} %convolution_add_fusion.26), channel_id=1, source_target_pairs={{0,6},{1,7},{2,4},{3,5},{4,2},{5,3},{6,0},{7,1},{8,14},{9,15},{10,... | collective-permute-start | bytes 6152 | tf_op jit(solution)/shard_map/ppermute | solution.py:110
  89.6 3.8 %collective-permute-start.11 = (f32[4,128]{1,0:T(4,128)S(1)}, f32[4,128]{1,0:T(4,128)S(1)}, u32[]{:S(2)}, u32[]{:S(2)}) collective-permute-start(f32[4,128]{1,0:T(4,128)S(1)} %convolution_add_fusion.24), channel_id=1, source_target_pairs={{0,8},{1,9},{2,10},{3,11},{4,12},{5,13},{6,14},{7,15},{8,0},{9,1},... | collective-permute-start | bytes 6152 | tf_op jit(solution)/shard_map/ppermute | solution.py:110
  94.4 4.8 %collective-permute-start.12 = (f32[4,128]{1,0:T(4,128)S(1)}, f32[4,128]{1,0:T(4,128)S(1)}, u32[]{:S(2)}, u32[]{:S(2)}) collective-permute-start(f32[4,128]{1,0:T(4,128)S(1)} %convolution_add_fusion.22), channel_id=1, source_target_pairs={{0,24},{1,25},{2,26},{3,27},{4,28},{5,29},{6,30},{7,31},{8,16},{9,... | collective-permute-start | bytes 6152 | tf_op jit(solution)/shard_map/ppermute | solution.py:110
  100.3 3.6 %collective-permute-start.13 = (f32[4,128]{1,0:T(4,128)S(1)}, f32[4,128]{1,0:T(4,128)S(1)}, u32[]{:S(2)}, u32[]{:S(2)}) collective-permute-start(f32[4,128]{1,0:T(4,128)S(1)} %convolution_add_fusion.20), channel_id=1, source_target_pairs={{0,32},{1,33},{2,34},{3,35},{4,36},{5,37},{6,38},{7,39},{8,40},{9,... | collective-permute-start | bytes 6152 | tf_op jit(solution)/shard_map/ppermute | solution.py:110
  104.9 4.8 %collective-permute-start.14 = (f32[4,128]{1,0:T(4,128)S(1)}, f32[4,128]{1,0:T(4,128)S(1)}, u32[]{:S(2)}, u32[]{:S(2)}) collective-permute-start(f32[4,128]{1,0:T(4,128)S(1)} %convolution_add_fusion.18), channel_id=1, source_target_pairs={{0,96},{1,97},{2,98},{3,99},{4,100},{5,101},{6,102},{7,103},{8,104... | collective-permute-start | bytes 6152 | tf_op jit(solution)/shard_map/ppermute | solution.py:110
  (33 other events, 128.4 us)

commit v10 on v8

--- a/solution.py
+++ b/solution.py
@@ -178,10 +178,10 @@
         totals = batched([first_map, back_first], [second_map, back_second])
         total_add = dot(first_add, second_map) + second_add
         spans = batched([got_map, got_back], [before_map, back_before])
-        if 1 <= k <= len(sweep):
-            (state, level), spans = lax.optimization_barrier(((state, sweep[k - 1]), spans))
+        if k < len(sweep):
+            (state, level), spans = lax.optimization_barrier(((state, sweep[k]), spans))
             state = down_level(state, *level)
-        elif k == len(sweep) + 1:
+        elif k == len(sweep):
             state, spans = lax.optimization_barrier((state, spans))
             state = down_steps(state, forward_adds, decay[0::2], closed_rows)
         before_add = jnp.where(upper, dot(got_add, before_map) + before_add, before_add)
@@ -189,9 +189,9 @@
         before_map = jnp.where(upper, spans[0], before_map)
         back_before = jnp.where(upper, back_before, spans[1])
 
-    for level in sweep[max(0, len(rounds) - 2):]:
+    for level in sweep[max(0, len(rounds) - 1):]:
         state = down_level(state, *level)
-    if len(sweep) + 1 > len(rounds) - 2:
+    if len(sweep) > len(rounds) - 2:
         state = down_steps(state, forward_adds, decay[0::2], closed_rows)
     excl_maps, excl_adds = state
     previous = jnp.einsum("bs,tsr->tbr", entering, excl_maps, precision=HIGHEST) + excl_adds

time: 106 us -> 104 us (0.981); the launches traced: 104 us -> 103 us
  starting transfers between devices: 12.4 us -> 11 us
    ppermute x14, starting transfers between devices: 4.27 us -> 2.88 us  [exchanged(): return lax.ppermute(x, 'tm', [(i, partner(i, bit)) for i in range(count)])]
    unnamed x130 -> x126, local copies, waits for them, and re-layouts: 3.74 us -> 3.73 us
where the time goes in v10:
time: 104 us; the launch traced here: 103 us
  waiting for transfers between devices  42.4 us (41%)
  matrix products  31.7 us (30%)
  local copies, waits for them, and re-layouts  13.6 us (13%)
  starting transfers between devices  11 us (11%)
  between operations  2.36 us (2%)
  other arithmetic  2.1 us (2%)
    ppermute x14, waiting for transfers between devices, exchanged(): return lax.ppermute(x, 'tm', [(i, partner(i, bit)) for i in range(count)])  42.4 us
    ppermute x1, starting transfers between devices, shifted(): return lax.ppermute(x, 'tm', pairs)  8.09 us
    dot_general x17, matrix products, batched(): jnp.einsum('kij,kjl->kil', jnp.stack(lhs), jnp.stack(rhs), precision=HIGH...  5.97 us
    dot_general x16, matrix products, dot(): return jnp.dot(a, b, precision=HIGHEST)  4.5 us
    dot_general x6, matrix products, step_right(): jnp.einsum('tbs,sr->tbr', x * scale[:, None, :], weights, precision=HIGHEST)  4.42 us
    unnamed x126, local copies, waits for them, and re-layouts  3.73 us
    ppermute x14, starting transfers between devices, exchanged(): return lax.ppermute(x, 'tm', [(i, partner(i, bit)) for i in range(count)])  2.88 us
    dot_general x4, matrix products, local(): jnp.einsum('dtij,dtjk->dtik', pairs[:, :, 0], pairs[:, :, 1], precision=H...  2.46 us
  transfers between devices with their start and end apart: 15, of which 12 were waited for; matrix products, arithmetic and copies ran while one was open for 21% of the time, Pallas kernels for 0%

profile of v10, /device:TPU:6, one launch (start us, length us, event | category | flops | bytes accessed | tf_op | source)
XLA Modules:
  0.0 103.2 jit_solution(16375190712210252999)
XLA Ops:
  1.4 8.1 %collective-permute-start = (f32[1,128]{1,0:T(1,128)S(1)}, f32[1,128]{1,0:T(1,128)S(1)}, u32[]{:S(2)}, u32[]{:S(2)}) collective-permute-start(f32[1,128]{1,0:T(1,128)S(1)} %slice.386), channel_id=1, source_target_pairs={{1,0},{2,1},{3,2},{4,3},{5,4},{6,5},{7,6},{8,7},{9,8},{10,9},{11,1... | collective-permute-start | bytes 1544 | tf_op jit(solution)/shard_map/ppermute | solution.py:16
  11.7 1.0 convolution_bitcast_fusion.8
  12.8 1.2 %fusion.160 = f32[128,128]{1,0:T(8,128)S(1)} fusion(f32[64,128]{1,0:T(8,128)} %param.9, f32[64]{0:T(128)} %param.10), kind=kOutput, calls=%fused_computation.325 | convolution fusion | flops 12591104 | bytes 98560 | tf_op jit(solution)/shard_map/dot_general | solution.py:10
  14.0 1.1 %convolution_subtract_fusion = f32[128,128]{1,0:T(8,128)S(1)} fusion(f32[128,128]{1,0:T(8,128)} %param.8, f32[128,128]{1,0:T(8,128)S(1)} %fusion.160), kind=kOutput, calls=%fused_computation.13 | convolution fusion | flops 25182208 | bytes 196608 | tf_op jit(solution)/shard_map/dot_general | solution.py:10
  15.5 1.0 convolution_multiply_fusion
  17.3 1.0 broadcast_multiply_fusion
  18.3 1.1 %fusion.18 = f32[2,8,128,128]{3,2,1,0:T(8,128)S(1)} fusion(f32[1,8,2,128,128]{4,3,2,1,0:T(8,128)S(1)} %bitcast.683, f32[1,8,2,128,128]{4,3,2,1,0:T(8,128)S(1)} %bitcast.678), kind=kOutput, calls=%fused_computation.68 | convolution fusion | flops 403177472 | bytes 5242880 | tf_op jit(solution)/shard_map/dtij,dtjk->dtik/dot_general | solution.py:141
  19.5 1.2 %fusion.264 = (f32[1,8,128,128]{3,2,1,0:T(8,128)}, f32[8,128,128]{2,1,0:T(8,128)}, f32[8,128,128]{2,1,0:T(8,128)S(1)}) fusion(f32[2,8,128,128]{3,2,1,0:T(8,128)S(1)} %fusion.18), kind=kLoop, calls=%fused_computation.484 | loop fusion | bytes 2621440 | tf_op jit(solution)/shard_map/slice | solution.py:145
  21.6 0.9 fusion.265
  26.2 5.1 %collective-permute-done.2 = f32[260,128]{1,0:T(8,128)S(1)} collective-permute-done((f32[260,128]{1,0:T(8,128)S(1)}, f32[260,128]{1,0:T(8,128)S(1)}, u32[]{:S(2)}, u32[]{:S(2)}) %collective-permute-start.2) | collective-permute-done | bytes 133152 | tf_op jit(solution)/shard_map/ppermute | solution.py:110
  33.0 5.1 %collective-permute-done.3 = f32[260,128]{1,0:T(8,128)S(1)} collective-permute-done((f32[260,128]{1,0:T(8,128)S(1)}, f32[260,128]{1,0:T(8,128)S(1)}, u32[]{:S(2)}, u32[]{:S(2)}) %collective-permute-start.3) | collective-permute-done | bytes 133152 | tf_op jit(solution)/shard_map/ppermute | solution.py:110
  39.9 3.8 %collective-permute-done.4 = f32[260,128]{1,0:T(8,128)S(1)} collective-permute-done((f32[260,128]{1,0:T(8,128)S(1)}, f32[260,128]{1,0:T(8,128)S(1)}, u32[]{:S(2)}, u32[]{:S(2)}) %collective-permute-start.4) | collective-permute-done | bytes 133152 | tf_op jit(solution)/shard_map/ppermute | solution.py:110
  45.2 0.7 collective-permute-start.5
  47.7 4.0 %collective-permute-done.5 = f32[260,128]{1,0:T(8,128)S(1)} collective-permute-done((f32[260,128]{1,0:T(8,128)S(1)}, f32[260,128]{1,0:T(8,128)S(1)}, u32[]{:S(2)}, u32[]{:S(2)}) %collective-permute-start.5) | collective-permute-done | bytes 133152 | tf_op jit(solution)/shard_map/ppermute | solution.py:110
  53.5 1.0 convolution_bitcast_fusion.1
  55.1 2.2 %collective-permute-done.6 = f32[260,128]{1,0:T(8,128)S(1)} collective-permute-done((f32[260,128]{1,0:T(8,128)S(1)}, f32[260,128]{1,0:T(8,128)S(1)}, u32[]{:S(2)}, u32[]{:S(2)}) %collective-permute-start.6) | collective-permute-done | bytes 133152 | tf_op jit(solution)/shard_map/ppermute | solution.py:110
  58.6 3.7 %collective-permute-done.7 = f32[4,128]{1,0:T(4,128)S(1)} collective-permute-done((f32[4,128]{1,0:T(4,128)S(1)}, f32[4,128]{1,0:T(4,128)S(1)}, u32[]{:S(2)}, u32[]{:S(2)}) %collective-permute-start.7) | collective-permute-done | bytes 2080 | tf_op jit(solution)/shard_map/ppermute | solution.py:110
  62.5 1.2 %fusion.268 = f32[32,128,4]{1,2,0:T(4,128)S(1)} fusion(f32[32,128,128]{2,1,0:T(8,128)S(1)} %bitcast.691, f32[4,128,1]{1,0,2:T(4,128)S(1)} %fusion.15), kind=kOutput, calls=%fused_computation.488 | convolution fusion | flops 25165824 | bytes 2164736 | tf_op jit(solution)/shard_map/bs,tsr->tbr/dot_general | solution.py:197
  65.2 1.0 convolution_add_fusion.2
  68.9 0.8 slice.583
  70.0 0.9 fusion.5
  73.4 1.0 convolution_bitcast_fusion
  76.2 4.7 %collective-permute-done.10 = f32[4,128]{1,0:T(4,128)S(1)} collective-permute-done((f32[4,128]{1,0:T(4,128)S(1)}, f32[4,128]{1,0:T(4,128)S(1)}, u32[]{:S(2)}, u32[]{:S(2)}) %collective-permute-start.10) | collective-permute-done | bytes 2080 | tf_op jit(solution)/shard_map/ppermute | solution.py:110
  82.2 2.8 %collective-permute-done.11 = f32[4,128]{1,0:T(4,128)S(1)} collective-permute-done((f32[4,128]{1,0:T(4,128)S(1)}, f32[4,128]{1,0:T(4,128)S(1)}, u32[]{:S(2)}, u32[]{:S(2)}) %collective-permute-start.11) | collective-permute-done | bytes 2080 | tf_op jit(solution)/shard_map/ppermute | solution.py:110
  85.8 0.8 slice.505
  86.7 3.4 %collective-permute-done.12 = f32[4,128]{1,0:T(4,128)S(1)} collective-permute-done((f32[4,128]{1,0:T(4,128)S(1)}, f32[4,128]{1,0:T(4,128)S(1)}, u32[]{:S(2)}, u32[]{:S(2)}) %collective-permute-start.12) | collective-permute-done | bytes 2080 | tf_op jit(solution)/shard_map/ppermute | solution.py:110
  90.1 1.1 %fusion.37 = f32[2,4,128]{2,1,0:T(4,128)S(1)} fusion(f32[1,128,128]{2,1,0:T(8,128)} %copy-done.20, f32[1,128,128]{2,1,0:T(8,128)} %copy-done.34, f32[1,4,128]{2,1,0:T(4,128)S(1)} %bitcast.751, f32[1,4,128]{2,1,0:T(4,128)S(1)} %select_bitcast_fusion.17), kind=kOutput, calls=%fused_computation.128 | convolution fusion | flops 1606656 | bytes 139264 | tf_op jit(solution)/shard_map/kij,kjl->kil/dot_general | solution.py:114
  91.2 0.9 add_bitcast_fusion
  92.2 2.6 %collective-permute-done.13 = f32[4,128]{1,0:T(4,128)S(1)} collective-permute-done((f32[4,128]{1,0:T(4,128)S(1)}, f32[4,128]{1,0:T(4,128)S(1)}, u32[]{:S(2)}, u32[]{:S(2)}) %collective-permute-start.13) | collective-permute-done | bytes 2080 | tf_op jit(solution)/shard_map/ppermute | solution.py:110
  94.8 1.1 %fusion.35 = f32[2,4,128]{2,1,0:T(4,128)S(1)} fusion(f32[1,128,128]{2,1,0:T(8,128)} %copy-done.37, f32[1,128,128]{2,1,0:T(8,128)} %get-tuple-element.98, f32[1,4,128]{2,1,0:T(4,128)S(1)} %bitcast.753, f32[1,4,128]{2,1,0:T(4,128)S(1)} %select_bitcast_fusion.16), kind=kOutput, calls=%fused_computation.126 | convolution fusion | flops 1606656 | bytes 139264 | tf_op jit(solution)/shard_map/kij,kjl->kil/dot_general | solution.py:114
  96.3 4.4 %collective-permute-done.14 = f32[4,128]{1,0:T(4,128)S(1)} collective-permute-done((f32[4,128]{1,0:T(4,128)S(1)}, f32[4,128]{1,0:T(4,128)S(1)}, u32[]{:S(2)}, u32[]{:S(2)}) %collective-permute-start.14) | collective-permute-done | bytes 2080 | tf_op jit(solution)/shard_map/ppermute | solution.py:110
  101.0 1.2 %fusion.269 = f32[32,128,4]{1,2,0:T(4,128)S(1)} fusion(f32[32,128,128]{2,1,0:T(8,128)S(1)} %bitcast.692, f32[4,128,1]{1,0,2:T(4,128)S(1)} %fusion.8), kind=kOutput, calls=%fused_computation.489 | convolution fusion | flops 25165824 | bytes 2164736 | tf_op jit(solution)/shard_map/bs,tsr->tbr/dot_general | solution.py:233
  (305 shorter events, 30.7 us)
Async XLA Ops:
  0.6 11.0 %copy-start = (f32[32,4,64]{2,1,0:T(4,128)S(1)}, f32[32,4,64]{2,1,0:T(4,128)}, u32[]{:S(2)}) copy-start(f32[32,4,64]{2,1,0:T(4,128)} %param.6) | copy-start | bytes 98308
  0.6 16.4 %copy-start.1 = (f32[128,128]{1,0:T(8,128)S(1)}, f32[128,128]{1,0:T(8,128)}, u32[]{:S(2)}) copy-start(f32[128,128]{1,0:T(8,128)} %param.11) | copy-start | bytes 196612
  1.4 15.8 %collective-permute-start = (f32[1,128]{1,0:T(1,128)S(1)}, f32[1,128]{1,0:T(1,128)S(1)}, u32[]{:S(2)}, u32[]{:S(2)}) collective-permute-start(f32[1,128]{1,0:T(1,128)S(1)} %slice.386), channel_id=1, source_target_pairs={{1,0},{2,1},{3,2},{4,3},{5,4},{6,5},{7,6},{8,7},{9,8},{10,9},{11,1... | collective-permute-start | bytes 1544 | tf_op jit(solution)/shard_map/ppermute | solution.py:16
  12.8 13.4 %copy-start.14 = (f32[1,1,128,128]{3,2,1,0:T(8,128)}, f32[1,1,128,128]{3,2,1,0:T(8,128)S(1)}, u32[]{:S(2)}) copy-start(f32[1,1,128,128]{3,2,1,0:T(8,128)S(1)} %fusion.152) | copy-start | bytes 196612
  12.8 12.9 %copy-start.24 = (f32[1,128,128]{2,1,0:T(8,128)}, f32[1,128,128]{2,1,0:T(8,128)S(1)}, u32[]{:S(2)}) copy-start(f32[1,128,128]{2,1,0:T(8,128)S(1)} %fusion.153) | copy-start | bytes 196612
  23.6 1.4 %collective-permute-start.1 = (f32[260,128]{1,0:T(8,128)S(1)}, f32[260,128]{1,0:T(8,128)S(1)}, u32[]{:S(2)}, u32[]{:S(2)}) collective-permute-start(f32[260,128]{1,0:T(8,128)S(1)} %pad_maximum_fusion.23), channel_id=1, source_target_pairs={{0,1},{1,0},{2,3},{3,2},{4,5},{5,4},{6,7},{7,6},{8,9},{9,8},{10,11... | collective-permute-start | bytes 399368 | tf_op jit(solution)/shard_map/ppermute | solution.py:110
  25.6 5.7 %collective-permute-start.2 = (f32[260,128]{1,0:T(8,128)S(1)}, f32[260,128]{1,0:T(8,128)S(1)}, u32[]{:S(2)}, u32[]{:S(2)}) collective-permute-start(f32[260,128]{1,0:T(8,128)S(1)} %pad_maximum_fusion.24), channel_id=1, source_target_pairs={{0,2},{1,3},{2,0},{3,1},{4,6},{5,7},{6,4},{7,5},{8,10},{9,11},{10,... | collective-permute-start | bytes 399368 | tf_op jit(solution)/shard_map/ppermute | solution.py:110
  25.9 18.2 %copy-start.4 = (f32[2,128,128]{2,1,0:T(8,128)}, f32[2,128,128]{2,1,0:T(8,128)S(1)}, u32[]{:S(2)}) copy-start(f32[2,128,128]{2,1,0:T(8,128)S(1)} %fusion.45) | copy-start | bytes 393220
  31.8 6.3 %collective-permute-start.3 = (f32[260,128]{1,0:T(8,128)S(1)}, f32[260,128]{1,0:T(8,128)S(1)}, u32[]{:S(2)}, u32[]{:S(2)}) collective-permute-start(f32[260,128]{1,0:T(8,128)S(1)} %pad_maximum_fusion.25), channel_id=1, source_target_pairs={{0,6},{1,7},{2,4},{3,5},{4,2},{5,3},{6,0},{7,1},{8,14},{9,15},{10,... | collective-permute-start | bytes 399368 | tf_op jit(solution)/shard_map/ppermute | solution.py:110
  32.2 11.9 %copy-start.7 = (f32[2,128,128]{2,1,0:T(8,128)}, f32[2,128,128]{2,1,0:T(8,128)S(1)}, u32[]{:S(2)}) copy-start(f32[2,128,128]{2,1,0:T(8,128)S(1)} %fusion.42) | copy-start | bytes 393220
  38.6 5.1 %collective-permute-start.4 = (f32[260,128]{1,0:T(8,128)S(1)}, f32[260,128]{1,0:T(8,128)S(1)}, u32[]{:S(2)}, u32[]{:S(2)}) collective-permute-start(f32[260,128]{1,0:T(8,128)S(1)} %pad_maximum_fusion.26), channel_id=1, source_target_pairs={{0,8},{1,9},{2,10},{3,11},{4,12},{5,13},{6,14},{7,15},{8,0},{9,1},... | collective-permute-start | bytes 399368 | tf_op jit(solution)/shard_map/ppermute | solution.py:110
  44.1 10.4 %copy-start.20 = (f32[1,128,128]{2,1,0:T(8,128)}, f32[1,128,128]{2,1,0:T(8,128)S(1)}, u32[]{:S(2)}) copy-start(f32[1,128,128]{2,1,0:T(8,128)S(1)} %get-tuple-element.116) | copy-start | bytes 196612
  45.2 6.5 %collective-permute-start.5 = (f32[260,128]{1,0:T(8,128)S(1)}, f32[260,128]{1,0:T(8,128)S(1)}, u32[]{:S(2)}, u32[]{:S(2)}) collective-permute-start(f32[260,128]{1,0:T(8,128)S(1)} %pad_maximum_fusion.27), channel_id=1, source_target_pairs={{0,24},{1,25},{2,26},{3,27},{4,28},{5,29},{6,30},{7,31},{8,16},{9,... | collective-permute-start | bytes 399368 | tf_op jit(solution)/shard_map/ppermute | solution.py:110
  52.2 5.1 %collective-permute-start.6 = (f32[260,128]{1,0:T(8,128)S(1)}, f32[260,128]{1,0:T(8,128)S(1)}, u32[]{:S(2)}, u32[]{:S(2)}) collective-permute-start(f32[260,128]{1,0:T(8,128)S(1)} %pad_maximum_fusion.28), channel_id=1, source_target_pairs={{0,32},{1,33},{2,34},{3,35},{4,36},{5,37},{6,38},{7,39},{8,40},{9,... | collective-permute-start | bytes 399368 | tf_op jit(solution)/shard_map/ppermute | solution.py:110
  53.5 9.0 %copy-start.37 = (f32[1,128,128]{2,1,0:T(8,128)}, f32[1,128,128]{2,1,0:T(8,128)S(1)}, u32[]{:S(2)}) copy-start(f32[1,128,128]{2,1,0:T(8,128)S(1)} %get-tuple-element.112) | copy-start | bytes 196612
  54.9 8.7 %copy-start.36 = (f32[32,4,128]{2,0,1:T(8,128)S(1)}, f32[32,4,128]{2,0,1:T(8,128)}, u32[]{:S(2)}) copy-start(f32[32,4,128]{2,0,1:T(8,128)} %copy-done.35) | copy-start | bytes 196612
  55.0 8.7 %copy-start.47 = (f32[32,128]{1,0:T(8,128)S(1)}, f32[32,128]{1,0:T(8,128)}, u32[]{:S(2)}) copy-start(f32[32,128]{1,0:T(8,128)} %param.7) | copy-start | bytes 49156
  55.0 9.0 %copy-start.42 = (f32[128,128]{1,0:T(8,128)S(1)}, f32[128,128]{1,0:T(8,128)}, u32[]{:S(2)}) copy-start(f32[128,128]{1,0:T(8,128)} %param.8) | copy-start | bytes 196612
  57.5 4.8 %collective-permute-start.7 = (f32[4,128]{1,0:T(4,128)S(1)}, f32[4,128]{1,0:T(4,128)S(1)}, u32[]{:S(2)}, u32[]{:S(2)}) collective-permute-start(f32[4,128]{1,0:T(4,128)S(1)} %convolution_add_fusion.25), channel_id=1, source_target_pairs={{0,96},{1,97},{2,98},{3,99},{4,100},{5,101},{6,102},{7,103},{8,104... | collective-permute-start | bytes 6152 | tf_op jit(solution)/shard_map/ppermute | solution.py:110
  58.6 8.2 %copy-start.6 = (f32[1,8,128,128]{3,2,1,0:T(8,128)S(1)}, f32[1,8,128,128]{3,2,1,0:T(8,128)}, u32[]{:S(2)}) copy-start(f32[1,8,128,128]{3,2,1,0:T(8,128)} %get-tuple-element.70) | copy-start | bytes 1572868
  62.5 7.2 %copy-start.15 = (f32[1,1,128,128]{3,2,1,0:T(8,128)S(1)}, f32[1,1,128,128]{3,2,1,0:T(8,128)}, u32[]{:S(2)}) copy-start(f32[1,1,128,128]{3,2,1,0:T(8,128)} %copy-done.14) | copy-start | bytes 196612
  62.5 7.2 %copy-start.11 = (f32[4,128,128]{2,1,0:T(8,128)S(1)}, f32[4,128,128]{2,1,0:T(8,128)}, u32[]{:S(2)}) copy-start(f32[4,128,128]{2,1,0:T(8,128)} %get-tuple-element.55) | copy-start | bytes 786436
  67.5 1.3 %collective-permute-start.8 = (f32[4,128]{1,0:T(4,128)S(1)}, f32[4,128]{1,0:T(4,128)S(1)}, u32[]{:S(2)}, u32[]{:S(2)}) collective-permute-start(f32[4,128]{1,0:T(4,128)S(1)} %convolution_add_fusion.18), channel_id=1, source_target_pairs={{0,1},{1,0},{2,3},{3,2},{4,5},{5,4},{6,7},{7,6},{8,9},{9,8},{10,11... | collective-permute-start | bytes 6152 | tf_op jit(solution)/shard_map/ppermute | solution.py:110
  71.8 3.9 %collective-permute-start.9 = (f32[4,128]{1,0:T(4,128)S(1)}, f32[4,128]{1,0:T(4,128)S(1)}, u32[]{:S(2)}, u32[]{:S(2)}) collective-permute-start(f32[4,128]{1,0:T(4,128)S(1)} %fusion.218), channel_id=1, source_target_pairs={{0,2},{1,3},{2,0},{3,1},{4,6},{5,7},{6,4},{7,5},{8,10},{9,11},{10,... | collective-permute-start | bytes 6152 | tf_op jit(solution)/shard_map/ppermute | solution.py:110
  74.4 10.6 %copy-start.22 = (f32[1,128,128]{2,1,0:T(8,128)S(1)}, f32[1,128,128]{2,1,0:T(8,128)}, u32[]{:S(2)}) copy-start(f32[1,128,128]{2,1,0:T(8,128)} %copy-done.21) | copy-start | bytes 196612
  74.5 10.6 %copy-start.33 = (f32[1,128,128]{2,1,0:T(8,128)S(1)}, f32[1,128,128]{2,1,0:T(8,128)}, u32[]{:S(2)}) copy-start(f32[1,128,128]{2,1,0:T(8,128)} %copy-done.32) | copy-start | bytes 196612
  76.0 9.8 %copy-start.58 = (f32[2,4,128]{2,1,0:T(4,128)}, f32[2,4,128]{2,1,0:T(4,128)S(1)}, u32[]{:S(2)}) copy-start(f32[2,4,128]{2,1,0:T(4,128)S(1)} %fusion.43) | copy-start | bytes 12292
  76.0 4.9 %collective-permute-start.10 = (f32[4,128]{1,0:T(4,128)S(1)}, f32[4,128]{1,0:T(4,128)S(1)}, u32[]{:S(2)}, u32[]{:S(2)}) collective-permute-start(f32[4,128]{1,0:T(4,128)S(1)} %fusion.217), channel_id=1, source_target_pairs={{0,6},{1,7},{2,4},{3,5},{4,2},{5,3},{6,0},{7,1},{8,14},{9,15},{10,... | collective-permute-start | bytes 6152 | tf_op jit(solution)/shard_map/ppermute | solution.py:110
  81.1 3.9 %collective-permute-start.11 = (f32[4,128]{1,0:T(4,128)S(1)}, f32[4,128]{1,0:T(4,128)S(1)}, u32[]{:S(2)}, u32[]{:S(2)}) collective-permute-start(f32[4,128]{1,0:T(4,128)S(1)} %fusion.216), channel_id=1, source_target_pairs={{0,8},{1,9},{2,10},{3,11},{4,12},{5,13},{6,14},{7,15},{8,0},{9,1},... | collective-permute-start | bytes 6152 | tf_op jit(solution)/shard_map/ppermute | solution.py:110
  85.2 4.9 %collective-permute-start.12 = (f32[4,128]{1,0:T(4,128)S(1)}, f32[4,128]{1,0:T(4,128)S(1)}, u32[]{:S(2)}, u32[]{:S(2)}) collective-permute-start(f32[4,128]{1,0:T(4,128)S(1)} %fusion.215), channel_id=1, source_target_pairs={{0,24},{1,25},{2,26},{3,27},{4,28},{5,29},{6,30},{7,31},{8,16},{9,... | collective-permute-start | bytes 6152 | tf_op jit(solution)/shard_map/ppermute | solution.py:110
  91.2 3.6 %collective-permute-start.13 = (f32[4,128]{1,0:T(4,128)S(1)}, f32[4,128]{1,0:T(4,128)S(1)}, u32[]{:S(2)}, u32[]{:S(2)}) collective-permute-start(f32[4,128]{1,0:T(4,128)S(1)} %fusion.214), channel_id=1, source_target_pairs={{0,32},{1,33},{2,34},{3,35},{4,36},{5,37},{6,38},{7,39},{8,40},{9,... | collective-permute-start | bytes 6152 | tf_op jit(solution)/shard_map/ppermute | solution.py:110
  95.9 4.8 %collective-permute-start.14 = (f32[4,128]{1,0:T(4,128)S(1)}, f32[4,128]{1,0:T(4,128)S(1)}, u32[]{:S(2)}, u32[]{:S(2)}) collective-permute-start(f32[4,128]{1,0:T(4,128)S(1)} %fusion.213), channel_id=1, source_target_pairs={{0,96},{1,97},{2,98},{3,99},{4,100},{5,101},{6,102},{7,103},{8,104... | collective-permute-start | bytes 6152 | tf_op jit(solution)/shard_map/ppermute | solution.py:110
  (45 other events, 166.9 us)

commit v11 on v10

--- a/solution.py
+++ b/solution.py
@@ -214,7 +214,7 @@
         upper = (index & bit) != 0
         own_map, second_map, own_before = stored[k]
         got_add = exchanged(total_add, bit)
-        if k == 0:
+        if k == min(1, len(rounds) - 1):
             late_b, got_add = lax.optimization_barrier((late_b, got_add))
         if k == len(rounds) - 1:
             before_add = jnp.where(upper, before_add, dot(got_add, own_before) + before_add)

time: 104 us -> 108 us (1.038)
  local copies, waits for them, and re-layouts: 13.6 us -> 16.4 us
    slice x4, local copies, waits for them, and re-layouts: 0.66 us -> 3.96 us  [up_sweep_adds(): adds = step_right(step_adds[0::2], odd_scale, weights) + step_adds[1::2]]
    unnamed x126 -> x122, local copies, waits for them, and re-layouts: 3.73 us -> 3.19 us
  transfers between devices with their start and end apart: 15 -> 15, of which waited for: 12 -> 14; matrix products, arithmetic and copies ran while one was open for 21% -> 21% of each run, Pallas kernels for 0% -> 0%
where the time goes in v11:
time: 108 us; the launch traced here: 107 us
  waiting for transfers between devices  42.6 us (39%)
  matrix products  32.6 us (30%)
  local copies, waits for them, and re-layouts  16.4 us (15%)
  starting transfers between devices  10.9 us (10%)
  between operations  2.32 us (2%)
  other arithmetic  2.09 us (2%)
    ppermute x14, waiting for transfers between devices, exchanged(): return lax.ppermute(x, 'tm', [(i, partner(i, bit)) for i in range(count)])  42.6 us
    ppermute x1, starting transfers between devices, shifted(): return lax.ppermute(x, 'tm', pairs)  8.09 us
    dot_general x17, matrix products, batched(): jnp.einsum('kij,kjl->kil', jnp.stack(lhs), jnp.stack(rhs), precision=HIGH...  6.8 us
    dot_general x16, matrix products, dot(): return jnp.dot(a, b, precision=HIGHEST)  4.5 us
    dot_general x6, matrix products, step_right(): jnp.einsum('tbs,sr->tbr', x * scale[:, None, :], weights, precision=HIGHEST)  4.43 us
    slice x4, local copies, waits for them, and re-layouts, up_sweep_adds(): adds = step_right(step_adds[0::2], odd_scale, weights) + step_adds[1::2]  3.96 us
    unnamed x122, local copies, waits for them, and re-layouts  3.19 us
    ppermute x14, starting transfers between devices, exchanged(): return lax.ppermute(x, 'tm', [(i, partner(i, bit)) for i in range(count)])  2.85 us
  transfers between devices with their start and end apart: 15, of which 14 were waited for; matrix products, arithmetic and copies ran while one was open for 21% of the time, Pallas kernels for 0%

profile of v11, /device:TPU:6, one launch (start us, length us, event | category | flops | bytes accessed | tf_op | source)
XLA Modules:
  0.0 107.0 jit_solution(421715636209608326)
XLA Ops:
  1.4 8.1 %collective-permute-start = (f32[1,128]{1,0:T(1,128)S(1)}, f32[1,128]{1,0:T(1,128)S(1)}, u32[]{:S(2)}, u32[]{:S(2)}) collective-permute-start(f32[1,128]{1,0:T(1,128)S(1)} %slice.386), channel_id=1, source_target_pairs={{1,0},{2,1},{3,2},{4,3},{5,4},{6,5},{7,6},{8,7},{9,8},{10,9},{11,1... | collective-permute-start | bytes 1544 | tf_op jit(solution)/shard_map/ppermute | solution.py:16
  11.7 1.0 convolution_bitcast_fusion.8
  12.8 1.2 %fusion.160 = f32[128,128]{1,0:T(8,128)S(1)} fusion(f32[64,128]{1,0:T(8,128)} %param.9, f32[64]{0:T(128)} %param.10), kind=kOutput, calls=%fused_computation.325 | convolution fusion | flops 12591104 | bytes 98560 | tf_op jit(solution)/shard_map/dot_general | solution.py:10
  14.0 1.1 %convolution_subtract_fusion = f32[128,128]{1,0:T(8,128)S(1)} fusion(f32[128,128]{1,0:T(8,128)} %param.8, f32[128,128]{1,0:T(8,128)S(1)} %fusion.160), kind=kOutput, calls=%fused_computation.13 | convolution fusion | flops 25182208 | bytes 196608 | tf_op jit(solution)/shard_map/dot_general | solution.py:10
  15.5 1.0 convolution_multiply_fusion
  17.3 1.0 broadcast_multiply_fusion
  18.3 1.1 %fusion.18 = f32[2,8,128,128]{3,2,1,0:T(8,128)S(1)} fusion(f32[1,8,2,128,128]{4,3,2,1,0:T(8,128)S(1)} %bitcast.683, f32[1,8,2,128,128]{4,3,2,1,0:T(8,128)S(1)} %bitcast.678), kind=kOutput, calls=%fused_computation.68 | convolution fusion | flops 403177472 | bytes 5242880 | tf_op jit(solution)/shard_map/dtij,dtjk->dtik/dot_general | solution.py:141
  19.5 1.2 %fusion.264 = (f32[1,8,128,128]{3,2,1,0:T(8,128)}, f32[8,128,128]{2,1,0:T(8,128)}, f32[8,128,128]{2,1,0:T(8,128)S(1)}) fusion(f32[2,8,128,128]{3,2,1,0:T(8,128)S(1)} %fusion.18), kind=kLoop, calls=%fused_computation.484 | loop fusion | bytes 2621440 | tf_op jit(solution)/shard_map/slice | solution.py:145
  26.2 5.1 %collective-permute-done.2 = f32[260,128]{1,0:T(8,128)S(1)} collective-permute-done((f32[260,128]{1,0:T(8,128)S(1)}, f32[260,128]{1,0:T(8,128)S(1)}, u32[]{:S(2)}, u32[]{:S(2)}) %collective-permute-start.2) | collective-permute-done | bytes 133152 | tf_op jit(solution)/shard_map/ppermute | solution.py:110
  33.0 5.1 %collective-permute-done.3 = f32[260,128]{1,0:T(8,128)S(1)} collective-permute-done((f32[260,128]{1,0:T(8,128)S(1)}, f32[260,128]{1,0:T(8,128)S(1)}, u32[]{:S(2)}, u32[]{:S(2)}) %collective-permute-start.3) | collective-permute-done | bytes 133152 | tf_op jit(solution)/shard_map/ppermute | solution.py:110
  40.0 3.8 %collective-permute-done.4 = f32[260,128]{1,0:T(8,128)S(1)} collective-permute-done((f32[260,128]{1,0:T(8,128)S(1)}, f32[260,128]{1,0:T(8,128)S(1)}, u32[]{:S(2)}, u32[]{:S(2)}) %collective-permute-start.4) | collective-permute-done | bytes 133152 | tf_op jit(solution)/shard_map/ppermute | solution.py:110
  47.8 4.0 %collective-permute-done.5 = f32[260,128]{1,0:T(8,128)S(1)} collective-permute-done((f32[260,128]{1,0:T(8,128)S(1)}, f32[260,128]{1,0:T(8,128)S(1)}, u32[]{:S(2)}, u32[]{:S(2)}) %collective-permute-start.5) | collective-permute-done | bytes 133152 | tf_op jit(solution)/shard_map/ppermute | solution.py:110
  53.5 1.0 convolution_bitcast_fusion.1
  55.2 2.2 %collective-permute-done.6 = f32[260,128]{1,0:T(8,128)S(1)} collective-permute-done((f32[260,128]{1,0:T(8,128)S(1)}, f32[260,128]{1,0:T(8,128)S(1)}, u32[]{:S(2)}, u32[]{:S(2)}) %collective-permute-start.6) | collective-permute-done | bytes 133152 | tf_op jit(solution)/shard_map/ppermute | solution.py:110
  58.6 3.7 %collective-permute-done.7 = f32[4,128]{1,0:T(4,128)S(1)} collective-permute-done((f32[4,128]{1,0:T(4,128)S(1)}, f32[4,128]{1,0:T(4,128)S(1)}, u32[]{:S(2)}, u32[]{:S(2)}) %collective-permute-start.7) | collective-permute-done | bytes 2080 | tf_op jit(solution)/shard_map/ppermute | solution.py:110
  62.5 1.2 %fusion.268 = f32[32,128,4]{1,2,0:T(4,128)S(1)} fusion(f32[32,128,128]{2,1,0:T(8,128)S(1)} %bitcast.691, f32[4,128,1]{1,0,2:T(4,128)S(1)} %fusion.15), kind=kOutput, calls=%fused_computation.488 | convolution fusion | flops 25165824 | bytes 2164736 | tf_op jit(solution)/shard_map/bs,tsr->tbr/dot_general | solution.py:197
  65.8 1.4 %slice.471 = f32[16,4,128]{2,0,1:T(8,128)} reverse(f32[16,4,128]{2,0,1:T(8,128)} %slice.470), dimensions={0} | reverse | bytes 65536 | tf_op jit(solution)/shard_map/slice | solution.py:61
  67.2 1.4 %slice.469 = f32[16,4,128]{2,0,1:T(8,128)} reverse(f32[16,4,128]{2,0,1:T(8,128)} %slice.468), dimensions={0} | reverse | bytes 65536 | tf_op jit(solution)/shard_map/slice | solution.py:61
  68.5 1.0 convolution_add_fusion.2
  70.9 1.2 %collective-permute-done.8 = f32[4,128]{1,0:T(4,128)S(1)} collective-permute-done((f32[4,128]{1,0:T(4,128)S(1)}, f32[4,128]{1,0:T(4,128)S(1)}, u32[]{:S(2)}, u32[]{:S(2)}) %collective-permute-start.8) | collective-permute-done | bytes 2080 | tf_op jit(solution)/shard_map/ppermute | solution.py:110
  72.0 1.0 fusion.46
  74.5 2.3 %collective-permute-done.9 = f32[4,128]{1,0:T(4,128)S(1)} collective-permute-done((f32[4,128]{1,0:T(4,128)S(1)}, f32[4,128]{1,0:T(4,128)S(1)}, u32[]{:S(2)}, u32[]{:S(2)}) %collective-permute-start.9) | collective-permute-done | bytes 2080 | tf_op jit(solution)/shard_map/ppermute | solution.py:110
  81.4 1.0 convolution_bitcast_fusion
  83.5 1.2 %collective-permute-done.10 = f32[4,128]{1,0:T(4,128)S(1)} collective-permute-done((f32[4,128]{1,0:T(4,128)S(1)}, f32[4,128]{1,0:T(4,128)S(1)}, u32[]{:S(2)}, u32[]{:S(2)}) %collective-permute-start.10) | collective-permute-done | bytes 2080 | tf_op jit(solution)/shard_map/ppermute | solution.py:110
  85.7 3.0 %collective-permute-done.11 = f32[4,128]{1,0:T(4,128)S(1)} collective-permute-done((f32[4,128]{1,0:T(4,128)S(1)}, f32[4,128]{1,0:T(4,128)S(1)}, u32[]{:S(2)}, u32[]{:S(2)}) %collective-permute-start.11) | collective-permute-done | bytes 2080 | tf_op jit(solution)/shard_map/ppermute | solution.py:110
  90.4 3.4 %collective-permute-done.12 = f32[4,128]{1,0:T(4,128)S(1)} collective-permute-done((f32[4,128]{1,0:T(4,128)S(1)}, f32[4,128]{1,0:T(4,128)S(1)}, u32[]{:S(2)}, u32[]{:S(2)}) %collective-permute-start.12) | collective-permute-done | bytes 2080 | tf_op jit(solution)/shard_map/ppermute | solution.py:110
  93.9 1.1 %fusion.37 = f32[2,4,128]{2,1,0:T(4,128)S(1)} fusion(f32[1,128,128]{2,1,0:T(8,128)} %copy-done.19, f32[1,128,128]{2,1,0:T(8,128)} %copy-done.32, f32[1,4,128]{2,1,0:T(4,128)S(1)} %bitcast.750, f32[1,4,128]{2,1,0:T(4,128)S(1)} %select_bitcast_fusion.17), kind=kOutput, calls=%fused_computation.128 | convolution fusion | flops 1606656 | bytes 139264 | tf_op jit(solution)/shard_map/kij,kjl->kil/dot_general | solution.py:114
  95.0 0.9 add_bitcast_fusion
  96.0 2.6 %collective-permute-done.13 = f32[4,128]{1,0:T(4,128)S(1)} collective-permute-done((f32[4,128]{1,0:T(4,128)S(1)}, f32[4,128]{1,0:T(4,128)S(1)}, u32[]{:S(2)}, u32[]{:S(2)}) %collective-permute-start.13) | collective-permute-done | bytes 2080 | tf_op jit(solution)/shard_map/ppermute | solution.py:110
  98.6 1.1 %fusion.35 = f32[2,4,128]{2,1,0:T(4,128)S(1)} fusion(f32[1,128,128]{2,1,0:T(8,128)} %copy-done.35, f32[1,128,128]{2,1,0:T(8,128)} %get-tuple-element.98, f32[1,4,128]{2,1,0:T(4,128)S(1)} %bitcast.752, f32[1,4,128]{2,1,0:T(4,128)S(1)} %select_bitcast_fusion.16), kind=kOutput, calls=%fused_computation.126 | convolution fusion | flops 1606656 | bytes 139264 | tf_op jit(solution)/shard_map/kij,kjl->kil/dot_general | solution.py:114
  100.1 4.4 %collective-permute-done.14 = f32[4,128]{1,0:T(4,128)S(1)} collective-permute-done((f32[4,128]{1,0:T(4,128)S(1)}, f32[4,128]{1,0:T(4,128)S(1)}, u32[]{:S(2)}, u32[]{:S(2)}) %collective-permute-start.14) | collective-permute-done | bytes 2080 | tf_op jit(solution)/shard_map/ppermute | solution.py:110
  104.7 1.2 %fusion.269 = f32[32,128,4]{1,2,0:T(4,128)S(1)} fusion(f32[32,128,128]{2,1,0:T(8,128)S(1)} %bitcast.692, f32[4,128,1]{1,0,2:T(4,128)S(1)} %fusion.8), kind=kOutput, calls=%fused_computation.489 | convolution fusion | flops 25165824 | bytes 2164736 | tf_op jit(solution)/shard_map/bs,tsr->tbr/dot_general | solution.py:233
  (301 shorter events, 34.7 us)
Async XLA Ops:
  0.6 11.0 %copy-start = (f32[32,4,64]{2,1,0:T(4,128)S(1)}, f32[32,4,64]{2,1,0:T(4,128)}, u32[]{:S(2)}) copy-start(f32[32,4,64]{2,1,0:T(4,128)} %param.6) | copy-start | bytes 98308
  0.6 16.4 %copy-start.1 = (f32[128,128]{1,0:T(8,128)S(1)}, f32[128,128]{1,0:T(8,128)}, u32[]{:S(2)}) copy-start(f32[128,128]{1,0:T(8,128)} %param.11) | copy-start | bytes 196612
  1.4 15.8 %collective-permute-start = (f32[1,128]{1,0:T(1,128)S(1)}, f32[1,128]{1,0:T(1,128)S(1)}, u32[]{:S(2)}, u32[]{:S(2)}) collective-permute-start(f32[1,128]{1,0:T(1,128)S(1)} %slice.386), channel_id=1, source_target_pairs={{1,0},{2,1},{3,2},{4,3},{5,4},{6,5},{7,6},{8,7},{9,8},{10,9},{11,1... | collective-permute-start | bytes 1544 | tf_op jit(solution)/shard_map/ppermute | solution.py:16
  12.8 13.4 %copy-start.13 = (f32[1,1,128,128]{3,2,1,0:T(8,128)}, f32[1,1,128,128]{3,2,1,0:T(8,128)S(1)}, u32[]{:S(2)}) copy-start(f32[1,1,128,128]{3,2,1,0:T(8,128)S(1)} %fusion.152) | copy-start | bytes 196612
  12.8 12.9 %copy-start.23 = (f32[1,128,128]{2,1,0:T(8,128)}, f32[1,128,128]{2,1,0:T(8,128)S(1)}, u32[]{:S(2)}) copy-start(f32[1,128,128]{2,1,0:T(8,128)S(1)} %fusion.153) | copy-start | bytes 196612
  23.6 1.4 %collective-permute-start.1 = (f32[260,128]{1,0:T(8,128)S(1)}, f32[260,128]{1,0:T(8,128)S(1)}, u32[]{:S(2)}, u32[]{:S(2)}) collective-permute-start(f32[260,128]{1,0:T(8,128)S(1)} %pad_maximum_fusion.23), channel_id=1, source_target_pairs={{0,1},{1,0},{2,3},{3,2},{4,5},{5,4},{6,7},{7,6},{8,9},{9,8},{10,11... | collective-permute-start | bytes 399368 | tf_op jit(solution)/shard_map/ppermute | solution.py:110
  25.6 5.7 %collective-permute-start.2 = (f32[260,128]{1,0:T(8,128)S(1)}, f32[260,128]{1,0:T(8,128)S(1)}, u32[]{:S(2)}, u32[]{:S(2)}) collective-permute-start(f32[260,128]{1,0:T(8,128)S(1)} %pad_maximum_fusion.24), channel_id=1, source_target_pairs={{0,2},{1,3},{2,0},{3,1},{4,6},{5,7},{6,4},{7,5},{8,10},{9,11},{10,... | collective-permute-start | bytes 399368 | tf_op jit(solution)/shard_map/ppermute | solution.py:110
  26.0 18.1 %copy-start.3 = (f32[2,128,128]{2,1,0:T(8,128)}, f32[2,128,128]{2,1,0:T(8,128)S(1)}, u32[]{:S(2)}) copy-start(f32[2,128,128]{2,1,0:T(8,128)S(1)} %fusion.45) | copy-start | bytes 393220
  31.8 6.3 %collective-permute-start.3 = (f32[260,128]{1,0:T(8,128)S(1)}, f32[260,128]{1,0:T(8,128)S(1)}, u32[]{:S(2)}, u32[]{:S(2)}) collective-permute-start(f32[260,128]{1,0:T(8,128)S(1)} %pad_maximum_fusion.25), channel_id=1, source_target_pairs={{0,6},{1,7},{2,4},{3,5},{4,2},{5,3},{6,0},{7,1},{8,14},{9,15},{10,... | collective-permute-start | bytes 399368 | tf_op jit(solution)/shard_map/ppermute | solution.py:110
  32.2 11.9 %copy-start.6 = (f32[2,128,128]{2,1,0:T(8,128)}, f32[2,128,128]{2,1,0:T(8,128)S(1)}, u32[]{:S(2)}) copy-start(f32[2,128,128]{2,1,0:T(8,128)S(1)} %fusion.42) | copy-start | bytes 393220
  38.7 5.1 %collective-permute-start.4 = (f32[260,128]{1,0:T(8,128)S(1)}, f32[260,128]{1,0:T(8,128)S(1)}, u32[]{:S(2)}, u32[]{:S(2)}) collective-permute-start(f32[260,128]{1,0:T(8,128)S(1)} %pad_maximum_fusion.26), channel_id=1, source_target_pairs={{0,8},{1,9},{2,10},{3,11},{4,12},{5,13},{6,14},{7,15},{8,0},{9,1},... | collective-permute-start | bytes 399368 | tf_op jit(solution)/shard_map/ppermute | solution.py:110
  44.1 10.4 %copy-start.19 = (f32[1,128,128]{2,1,0:T(8,128)}, f32[1,128,128]{2,1,0:T(8,128)S(1)}, u32[]{:S(2)}) copy-start(f32[1,128,128]{2,1,0:T(8,128)S(1)} %get-tuple-element.116) | copy-start | bytes 196612
  45.2 6.5 %collective-permute-start.5 = (f32[260,128]{1,0:T(8,128)S(1)}, f32[260,128]{1,0:T(8,128)S(1)}, u32[]{:S(2)}, u32[]{:S(2)}) collective-permute-start(f32[260,128]{1,0:T(8,128)S(1)} %pad_maximum_fusion.27), channel_id=1, source_target_pairs={{0,24},{1,25},{2,26},{3,27},{4,28},{5,29},{6,30},{7,31},{8,16},{9,... | collective-permute-start | bytes 399368 | tf_op jit(solution)/shard_map/ppermute | solution.py:110
  52.3 5.1 %collective-permute-start.6 = (f32[260,128]{1,0:T(8,128)S(1)}, f32[260,128]{1,0:T(8,128)S(1)}, u32[]{:S(2)}, u32[]{:S(2)}) collective-permute-start(f32[260,128]{1,0:T(8,128)S(1)} %pad_maximum_fusion.28), channel_id=1, source_target_pairs={{0,32},{1,33},{2,34},{3,35},{4,36},{5,37},{6,38},{7,39},{8,40},{9,... | collective-permute-start | bytes 399368 | tf_op jit(solution)/shard_map/ppermute | solution.py:110
  53.5 9.0 %copy-start.35 = (f32[1,128,128]{2,1,0:T(8,128)}, f32[1,128,128]{2,1,0:T(8,128)S(1)}, u32[]{:S(2)}) copy-start(f32[1,128,128]{2,1,0:T(8,128)S(1)} %get-tuple-element.112) | copy-start | bytes 196612
  55.0 8.8 %copy-start.34 = (f32[32,4,128]{2,0,1:T(8,128)S(1)}, f32[32,4,128]{2,0,1:T(8,128)}, u32[]{:S(2)}) copy-start(f32[32,4,128]{2,0,1:T(8,128)} %copy-done.33) | copy-start | bytes 196612
  55.0 8.7 %copy-start.45 = (f32[32,128]{1,0:T(8,128)S(1)}, f32[32,128]{1,0:T(8,128)}, u32[]{:S(2)}) copy-start(f32[32,128]{1,0:T(8,128)} %param.7) | copy-start | bytes 49156
  55.0 9.0 %copy-start.40 = (f32[128,128]{1,0:T(8,128)S(1)}, f32[128,128]{1,0:T(8,128)}, u32[]{:S(2)}) copy-start(f32[128,128]{1,0:T(8,128)} %param.8) | copy-start | bytes 196612
  57.5 4.8 %collective-permute-start.7 = (f32[4,128]{1,0:T(4,128)S(1)}, f32[4,128]{1,0:T(4,128)S(1)}, u32[]{:S(2)}, u32[]{:S(2)}) collective-permute-start(f32[4,128]{1,0:T(4,128)S(1)} %convolution_add_fusion.25), channel_id=1, source_target_pairs={{0,96},{1,97},{2,98},{3,99},{4,100},{5,101},{6,102},{7,103},{8,104... | collective-permute-start | bytes 6152 | tf_op jit(solution)/shard_map/ppermute | solution.py:110
  58.6 11.5 %copy-start.5 = (f32[1,8,128,128]{3,2,1,0:T(8,128)S(1)}, f32[1,8,128,128]{3,2,1,0:T(8,128)}, u32[]{:S(2)}) copy-start(f32[1,8,128,128]{3,2,1,0:T(8,128)} %get-tuple-element.70) | copy-start | bytes 1572868
  62.5 9.5 %copy-start.24 = (f32[1,128,128]{2,1,0:T(8,128)S(1)}, f32[1,128,128]{2,1,0:T(8,128)}, u32[]{:S(2)}) copy-start(f32[1,128,128]{2,1,0:T(8,128)} %copy-done.23) | copy-start | bytes 196612
  62.5 15.1 %copy-start.14 = (f32[1,1,128,128]{3,2,1,0:T(8,128)S(1)}, f32[1,1,128,128]{3,2,1,0:T(8,128)}, u32[]{:S(2)}) copy-start(f32[1,1,128,128]{3,2,1,0:T(8,128)} %copy-done.13) | copy-start | bytes 196612
  63.7 13.9 %copy-start.10 = (f32[4,128,128]{2,1,0:T(8,128)S(1)}, f32[4,128,128]{2,1,0:T(8,128)}, u32[]{:S(2)}) copy-start(f32[4,128,128]{2,1,0:T(8,128)} %get-tuple-element.55) | copy-start | bytes 786436
  64.3 14.7 %copy-start.2 = (f32[8,128,128]{2,1,0:T(8,128)S(1)}, f32[8,128,128]{2,1,0:T(8,128)}, u32[]{:S(2)}) copy-start(f32[8,128,128]{2,1,0:T(8,128)} %get-tuple-element.56) | copy-start | bytes 1572868
  64.6 14.4 %copy-start.11 = (f32[32,4,128]{2,0,1:T(8,128)}, f32[32,4,128]{2,0,1:T(8,128)S(1)}, u32[]{:S(2)}) copy-start(f32[32,4,128]{2,0,1:T(8,128)S(1)} %convolution_subtract_fusion.1) | copy-start | bytes 196612
  70.9 1.2 %collective-permute-start.8 = (f32[4,128]{1,0:T(4,128)S(1)}, f32[4,128]{1,0:T(4,128)S(1)}, u32[]{:S(2)}, u32[]{:S(2)}) collective-permute-start(f32[4,128]{1,0:T(4,128)S(1)} %convolution_add_fusion.18), channel_id=1, source_target_pairs={{0,1},{1,0},{2,3},{3,2},{4,5},{5,4},{6,7},{7,6},{8,9},{9,8},{10,11... | collective-permute-start | bytes 6152 | tf_op jit(solution)/shard_map/ppermute | solution.py:110
  73.1 3.7 %collective-permute-start.9 = (f32[4,128]{1,0:T(4,128)S(1)}, f32[4,128]{1,0:T(4,128)S(1)}, u32[]{:S(2)}, u32[]{:S(2)}) collective-permute-start(f32[4,128]{1,0:T(4,128)S(1)} %fusion.219), channel_id=1, source_target_pairs={{0,2},{1,3},{2,0},{3,1},{4,6},{5,7},{6,4},{7,5},{8,10},{9,11},{10,... | collective-permute-start | bytes 6152 | tf_op jit(solution)/shard_map/ppermute | solution.py:110
  79.8 4.9 %collective-permute-start.10 = (f32[4,128]{1,0:T(4,128)S(1)}, f32[4,128]{1,0:T(4,128)S(1)}, u32[]{:S(2)}, u32[]{:S(2)}) collective-permute-start(f32[4,128]{1,0:T(4,128)S(1)} %fusion.217), channel_id=1, source_target_pairs={{0,6},{1,7},{2,4},{3,5},{4,2},{5,3},{6,0},{7,1},{8,14},{9,15},{10,... | collective-permute-start | bytes 6152 | tf_op jit(solution)/shard_map/ppermute | solution.py:110
  84.9 3.9 %collective-permute-start.11 = (f32[4,128]{1,0:T(4,128)S(1)}, f32[4,128]{1,0:T(4,128)S(1)}, u32[]{:S(2)}, u32[]{:S(2)}) collective-permute-start(f32[4,128]{1,0:T(4,128)S(1)} %fusion.216), channel_id=1, source_target_pairs={{0,8},{1,9},{2,10},{3,11},{4,12},{5,13},{6,14},{7,15},{8,0},{9,1},... | collective-permute-start | bytes 6152 | tf_op jit(solution)/shard_map/ppermute | solution.py:110
  89.0 4.9 %collective-permute-start.12 = (f32[4,128]{1,0:T(4,128)S(1)}, f32[4,128]{1,0:T(4,128)S(1)}, u32[]{:S(2)}, u32[]{:S(2)}) collective-permute-start(f32[4,128]{1,0:T(4,128)S(1)} %fusion.215), channel_id=1, source_target_pairs={{0,24},{1,25},{2,26},{3,27},{4,28},{5,29},{6,30},{7,31},{8,16},{9,... | collective-permute-start | bytes 6152 | tf_op jit(solution)/shard_map/ppermute | solution.py:110
  94.9 3.6 %collective-permute-start.13 = (f32[4,128]{1,0:T(4,128)S(1)}, f32[4,128]{1,0:T(4,128)S(1)}, u32[]{:S(2)}, u32[]{:S(2)}) collective-permute-start(f32[4,128]{1,0:T(4,128)S(1)} %fusion.214), channel_id=1, source_target_pairs={{0,32},{1,33},{2,34},{3,35},{4,36},{5,37},{6,38},{7,39},{8,40},{9,... | collective-permute-start | bytes 6152 | tf_op jit(solution)/shard_map/ppermute | solution.py:110
  99.7 4.8 %collective-permute-start.14 = (f32[4,128]{1,0:T(4,128)S(1)}, f32[4,128]{1,0:T(4,128)S(1)}, u32[]{:S(2)}, u32[]{:S(2)}) collective-permute-start(f32[4,128]{1,0:T(4,128)S(1)} %fusion.213), channel_id=1, source_target_pairs={{0,96},{1,97},{2,98},{3,99},{4,100},{5,101},{6,102},{7,103},{8,104... | collective-permute-start | bytes 6152 | tf_op jit(solution)/shard_map/ppermute | solution.py:110
  (43 other events, 168.4 us)
